TPU v7x, 256 devices: a whole 4x4x8 slice. The times are simulated.
256 devices in a mesh: row: 16 (over x_hi, z), col: 16 (over x_lo, y, core).
Axes of the slice: x: 4 (x_hi: 2, x_lo: 2; x = x_hi * 2 + x_lo), y: 4, z: 8, core: 2. Of those that a mesh axis runs over, the one named last changes fastest.
Arguments:
- features: bfloat16 [3, 256, 256, 1024], P(None, 'row', 'col'), may hold values from -6 to 6
- dw_kernel: bfloat16 [7, 7, 1024], replicated, may hold values from -0.875 to 0.875
- ln_gain: float32 [1024], replicated, may hold values from 0.1 to 1.9
- w_in: bfloat16 [1024, 4096], P(None, 'col'), may hold values from -0.1875 to 0.1875
- w_down: bfloat16 [1024, 4096], P(None, 'col'), may hold values from -0.09375 to 0.09375
- gamma: float32 [1024], replicated, may hold values from 0.3 to 1.5
- labels: int32 [3, 256, 256], P(None, 'row', 'col'), may hold values from 0 to 15
- valid: int32 [3, 256, 256], P(None, 'row', 'col'), may hold values 0 or 1
Outputs:
- gram: float32 [1024, 1024], P(('row', 'col'))
- cross: float32 [1024, 16], P(('row', 'col'))
All inputs are finite; a program needn't handle non-finite values. No bound on the sum of `valid` on one device may be relied on, other than what follows from the above.
Results may differ from a plain program's by a relative error of at most 0.0037.
Values may be sent and summed in bfloat16 or wider, within the bound.
No kernel may reach another device: no remote copies, remote signals or barrier semaphores. Data moves between devices by JAX's collectives and lax.ppermute only.
A program may use at most 128 MiB of HBM per device.

v0:
```python
import jax
import jax.numpy as jnp
from jax import lax
from jax.sharding import PartitionSpec as P

NCLS = 16
KSIZE = 7
LANES = 128


def with_halo(shard, sides, width):
    for axis, dim in sides:
        size, length = (lax.axis_size(axis), shard.shape[dim])
        up = [(i, (i + 1) % size) for i in range(size - 1)]
        down = [(j, i) for i, j in up]
        last = lax.slice_in_dim(shard, length - width, length, axis=dim)
        leading = lax.slice_in_dim(shard, 0, width, axis=dim)
        before = lax.ppermute(last, axis, up)
        after = lax.ppermute(leading, axis, down)
        shard = jnp.concatenate([before, shard, after], axis=dim)
    return shard


def apply_norm(rows, ln_gain):
    mean = jnp.mean(rows, axis=(-2, -1), keepdims=True)
    centered = rows - mean
    var = jnp.mean(centered * centered, axis=(-2, -1), keepdims=True)
    return (centered * lax.rsqrt(var + 1e-06) * ln_gain).astype(jnp.bfloat16)


def expand(normed, piece):
    return jax.nn.gelu(
        jnp.dot(normed, piece, preferred_element_type=jnp.float32), approximate=False
    ).astype(jnp.bfloat16)


def contract(hidden, piece):
    return lax.dot_general(
        hidden, piece, (((1,), (1,)), ((), ())), preferred_element_type=jnp.float32
    )


HALVING_BITS = ((0, 1, 3, 4, 2, 5, 7, 6), (0, 3, 1, 2, 4, 7, 5, 6))


def halving_order(rows):
    count, width = rows.shape
    bits = HALVING_BITS[0]
    split = rows.reshape((count,) + (2,) * len(bits) + (width >> len(bits),))
    order = (0,) + tuple(len(bits) - bit for bit in bits) + (len(bits) + 1,)
    return split.transpose(order).reshape(count, width)


def halving_sum(part, axes):
    size = 1
    for axis in axes:
        size *= lax.axis_size(axis)
    me = lax.axis_index(axes)
    core = me & 1
    for step in range(len(HALVING_BITS[0])):
        bit = jnp.where(core, HALVING_BITS[1][step], HALVING_BITS[0][step])
        mine = (me >> bit) & 1
        if HALVING_BITS[0][step] != HALVING_BITS[1][step] and (
            HALVING_BITS[0][step] == HALVING_BITS[1][step + 1]
        ):
            quarters = part.reshape((2, 2, part.shape[0] // 4) + part.shape[1:])
            rest = quarters.shape[2:]

            def half(value):
                pieces = []
                for other in (0, 1):
                    first = jnp.where(core, other, value)
                    second = jnp.where(core, value, other)
                    start = (first, second) + (0,) * len(rest)
                    piece = lax.dynamic_slice(quarters, start, (1, 1) + rest)
                    pieces.append(piece.reshape(rest))
                return jnp.concatenate(pieces, axis=0)

            keep, send = half(mine), half(1 - mine)
        else:
            halves = part.reshape((2, part.shape[0] // 2) + part.shape[1:])
            keep = lax.dynamic_index_in_dim(halves, mine, 0, keepdims=False)
            send = lax.dynamic_index_in_dim(halves, 1 - mine, 0, keepdims=False)
        pairs = [(i, i ^ (1 << HALVING_BITS[i & 1][step])) for i in range(size)]
        part = keep + lax.ppermute(send, axes, pairs)
    return part


def targets_of(labels, count):
    classes = jnp.arange(NCLS, dtype=jnp.int32)
    onehot = (labels.reshape(count, 1) == classes[None, :]).astype(jnp.float32)
    return (onehot - 1.0 / NCLS).astype(jnp.bfloat16)


def on_device(features, dw_kernel, ln_gain, w_in, w_down, gamma, labels, valid):
    tiles, high, wide, width = features.shape
    tile = (width // LANES, LANES)
    padded = with_halo(features, (("row", 1), ("col", 2)), 3).astype(jnp.float32)
    padded = padded.reshape(padded.shape[:3] + tile)
    kernel = dw_kernel.astype(jnp.float32).reshape((KSIZE, KSIZE) + tile)
    conv = jnp.zeros((tiles, high, wide) + tile, jnp.float32)
    for i in range(KSIZE):
        for j in range(KSIZE):
            conv = conv + padded[:, i : i + high, j : j + wide] * kernel[i, j]
    count = tiles * high * wide
    normed = apply_norm(conv.reshape(count, *tile), ln_gain.reshape(tile)).reshape(count, width)
    hidden = expand(normed, lax.all_gather(w_in, "col", axis=1, tiled=True))
    branch = contract(hidden, lax.all_gather(w_down, "col", axis=1, tiled=True))
    out = (features.reshape(count, width).astype(jnp.float32) + gamma * branch).astype(jnp.bfloat16)
    keep = valid.reshape(count, 1)
    masked = out * keep.astype(jnp.bfloat16)
    both = lax.dot_general(
        halving_order(masked),
        jnp.concatenate([out, targets_of(labels, count)], axis=1),
        (((0,), (0,)), ((), ())),
        preferred_element_type=jnp.float32,
    )
    summed = halving_sum(both, ("row", "col"))
    gram_sum, cross_sum = summed[:, :width], summed[:, width:]
    total = float(tiles * high * lax.axis_size("row") * wide * lax.axis_size("col"))
    return (gram_sum / total, cross_sum / jnp.sqrt(jnp.float32(total)))


def solution(mesh):
    return jax.shard_map(
        on_device,
        mesh=mesh,
        in_specs=(
            P(None, "row", "col", None),
            P(),
            P(),
            P(None, "col"),
            P(None, "col"),
            P(),
            P(None, "row", "col"),
            P(None, "row", "col"),
        ),
        out_specs=(P(("row", "col"), None), P(("row", "col"), None)),
        check_vma=False,
    )
```

profile of v0, /device:TPU:120, one launch (start us, length us, event | category | flops | bytes accessed | tf_op | source)
XLA Modules:
  0.0 269.3 jit_solution(7226295197161033471)
XLA Ops:
  9.8 5.0 %collective-permute-start = (bf16[3,3,16,1024]{3,2,1,0:T(8,128)(2,1)S(1)}, bf16[3,3,16,1024]{3,2,1,0:T(8,128)(2,1)S(1)}, u32[]{:S(2)}, u32[]{:S(2)}) collective-permute-start(bf16[3,3,16,1024]{3,2,1,0:T(8,128)(2,1)S(1)} %get-tuple-element.10), channel_id=1, source_target_pairs={{0,16},{16,32},{32,48},{48,64},{64,80},{80,96},{96,112},{112,128},... | collective-permute-start | bytes 884744 | tf_op jit(solution)/shard_map/ppermute | solution.py:18
  21.6 4.9 %collective-permute-done.1 = bf16[3,3,16,1024]{3,2,1,0:T(8,128)(2,1)S(1)} collective-permute-done((bf16[3,3,16,1024]{3,2,1,0:T(8,128)(2,1)S(1)}, bf16[3,3,16,1024]{3,2,1,0:T(8,128)(2,1)S(1)}, u32[]{:S(2)}, u32[]{:S(2)}) %collective-permute-start.1) | collective-permute-done | bytes 294944 | tf_op jit(solution)/shard_map/ppermute | solution.py:19
  26.7 3.0 %pad_maximum_fusion.1 = bf16[3,22,16,1024]{3,1,2,0:T(8,128)(2,1)S(1)} fusion(bf16[3,3,16,1024]{3,1,2,0:T(4,128)(2,1)S(1)} %copy.68, bf16[3,16,16,1024]{3,1,2,0:T(8,128)(2,1)} %copy.67, bf16[3,3,16,1024]{3,1,2,0:T(4,128)(2,1)S(1)} %copy.66), kind=kLoop, calls=%fused_computation.126 | loop fusion | flops 6488064 | bytes 4325376 | tf_op jit(solution)/shard_map/concatenate | solution.py:20
  31.6 3.6 %collective-permute-start.3 = (bf16[3,22,3,1024]{3,1,2,0:T(8,128)(2,1)S(1)}, bf16[3,22,3,1024]{3,1,2,0:T(8,128)(2,1)}, u32[]{:S(2)}, u32[]{:S(2)}) collective-permute-start(bf16[3,22,3,1024]{3,1,2,0:T(8,128)(2,1)S(1)} %get-tuple-element.5), channel_id=1, source_target_pairs={{1,0},{2,1},{3,2},{4,3},{5,4},{6,5},{7,6},{8,7},{9,8},{10,9},{11,1... | collective-permute-start | bytes 1216520 | tf_op jit(solution)/shard_map/ppermute | solution.py:19
  36.6 2.8 %reshape.208 = bf16[3,22,16,8,128]{4,3,1,2,0:T(8,128)(2,1)} reshape(bf16[3,22,16,1024]{3,1,2,0:T(8,128)(2,1)S(1)} %pad_maximum_fusion.1) | data formatting | bytes 4325376 | tf_op jit(solution)/shard_map/concatenate | solution.py:20
  39.3 7.0 %collective-permute-done.2 = bf16[3,22,3,1024]{3,1,2,0:T(8,128)(2,1)} collective-permute-done((bf16[3,22,3,1024]{3,1,2,0:T(8,128)(2,1)S(1)}, bf16[3,22,3,1024]{3,1,2,0:T(8,128)(2,1)}, u32[]{:S(2)}, u32[]{:S(2)}) %collective-permute-start.2) | collective-permute-done | bytes 405536 | tf_op jit(solution)/shard_map/ppermute | solution.py:18
  49.3 4.0 %copy_convert_fusion = f32[3,22,22,8,128]{4,3,2,1,0:T(8,128)} fusion(bf16[3,22,3,8,128]{4,3,1,2,0:T(8,128)(2,1)S(1)} %concatenate.37, bf16[3,22,16,8,128]{4,3,1,2,0:T(8,128)(2,1)} %reshape.208, bf16[3,22,3,8,128]{4,3,1,2,0:T(8,128)(2,1)S(1)} %concatenate.35), kind=kLoop, calls=%fused_computation.125 | loop fusion | flops 4460544 | bytes 8921088 | tf_op jit(solution)/shard_map/convert_element_type | solution.py:98
  53.4 62.4 %fusion.113 = (f32[3,16,16]{2,1,0:T(8,128)S(1)}, f32[3,16,16,8,128]{4,3,2,1,0:T(8,128)S(1)}) fusion(f32[8,128]{1,0:T(8,128)S(1)} %get-tuple-element.19, f32[3,22,22,8,128]{4,3,2,1,0:T(8,128)} %copy_convert_fusion, f32[8,128]{1,0:T(8,128)S(1)} %get-tuple-element.20, f32[8,128]{1,0:T(8,128)S(1)} %get-tuple-element.21, f32[8,128]{1,0:T(8,128)S(1)} %get-tuple-element.22, ...), kind=kLoop, calls=%fused_computation.252 | loop fusion | flops 77069568 | bytes 157490176 | tf_op jit(solution)/shard_map/reduce_sum | solution.py:25
  116.0 11.0 %multiply_reduce_fusion = f32[3,16,16]{2,1,0:T(8,128)S(1)} fusion(f32[3,16,16,8,128]{4,3,2,1,0:T(8,128)S(1)} %get-tuple-element.3, f32[3,16,16]{2,1,0:T(8,128)S(1)} %broadcast_multiply_fusion.1), kind=kLoop, calls=%fused_computation.123 | loop fusion | flops 2358528 | bytes 3151872 | tf_op jit(solution)/shard_map/reduce_sum | solution.py:27
  127.1 37.4 %fusion.65.clone.4 = bf16[768,4096]{1,0:T(8,128)(2,1)} fusion(bf16[1024,4096]{1,0:T(8,128)(2,1)} %all-gather.3.cloned.1.call-done, f32[96,8,8,128]{3,2,1,0:T(8,128)S(1)} %bitcast.193, f32[1024]{0:T(1024)S(1)} %copy-done.28, f32[768]{0:T(1024)S(1)} %rsqrt.12, f32[768]{0:T(1024)S(1)} %div.21), kind=kOutput, calls=%fused_computation.3.clone.clone.clone.clone.clone.clone.1 | convolution fusion | flops 6650068992 | bytes 17836032 | tf_op jit(solution)/shard_map/dot_general | solution.py:33
  164.4 12.5 %broadcast_multiply_fusion = (bf16[768,1024]{1,0:T(8,128)(2,1)S(1)}, bf16[768,1024]{1,0:T(8,128)(2,1)}) fusion(bf16[768]{0:T(1024)(128)(2,1)S(1)} %copy-done.27, bf16[1024,4096]{1,0:T(8,128)(2,1)} %all-gather.5.cloned.1.call-done, f32[1024]{0:T(1024)S(1)} %copy-done.29, bf16[768,1024]{1,0:T(8,128)(2,1)} %bitcast.195, bf16[768,4096]{1,0:T(8,128)(2,1)} %fusion.65.clone.4), kind=kOutput, calls=%fused_computation.139 | convolution fusion | flops 6446383104 | bytes 19404288 | tf_op jit(solution)/shard_map/dot_general | solution.py:38
  179.5 3.3 %fusion.66 = f32[2,512,1040]{1,2,0:T(8,128)S(1)} fusion(bf16[2,512,768]{2,1,0:T(8,128)(2,1)S(1)} %bitcast.201, bf16[768,16]{1,0:T(8,128)(2,1)S(1)} %copy-done.2, bf16[768,1024]{1,0:T(8,128)(2,1)} %get-tuple-element.72), kind=kOutput, calls=%fused_computation.130 | convolution fusion | flops 1638973440 | bytes 7430144 | tf_op jit(solution)/shard_map/dot_general | solution.py:112
  189.0 4.0 %collective-permute-done.4 = f32[512,1040]{0,1:T(8,128)S(1)} collective-permute-done((f32[512,1040]{0,1:T(8,128)}, f32[512,1040]{0,1:T(8,128)S(1)}, u32[]{:S(2)}, u32[]{:S(2)}) %collective-permute-start.4) | collective-permute-done | bytes 2129952 | tf_op jit(solution)/shard_map/ppermute | solution.py:85
  193.0 3.4 %bitcast_add_fusion = f32[512,1040]{0,1:T(8,128)} fusion(f32[512,1040]{0,1:T(8,128)S(1)} %collective-permute-done.4, f32[2,512,1040]{1,2,0:T(8,128)} %copy-done, s32[]{:T(128)S(6)} %select_n.202), kind=kLoop, calls=%fused_computation.127 | loop fusion | flops 532480 | bytes 6389764 | tf_op jit(solution)/shard_map/add | solution.py:85
  196.5 2.7 reshape.185
  201.4 14.8 %collective-permute-done.5 = f32[256,1040]{0,1:T(8,128)S(1)} collective-permute-done((f32[256,1040]{0,1:T(8,128)S(1)}, f32[256,1040]{0,1:T(8,128)S(1)}, u32[]{:S(2)}, u32[]{:S(2)}) %collective-permute-start.5) | collective-permute-done | bytes 1064992 | tf_op jit(solution)/shard_map/ppermute | solution.py:85
  219.1 8.3 %collective-permute-done.6 = f32[128,1040]{0,1:T(8,128)S(1)} collective-permute-done((f32[128,1040]{0,1:T(8,128)S(1)}, f32[128,1040]{0,1:T(8,128)S(1)}, u32[]{:S(2)}, u32[]{:S(2)}) %collective-permute-start.6) | collective-permute-done | bytes 532512 | tf_op jit(solution)/shard_map/ppermute | solution.py:85
  227.9 6.7 %collective-permute-done.7 = f32[64,1040]{1,0:T(8,128)S(1)} collective-permute-done((f32[64,1040]{1,0:T(8,128)S(1)}, f32[64,1040]{1,0:T(8,128)S(1)}, u32[]{:S(2)}, u32[]{:S(2)}) %collective-permute-start.7) | collective-permute-done | bytes 266272 | tf_op jit(solution)/shard_map/ppermute | solution.py:85
  234.8 6.6 %collective-permute-done.8 = f32[32,1040]{1,0:T(8,128)S(1)} collective-permute-done((f32[32,1040]{1,0:T(8,128)S(1)}, f32[32,1040]{1,0:T(8,128)S(1)}, u32[]{:S(2)}, u32[]{:S(2)}) %collective-permute-start.8) | collective-permute-done | bytes 133152 | tf_op jit(solution)/shard_map/ppermute | solution.py:85
  241.6 6.2 %collective-permute-done.9 = f32[16,1040]{1,0:T(8,128)S(1)} collective-permute-done((f32[16,1040]{1,0:T(8,128)S(1)}, f32[16,1040]{1,0:T(8,128)S(1)}, u32[]{:S(2)}, u32[]{:S(2)}) %collective-permute-start.9) | collective-permute-done | bytes 66592 | tf_op jit(solution)/shard_map/ppermute | solution.py:85
  247.9 3.0 %collective-permute-start.10 = (f32[8,1040]{1,0:T(8,128)S(1)}, f32[8,1040]{1,0:T(8,128)S(1)}, u32[]{:S(2)}, u32[]{:S(2)}) collective-permute-start(f32[8,1040]{1,0:T(8,128)S(1)} %dynamic-slice_bitcast_fusion.6), channel_id=1, source_target_pairs={{0,128},{1,33},{2,130},{3,35},{4,132},{5,37},{6,134},{7,39},{8,136... | collective-permute-start | bytes 99848 | tf_op jit(solution)/shard_map/ppermute | solution.py:85
  250.9 2.6 collective-permute-done.10
  253.5 3.7 %collective-permute-start.11 = (f32[4,1040]{1,0:T(4,128)S(1)}, f32[4,1040]{1,0:T(4,128)S(1)}, u32[]{:S(2)}, u32[]{:S(2)}) collective-permute-start(f32[4,1040]{1,0:T(4,128)S(1)} %dynamic-slice_bitcast_fusion.11), channel_id=1, source_target_pairs={{0,64},{1,65},{2,66},{3,67},{4,68},{5,69},{6,70},{7,71},{8,72},{9,... | collective-permute-start | bytes 49928 | tf_op jit(solution)/shard_map/ppermute | solution.py:85
  257.2 4.0 %collective-permute-done.11 = f32[4,1040]{1,0:T(4,128)S(1)} collective-permute-done((f32[4,1040]{1,0:T(4,128)S(1)}, f32[4,1040]{1,0:T(4,128)S(1)}, u32[]{:S(2)}, u32[]{:S(2)}) %collective-permute-start.11) | collective-permute-done | bytes 16672 | tf_op jit(solution)/shard_map/ppermute | solution.py:85
  (124 shorter events, 31.5 us)
Async XLA Ops:
  7.2 10.4 %copy-start.1 = (bf16[3,16,16,1024]{3,2,1,0:T(8,128)(2,1)S(1)}, bf16[3,16,16,1024]{3,2,1,0:T(8,128)(2,1)}, u32[]{:S(2)}) copy-start(bf16[3,16,16,1024]{3,2,1,0:T(8,128)(2,1)} %param.8) | copy-start | bytes 4718596
  7.2 12.5 %copy-start.3 = (bf16[7,7,1024]{2,1,0:T(8,128)(2,1)S(1)}, bf16[7,7,1024]{2,1,0:T(8,128)(2,1)}, u32[]{:S(2)}) copy-start(bf16[7,7,1024]{2,1,0:T(8,128)(2,1)} %param.9) | copy-start | bytes 301060
  7.2 12.6 %copy-start.4 = (s32[3,16,16]{2,1,0:T(8,128)S(1)}, s32[3,16,16]{2,1,0:T(8,128)}, u32[]{:S(2)}) copy-start(s32[3,16,16]{2,1,0:T(8,128)} %param.15) | copy-start | bytes 9220
  7.2 119.8 %all-gather.3.cloned.1.call-start = ((), (), s32[]{:S(2)}) async-start(), calls=%async_computation | async-start | bytes 8912896 | tf_op jit(solution)/shard_map/all_gather | solution.py:107
  7.9 156.5 %all-gather.5.cloned.1.call-start = ((), (), s32[]{:S(2)}) async-start(), calls=%async_computation.1 | async-start | bytes 8912896 | tf_op jit(solution)/shard_map/all_gather | solution.py:108
  9.8 11.5 %collective-permute-start = (bf16[3,3,16,1024]{3,2,1,0:T(8,128)(2,1)S(1)}, bf16[3,3,16,1024]{3,2,1,0:T(8,128)(2,1)S(1)}, u32[]{:S(2)}, u32[]{:S(2)}) collective-permute-start(bf16[3,3,16,1024]{3,2,1,0:T(8,128)(2,1)S(1)} %get-tuple-element.10), channel_id=1, source_target_pairs={{0,16},{16,32},{32,48},{48,64},{64,80},{80,96},{96,112},{112,128},... | collective-permute-start | bytes 884744 | tf_op jit(solution)/shard_map/ppermute | solution.py:18
  14.8 11.6 %collective-permute-start.1 = (bf16[3,3,16,1024]{3,2,1,0:T(8,128)(2,1)S(1)}, bf16[3,3,16,1024]{3,2,1,0:T(8,128)(2,1)S(1)}, u32[]{:S(2)}, u32[]{:S(2)}) collective-permute-start(bf16[3,3,16,1024]{3,2,1,0:T(8,128)(2,1)S(1)} %get-tuple-element.11), channel_id=1, source_target_pairs={{16,0},{32,16},{48,32},{64,48},{80,64},{96,80},{112,96},{128,112},... | collective-permute-start | bytes 884744 | tf_op jit(solution)/shard_map/ppermute | solution.py:19
  29.7 16.6 %collective-permute-start.2 = (bf16[3,22,3,1024]{3,1,2,0:T(8,128)(2,1)S(1)}, bf16[3,22,3,1024]{3,1,2,0:T(8,128)(2,1)}, u32[]{:S(2)}, u32[]{:S(2)}) collective-permute-start(bf16[3,22,3,1024]{3,1,2,0:T(8,128)(2,1)S(1)} %get-tuple-element.4), channel_id=1, source_target_pairs={{0,1},{1,2},{2,3},{3,4},{4,5},{5,6},{6,7},{7,8},{8,9},{9,10},{10,1... | collective-permute-start | bytes 1216520 | tf_op jit(solution)/shard_map/ppermute | solution.py:18
  31.6 16.1 %collective-permute-start.3 = (bf16[3,22,3,1024]{3,1,2,0:T(8,128)(2,1)S(1)}, bf16[3,22,3,1024]{3,1,2,0:T(8,128)(2,1)}, u32[]{:S(2)}, u32[]{:S(2)}) collective-permute-start(bf16[3,22,3,1024]{3,1,2,0:T(8,128)(2,1)S(1)} %get-tuple-element.5), channel_id=1, source_target_pairs={{1,0},{2,1},{3,2},{4,3},{5,4},{6,5},{7,6},{8,7},{9,8},{10,9},{11,1... | collective-permute-start | bytes 1216520 | tf_op jit(solution)/shard_map/ppermute | solution.py:19
  49.1 4.2 %copy-start.5 = (f32[8,128]{1,0:T(8,128)S(1)}, f32[8,128]{1,0:T(8,128)}, u32[]{:S(2)}) copy-start(f32[8,128]{1,0:T(8,128)} %get-tuple-element.64) | copy-start | bytes 12292
  49.1 4.2 %copy-start.6 = (f32[8,128]{1,0:T(8,128)S(1)}, f32[8,128]{1,0:T(8,128)}, u32[]{:S(2)}) copy-start(f32[8,128]{1,0:T(8,128)} %get-tuple-element.65) | copy-start | bytes 12292
  49.1 4.2 %copy-start.7 = (f32[8,128]{1,0:T(8,128)S(1)}, f32[8,128]{1,0:T(8,128)}, u32[]{:S(2)}) copy-start(f32[8,128]{1,0:T(8,128)} %get-tuple-element.66) | copy-start | bytes 12292
  49.1 4.2 %copy-start.8 = (f32[8,128]{1,0:T(8,128)S(1)}, f32[8,128]{1,0:T(8,128)}, u32[]{:S(2)}) copy-start(f32[8,128]{1,0:T(8,128)} %get-tuple-element.37) | copy-start | bytes 12292
  115.8 11.2 %copy-start.28 = (f32[1024]{0:T(1024)S(1)}, f32[1024]{0:T(1024)}, u32[]{:S(2)}) copy-start(f32[1024]{0:T(1024)} %param.10) | copy-start | bytes 12292
  127.0 37.4 %copy-start.27 = (bf16[768]{0:T(1024)(128)(2,1)S(1)}, bf16[768]{0:T(1024)(128)(2,1)}, u32[]{:S(2)}) copy-start(bf16[768]{0:T(1024)(128)(2,1)} %convert_element_type.45) | copy-start | bytes 4612
  127.0 37.4 %copy-start.29 = (f32[1024]{0:T(1024)S(1)}, f32[1024]{0:T(1024)}, u32[]{:S(2)}) copy-start(f32[1024]{0:T(1024)} %param.13) | copy-start | bytes 12292
  186.4 6.6 %collective-permute-start.4 = (f32[512,1040]{0,1:T(8,128)}, f32[512,1040]{0,1:T(8,128)S(1)}, u32[]{:S(2)}, u32[]{:S(2)}) collective-permute-start(f32[512,1040]{0,1:T(8,128)} %dynamic-slice_bitcast_fusion), channel_id=1, source_target_pairs={{0,1},{1,0},{2,3},{3,2},{4,5},{5,4},{6,7},{7,6},{8,9},{9,8},{10,11... | collective-permute-start | bytes 6389768 | tf_op jit(solution)/shard_map/ppermute | solution.py:85
  201.2 15.1 %collective-permute-start.5 = (f32[256,1040]{0,1:T(8,128)S(1)}, f32[256,1040]{0,1:T(8,128)S(1)}, u32[]{:S(2)}, u32[]{:S(2)}) collective-permute-start(f32[256,1040]{0,1:T(8,128)S(1)} %pad_maximum_fusion.2), channel_id=1, source_target_pairs={{0,2},{1,9},{2,0},{3,11},{4,6},{5,13},{6,4},{7,15},{8,10},{9,1},{1... | collective-permute-start | bytes 3194888 | tf_op jit(solution)/shard_map/ppermute | solution.py:85
  218.1 9.4 %collective-permute-start.6 = (f32[128,1040]{0,1:T(8,128)S(1)}, f32[128,1040]{0,1:T(8,128)S(1)}, u32[]{:S(2)}, u32[]{:S(2)}) collective-permute-start(f32[128,1040]{0,1:T(8,128)S(1)} %bitcast.205), channel_id=1, source_target_pairs={{0,8},{1,3},{2,10},{3,1},{4,12},{5,7},{6,14},{7,5},{8,0},{9,11},{1... | collective-permute-start | bytes 1597448 | tf_op jit(solution)/shard_map/ppermute | solution.py:85
  227.8 6.8 %collective-permute-start.7 = (f32[64,1040]{1,0:T(8,128)S(1)}, f32[64,1040]{1,0:T(8,128)S(1)}, u32[]{:S(2)}, u32[]{:S(2)}) collective-permute-start(f32[64,1040]{1,0:T(8,128)S(1)} %pad_maximum_fusion.3), channel_id=1, source_target_pairs={{0,16},{1,5},{2,18},{3,7},{4,20},{5,1},{6,22},{7,3},{8,24},{9,13},... | collective-permute-start | bytes 798728 | tf_op jit(solution)/shard_map/ppermute | solution.py:85
  234.7 6.7 %collective-permute-start.8 = (f32[32,1040]{1,0:T(8,128)S(1)}, f32[32,1040]{1,0:T(8,128)S(1)}, u32[]{:S(2)}, u32[]{:S(2)}) collective-permute-start(f32[32,1040]{1,0:T(8,128)S(1)} %dynamic-slice_bitcast_fusion.1), channel_id=1, source_target_pairs={{0,4},{1,17},{2,6},{3,19},{4,0},{5,21},{6,2},{7,23},{8,12},{9,25},... | collective-permute-start | bytes 399368 | tf_op jit(solution)/shard_map/ppermute | solution.py:85
  241.5 6.4 %collective-permute-start.9 = (f32[16,1040]{1,0:T(8,128)S(1)}, f32[16,1040]{1,0:T(8,128)S(1)}, u32[]{:S(2)}, u32[]{:S(2)}) collective-permute-start(f32[16,1040]{1,0:T(8,128)S(1)} %pad_maximum_fusion.4), channel_id=1, source_target_pairs={{0,32},{1,129},{2,34},{3,131},{4,36},{5,133},{6,38},{7,135},{8,40}... | collective-permute-start | bytes 199688 | tf_op jit(solution)/shard_map/ppermute | solution.py:85
  247.9 5.5 %collective-permute-start.10 = (f32[8,1040]{1,0:T(8,128)S(1)}, f32[8,1040]{1,0:T(8,128)S(1)}, u32[]{:S(2)}, u32[]{:S(2)}) collective-permute-start(f32[8,1040]{1,0:T(8,128)S(1)} %dynamic-slice_bitcast_fusion.6), channel_id=1, source_target_pairs={{0,128},{1,33},{2,130},{3,35},{4,132},{5,37},{6,134},{7,39},{8,136... | collective-permute-start | bytes 99848 | tf_op jit(solution)/shard_map/ppermute | solution.py:85
  253.5 7.8 %collective-permute-start.11 = (f32[4,1040]{1,0:T(4,128)S(1)}, f32[4,1040]{1,0:T(4,128)S(1)}, u32[]{:S(2)}, u32[]{:S(2)}) collective-permute-start(f32[4,1040]{1,0:T(4,128)S(1)} %dynamic-slice_bitcast_fusion.11), channel_id=1, source_target_pairs={{0,64},{1,65},{2,66},{3,67},{4,68},{5,69},{6,70},{7,71},{8,72},{9,... | collective-permute-start | bytes 49928 | tf_op jit(solution)/shard_map/ppermute | solution.py:85
  (20 other events, 78.3 us)
Sparse Core Ops, SparseCore 0:
  9.8 67.4 all-gather.2
  79.0 62.7 all-gather.4
where the time goes:
time: 271 us; the launch traced here: 269 us
  other arithmetic  85.3 us (31%)
  waiting for transfers between devices  66.8 us (25%)
  matrix products  53.2 us (20%)
  local copies, waits for them, and re-layouts  26.7 us (10%)
  starting transfers between devices  22.5 us (8%)
  between operations  14.8 us (5%)
    reduce_sum x1, other arithmetic, apply_norm(): mean = jnp.mean(rows, axis=(-2, -1), keepdims=True)  62.4 us
    ppermute x8, waiting for transfers between devices, halving_sum(): part = keep + lax.ppermute(send, axes, pairs)  53.4 us
    dot_general x1, matrix products, expand(): jnp.dot(normed, piece, preferred_element_type=jnp.float32)  37.4 us
    dot_general x1, matrix products, contract(): lax.dot_general(hidden, piece, (((1,), (1,)), ((), ())), preferred_elemen...  12.5 us
    reduce_sum x1, other arithmetic, apply_norm(): var = jnp.mean(centered * centered, axis=(-2, -1), keepdims=True)  11 us
    ppermute x8, starting transfers between devices, halving_sum(): part = keep + lax.ppermute(send, axes, pairs)  9.9 us
    ppermute x2, starting transfers between devices, with_halo(): before = lax.ppermute(last, axis, up)  6.96 us
    ppermute x2, waiting for transfers between devices, with_halo(): before = lax.ppermute(last, axis, up)  6.95 us
  transfers between devices with their start and end apart: 14, of which 11 were waited for; matrix products, arithmetic and copies ran while one was open for 49% of the time, Pallas kernels for 0%

commit v1 on v0

--- a/solution.py
+++ b/solution.py
@@ -51,13 +51,13 @@
     return split.transpose(order).reshape(count, width)
 
 
-def halving_sum(part, axes):
+def halving_sum(part, axes, begin):
     size = 1
     for axis in axes:
         size *= lax.axis_size(axis)
     me = lax.axis_index(axes)
     core = me & 1
-    for step in range(len(HALVING_BITS[0])):
+    for step in range(begin, len(HALVING_BITS[0])):
         bit = jnp.where(core, HALVING_BITS[1][step], HALVING_BITS[0][step])
         mine = (me >> bit) & 1
         if HALVING_BITS[0][step] != HALVING_BITS[1][step] and (
@@ -109,13 +109,22 @@
     out = (features.reshape(count, width).astype(jnp.float32) + gamma * branch).astype(jnp.bfloat16)
     keep = valid.reshape(count, 1)
     masked = out * keep.astype(jnp.bfloat16)
-    both = lax.dot_general(
-        halving_order(masked),
-        jnp.concatenate([out, targets_of(labels, count)], axis=1),
-        (((0,), (0,)), ((), ())),
-        preferred_element_type=jnp.float32,
-    )
-    summed = halving_sum(both, ("row", "col"))
+    axes = ("row", "col")
+    core = lax.axis_index(axes) & 1
+    ordered = halving_order(masked)
+    rhs = jnp.concatenate([out, targets_of(labels, count)], axis=1)
+    half = width // 2
+
+    def rows_of(which):
+        lhs = lax.dynamic_slice_in_dim(ordered, which * half, half, axis=1)
+        return lax.dot_general(
+            lhs, rhs, (((0,), (0,)), ((), ())), preferred_element_type=jnp.float32
+        )
+
+    size = lax.axis_size("row") * lax.axis_size("col")
+    sent = lax.ppermute(rows_of(1 - core), axes, [(i, i ^ 1) for i in range(size)])
+    kept = lax.optimization_barrier(rows_of(core))
+    summed = halving_sum(kept + sent, axes, 1)
     gram_sum, cross_sum = summed[:, :width], summed[:, width:]
     total = float(tiles * high * lax.axis_size("row") * wide * lax.axis_size("col"))
     return (gram_sum / total, cross_sum / jnp.sqrt(jnp.float32(total)))

time: 271 us -> 267 us (0.985)
  matrix products: 53.2 us -> 56.4 us
    ppermute x8 -> x7, waiting for transfers between devices: 53.4 us -> 49.3 us  [halving_sum(): part = keep + lax.ppermute(send, axes, pairs)]
    add x7 -> x6, other arithmetic: 3.7 us -> 0.25 us  [halving_sum(): part = keep + lax.ppermute(send, axes, pairs)]
    dot_general x1 -> x2, matrix products: 3.32 us -> 6.49 us  [rows_of(): lax.dot_general(lhs, rhs, (((0,), (0,)), ((), ())), preferred_element_typ...]
    ppermute x8 -> x7, starting transfers between devices: 9.9 us -> 7.33 us  [halving_sum(): part = keep + lax.ppermute(send, axes, pairs)]
  transfers between devices with their start and end apart: 14 -> 14, of which waited for: 11 -> 11; matrix products, arithmetic and copies ran while one was open for 49% -> 50% of each run, Pallas kernels for 0% -> 0%
where the time goes in v1:
time: 267 us; the launch traced here: 266 us
  other arithmetic  83.7 us (31%)
  waiting for transfers between devices  64.1 us (24%)
  matrix products  56.4 us (21%)
  local copies, waits for them, and re-layouts  24.2 us (9%)
  starting transfers between devices  22.5 us (8%)
  between operations  14.8 us (6%)
    reduce_sum x1, other arithmetic, apply_norm(): mean = jnp.mean(rows, axis=(-2, -1), keepdims=True)  62.4 us
    ppermute x7, waiting for transfers between devices, halving_sum(): part = keep + lax.ppermute(send, axes, pairs)  49.3 us
    dot_general x1, matrix products, expand(): jnp.dot(normed, piece, preferred_element_type=jnp.float32)  37.4 us
    dot_general x1, matrix products, contract(): lax.dot_general(hidden, piece, (((1,), (1,)), ((), ())), preferred_elemen...  12.5 us
    reduce_sum x1, other arithmetic, apply_norm(): var = jnp.mean(centered * centered, axis=(-2, -1), keepdims=True)  11 us
    ppermute x7, starting transfers between devices, halving_sum(): part = keep + lax.ppermute(send, axes, pairs)  7.33 us
    ppermute x2, starting transfers between devices, with_halo(): before = lax.ppermute(last, axis, up)  6.96 us
    ppermute x2, waiting for transfers between devices, with_halo(): before = lax.ppermute(last, axis, up)  6.95 us
  transfers between devices with their start and end apart: 14, of which 11 were waited for; matrix products, arithmetic and copies ran while one was open for 50% of the time, Pallas kernels for 0%

profile of v1, /device:TPU:120, one launch (start us, length us, event | category | flops | bytes accessed | tf_op | source)
XLA Modules:
  0.0 265.8 jit_solution(268216925033414418)
XLA Ops:
  9.8 5.0 %collective-permute-start = (bf16[3,3,16,1024]{3,2,1,0:T(8,128)(2,1)S(1)}, bf16[3,3,16,1024]{3,2,1,0:T(8,128)(2,1)S(1)}, u32[]{:S(2)}, u32[]{:S(2)}) collective-permute-start(bf16[3,3,16,1024]{3,2,1,0:T(8,128)(2,1)S(1)} %get-tuple-element.10), channel_id=1, source_target_pairs={{0,16},{16,32},{32,48},{48,64},{64,80},{80,96},{96,112},{112,128},... | collective-permute-start | bytes 884744 | tf_op jit(solution)/shard_map/ppermute | solution.py:18
  21.6 4.9 %collective-permute-done.1 = bf16[3,3,16,1024]{3,2,1,0:T(8,128)(2,1)S(1)} collective-permute-done((bf16[3,3,16,1024]{3,2,1,0:T(8,128)(2,1)S(1)}, bf16[3,3,16,1024]{3,2,1,0:T(8,128)(2,1)S(1)}, u32[]{:S(2)}, u32[]{:S(2)}) %collective-permute-start.1) | collective-permute-done | bytes 294944 | tf_op jit(solution)/shard_map/ppermute | solution.py:19
  26.7 3.0 %pad_maximum_fusion.1 = bf16[3,22,16,1024]{3,1,2,0:T(8,128)(2,1)S(1)} fusion(bf16[3,3,16,1024]{3,1,2,0:T(4,128)(2,1)S(1)} %copy.62, bf16[3,16,16,1024]{3,1,2,0:T(8,128)(2,1)} %copy.61, bf16[3,3,16,1024]{3,1,2,0:T(4,128)(2,1)S(1)} %copy.60), kind=kLoop, calls=%fused_computation.126 | loop fusion | flops 6488064 | bytes 4325376 | tf_op jit(solution)/shard_map/concatenate | solution.py:20
  31.6 3.6 %collective-permute-start.3 = (bf16[3,22,3,1024]{3,1,2,0:T(8,128)(2,1)S(1)}, bf16[3,22,3,1024]{3,1,2,0:T(8,128)(2,1)}, u32[]{:S(2)}, u32[]{:S(2)}) collective-permute-start(bf16[3,22,3,1024]{3,1,2,0:T(8,128)(2,1)S(1)} %get-tuple-element.5), channel_id=1, source_target_pairs={{1,0},{2,1},{3,2},{4,3},{5,4},{6,5},{7,6},{8,7},{9,8},{10,9},{11,1... | collective-permute-start | bytes 1216520 | tf_op jit(solution)/shard_map/ppermute | solution.py:19
  36.6 2.8 %reshape.205 = bf16[3,22,16,8,128]{4,3,1,2,0:T(8,128)(2,1)} reshape(bf16[3,22,16,1024]{3,1,2,0:T(8,128)(2,1)S(1)} %pad_maximum_fusion.1) | data formatting | bytes 4325376 | tf_op jit(solution)/shard_map/concatenate | solution.py:20
  39.3 7.0 %collective-permute-done.2 = bf16[3,22,3,1024]{3,1,2,0:T(8,128)(2,1)} collective-permute-done((bf16[3,22,3,1024]{3,1,2,0:T(8,128)(2,1)S(1)}, bf16[3,22,3,1024]{3,1,2,0:T(8,128)(2,1)}, u32[]{:S(2)}, u32[]{:S(2)}) %collective-permute-start.2) | collective-permute-done | bytes 405536 | tf_op jit(solution)/shard_map/ppermute | solution.py:18
  49.3 4.0 %copy_convert_fusion = f32[3,22,22,8,128]{4,3,2,1,0:T(8,128)} fusion(bf16[3,22,3,8,128]{4,3,1,2,0:T(8,128)(2,1)S(1)} %concatenate.37, bf16[3,22,16,8,128]{4,3,1,2,0:T(8,128)(2,1)} %reshape.205, bf16[3,22,3,8,128]{4,3,1,2,0:T(8,128)(2,1)S(1)} %concatenate.35), kind=kLoop, calls=%fused_computation.125 | loop fusion | flops 4460544 | bytes 8921088 | tf_op jit(solution)/shard_map/convert_element_type | solution.py:98
  53.4 62.4 %fusion.117 = (f32[3,16,16]{2,1,0:T(8,128)S(1)}, f32[3,16,16,8,128]{4,3,2,1,0:T(8,128)S(1)}) fusion(f32[8,128]{1,0:T(8,128)S(1)} %get-tuple-element.19, f32[3,22,22,8,128]{4,3,2,1,0:T(8,128)} %copy_convert_fusion, f32[8,128]{1,0:T(8,128)S(1)} %get-tuple-element.20, f32[8,128]{1,0:T(8,128)S(1)} %get-tuple-element.21, f32[8,128]{1,0:T(8,128)S(1)} %get-tuple-element.22, ...), kind=kLoop, calls=%fused_computation.254 | loop fusion | flops 77069568 | bytes 157490176 | tf_op jit(solution)/shard_map/reduce_sum | solution.py:25
  116.0 11.0 %multiply_reduce_fusion = f32[3,16,16]{2,1,0:T(8,128)S(1)} fusion(f32[3,16,16,8,128]{4,3,2,1,0:T(8,128)S(1)} %get-tuple-element.3, f32[3,16,16]{2,1,0:T(8,128)S(1)} %broadcast_multiply_fusion.1), kind=kLoop, calls=%fused_computation.123 | loop fusion | flops 2358528 | bytes 3151872 | tf_op jit(solution)/shard_map/reduce_sum | solution.py:27
  127.1 37.4 %fusion.65.clone.4 = bf16[768,4096]{1,0:T(8,128)(2,1)} fusion(bf16[1024,4096]{1,0:T(8,128)(2,1)} %all-gather.3.cloned.1.call-done, f32[96,8,8,128]{3,2,1,0:T(8,128)S(1)} %bitcast.186, f32[1024]{0:T(1024)S(1)} %copy-done.28, f32[768]{0:T(1024)S(1)} %rsqrt.12, f32[768]{0:T(1024)S(1)} %div.21), kind=kOutput, calls=%fused_computation.3.clone.clone.clone.clone.clone.clone.1 | convolution fusion | flops 6650068992 | bytes 17836032 | tf_op jit(solution)/shard_map/dot_general | solution.py:33
  164.4 12.5 %broadcast_multiply_fusion = (bf16[768,1024]{1,0:T(8,128)(2,1)S(1)}, bf16[768,1024]{1,0:T(8,128)(2,1)}) fusion(bf16[768]{0:T(1024)(128)(2,1)S(1)} %copy-done.27, bf16[1024,4096]{1,0:T(8,128)(2,1)} %all-gather.5.cloned.1.call-done, f32[1024]{0:T(1024)S(1)} %copy-done.29, bf16[768,1024]{1,0:T(8,128)(2,1)} %bitcast.188, bf16[768,4096]{1,0:T(8,128)(2,1)} %fusion.65.clone.4), kind=kOutput, calls=%fused_computation.138 | convolution fusion | flops 6446383104 | bytes 19404288 | tf_op jit(solution)/shard_map/dot_general | solution.py:38
  180.7 3.8 %fusion.78 = f32[512,1040]{0,1:T(8,128)} fusion(bf16[768,16]{1,0:T(8,128)(2,1)S(1)} %copy-done.2, bf16[768,1024]{1,0:T(8,128)(2,1)} %get-tuple-element.72, bf16[768,1024]{0,1:T(8,128)(2,1)S(1)} %reshape.182, s32[]{:T(128)S(6)} %select_n.201), kind=kOutput, calls=%fused_computation.132 | convolution fusion | flops 821084160 | bytes 4685828 | tf_op jit(solution)/shard_map/dot_general | solution.py:120
  184.5 2.6 collective-permute-start.4
  187.0 2.7 %fusion.79 = f32[512,1040]{0,1:T(8,128)S(1)} fusion(bf16[768,16]{1,0:T(8,128)(2,1)S(1)} %copy-done.2, bf16[768,1024]{1,0:T(8,128)(2,1)} %get-tuple-element.72, bf16[768,1024]{0,1:T(8,128)(2,1)} %copy-done.1, s32[]{:T(128)S(6)} %select_n.200), kind=kOutput, calls=%fused_computation.133 | convolution fusion | flops 821084160 | bytes 4513796 | tf_op jit(solution)/shard_map/dot_general | solution.py:120
  192.9 2.7 %reshape.183 = f32[2,2,128,1040]{2,1,0,3:T(2,128)S(1)} reshape(f32[512,1040]{0,1:T(8,128)} %add.352) | data formatting | bytes 4259840 | tf_op jit(solution)/shard_map/reshape | solution.py:66
  197.9 14.8 %collective-permute-done.5 = f32[256,1040]{0,1:T(8,128)S(1)} collective-permute-done((f32[256,1040]{0,1:T(8,128)S(1)}, f32[256,1040]{0,1:T(8,128)S(1)}, u32[]{:S(2)}, u32[]{:S(2)}) %collective-permute-start.5) | collective-permute-done | bytes 1064992 | tf_op jit(solution)/shard_map/ppermute | solution.py:85
  215.5 8.3 %collective-permute-done.6 = f32[128,1040]{0,1:T(8,128)S(1)} collective-permute-done((f32[128,1040]{0,1:T(8,128)S(1)}, f32[128,1040]{0,1:T(8,128)S(1)}, u32[]{:S(2)}, u32[]{:S(2)}) %collective-permute-start.6) | collective-permute-done | bytes 532512 | tf_op jit(solution)/shard_map/ppermute | solution.py:85
  224.4 6.7 %collective-permute-done.7 = f32[64,1040]{1,0:T(8,128)S(1)} collective-permute-done((f32[64,1040]{1,0:T(8,128)S(1)}, f32[64,1040]{1,0:T(8,128)S(1)}, u32[]{:S(2)}, u32[]{:S(2)}) %collective-permute-start.7) | collective-permute-done | bytes 266272 | tf_op jit(solution)/shard_map/ppermute | solution.py:85
  231.3 6.6 %collective-permute-done.8 = f32[32,1040]{1,0:T(8,128)S(1)} collective-permute-done((f32[32,1040]{1,0:T(8,128)S(1)}, f32[32,1040]{1,0:T(8,128)S(1)}, u32[]{:S(2)}, u32[]{:S(2)}) %collective-permute-start.8) | collective-permute-done | bytes 133152 | tf_op jit(solution)/shard_map/ppermute | solution.py:85
  238.1 6.2 %collective-permute-done.9 = f32[16,1040]{1,0:T(8,128)S(1)} collective-permute-done((f32[16,1040]{1,0:T(8,128)S(1)}, f32[16,1040]{1,0:T(8,128)S(1)}, u32[]{:S(2)}, u32[]{:S(2)}) %collective-permute-start.9) | collective-permute-done | bytes 66592 | tf_op jit(solution)/shard_map/ppermute | solution.py:85
  244.4 2.9 %collective-permute-start.10 = (f32[8,1040]{1,0:T(8,128)S(1)}, f32[8,1040]{1,0:T(8,128)S(1)}, u32[]{:S(2)}, u32[]{:S(2)}) collective-permute-start(f32[8,1040]{1,0:T(8,128)S(1)} %dynamic-slice_bitcast_fusion.5), channel_id=1, source_target_pairs={{0,128},{1,33},{2,130},{3,35},{4,132},{5,37},{6,134},{7,39},{8,136... | collective-permute-start | bytes 99848 | tf_op jit(solution)/shard_map/ppermute | solution.py:85
  247.3 2.6 collective-permute-done.10
  250.0 3.7 %collective-permute-start.11 = (f32[4,1040]{1,0:T(4,128)S(1)}, f32[4,1040]{1,0:T(4,128)S(1)}, u32[]{:S(2)}, u32[]{:S(2)}) collective-permute-start(f32[4,1040]{1,0:T(4,128)S(1)} %dynamic-slice_bitcast_fusion.10), channel_id=1, source_target_pairs={{0,64},{1,65},{2,66},{3,67},{4,68},{5,69},{6,70},{7,71},{8,72},{9,... | collective-permute-start | bytes 49928 | tf_op jit(solution)/shard_map/ppermute | solution.py:85
  253.7 4.0 %collective-permute-done.11 = f32[4,1040]{1,0:T(4,128)S(1)} collective-permute-done((f32[4,1040]{1,0:T(4,128)S(1)}, f32[4,1040]{1,0:T(4,128)S(1)}, u32[]{:S(2)}, u32[]{:S(2)}) %collective-permute-start.11) | collective-permute-done | bytes 16672 | tf_op jit(solution)/shard_map/ppermute | solution.py:85
  (124 shorter events, 29.7 us)
Async XLA Ops:
  7.2 10.4 %copy-start = (bf16[3,16,16,1024]{3,2,1,0:T(8,128)(2,1)S(1)}, bf16[3,16,16,1024]{3,2,1,0:T(8,128)(2,1)}, u32[]{:S(2)}) copy-start(bf16[3,16,16,1024]{3,2,1,0:T(8,128)(2,1)} %param.8) | copy-start | bytes 4718596
  7.2 12.5 %copy-start.3 = (bf16[7,7,1024]{2,1,0:T(8,128)(2,1)S(1)}, bf16[7,7,1024]{2,1,0:T(8,128)(2,1)}, u32[]{:S(2)}) copy-start(bf16[7,7,1024]{2,1,0:T(8,128)(2,1)} %param.9) | copy-start | bytes 301060
  7.2 12.6 %copy-start.4 = (s32[3,16,16]{2,1,0:T(8,128)S(1)}, s32[3,16,16]{2,1,0:T(8,128)}, u32[]{:S(2)}) copy-start(s32[3,16,16]{2,1,0:T(8,128)} %param.15) | copy-start | bytes 9220
  7.2 119.8 %all-gather.3.cloned.1.call-start = ((), (), s32[]{:S(2)}) async-start(), calls=%async_computation | async-start | bytes 8912896 | tf_op jit(solution)/shard_map/all_gather | solution.py:107
  7.9 156.5 %all-gather.5.cloned.1.call-start = ((), (), s32[]{:S(2)}) async-start(), calls=%async_computation.1 | async-start | bytes 8912896 | tf_op jit(solution)/shard_map/all_gather | solution.py:108
  9.8 11.5 %collective-permute-start = (bf16[3,3,16,1024]{3,2,1,0:T(8,128)(2,1)S(1)}, bf16[3,3,16,1024]{3,2,1,0:T(8,128)(2,1)S(1)}, u32[]{:S(2)}, u32[]{:S(2)}) collective-permute-start(bf16[3,3,16,1024]{3,2,1,0:T(8,128)(2,1)S(1)} %get-tuple-element.10), channel_id=1, source_target_pairs={{0,16},{16,32},{32,48},{48,64},{64,80},{80,96},{96,112},{112,128},... | collective-permute-start | bytes 884744 | tf_op jit(solution)/shard_map/ppermute | solution.py:18
  14.8 11.6 %collective-permute-start.1 = (bf16[3,3,16,1024]{3,2,1,0:T(8,128)(2,1)S(1)}, bf16[3,3,16,1024]{3,2,1,0:T(8,128)(2,1)S(1)}, u32[]{:S(2)}, u32[]{:S(2)}) collective-permute-start(bf16[3,3,16,1024]{3,2,1,0:T(8,128)(2,1)S(1)} %get-tuple-element.11), channel_id=1, source_target_pairs={{16,0},{32,16},{48,32},{64,48},{80,64},{96,80},{112,96},{128,112},... | collective-permute-start | bytes 884744 | tf_op jit(solution)/shard_map/ppermute | solution.py:19
  29.7 16.6 %collective-permute-start.2 = (bf16[3,22,3,1024]{3,1,2,0:T(8,128)(2,1)S(1)}, bf16[3,22,3,1024]{3,1,2,0:T(8,128)(2,1)}, u32[]{:S(2)}, u32[]{:S(2)}) collective-permute-start(bf16[3,22,3,1024]{3,1,2,0:T(8,128)(2,1)S(1)} %get-tuple-element.4), channel_id=1, source_target_pairs={{0,1},{1,2},{2,3},{3,4},{4,5},{5,6},{6,7},{7,8},{8,9},{9,10},{10,1... | collective-permute-start | bytes 1216520 | tf_op jit(solution)/shard_map/ppermute | solution.py:18
  31.6 16.1 %collective-permute-start.3 = (bf16[3,22,3,1024]{3,1,2,0:T(8,128)(2,1)S(1)}, bf16[3,22,3,1024]{3,1,2,0:T(8,128)(2,1)}, u32[]{:S(2)}, u32[]{:S(2)}) collective-permute-start(bf16[3,22,3,1024]{3,1,2,0:T(8,128)(2,1)S(1)} %get-tuple-element.5), channel_id=1, source_target_pairs={{1,0},{2,1},{3,2},{4,3},{5,4},{6,5},{7,6},{8,7},{9,8},{10,9},{11,1... | collective-permute-start | bytes 1216520 | tf_op jit(solution)/shard_map/ppermute | solution.py:19
  49.1 4.2 %copy-start.5 = (f32[8,128]{1,0:T(8,128)S(1)}, f32[8,128]{1,0:T(8,128)}, u32[]{:S(2)}) copy-start(f32[8,128]{1,0:T(8,128)} %get-tuple-element.64) | copy-start | bytes 12292
  49.1 4.2 %copy-start.6 = (f32[8,128]{1,0:T(8,128)S(1)}, f32[8,128]{1,0:T(8,128)}, u32[]{:S(2)}) copy-start(f32[8,128]{1,0:T(8,128)} %get-tuple-element.65) | copy-start | bytes 12292
  49.1 4.2 %copy-start.7 = (f32[8,128]{1,0:T(8,128)S(1)}, f32[8,128]{1,0:T(8,128)}, u32[]{:S(2)}) copy-start(f32[8,128]{1,0:T(8,128)} %get-tuple-element.66) | copy-start | bytes 12292
  49.1 4.2 %copy-start.8 = (f32[8,128]{1,0:T(8,128)S(1)}, f32[8,128]{1,0:T(8,128)}, u32[]{:S(2)}) copy-start(f32[8,128]{1,0:T(8,128)} %get-tuple-element.37) | copy-start | bytes 12292
  115.8 11.2 %copy-start.28 = (f32[1024]{0:T(1024)S(1)}, f32[1024]{0:T(1024)}, u32[]{:S(2)}) copy-start(f32[1024]{0:T(1024)} %param.10) | copy-start | bytes 12292
  127.0 37.4 %copy-start.27 = (bf16[768]{0:T(1024)(128)(2,1)S(1)}, bf16[768]{0:T(1024)(128)(2,1)}, u32[]{:S(2)}) copy-start(bf16[768]{0:T(1024)(128)(2,1)} %convert_element_type.45) | copy-start | bytes 4612
  127.0 37.4 %copy-start.29 = (f32[1024]{0:T(1024)S(1)}, f32[1024]{0:T(1024)}, u32[]{:S(2)}) copy-start(f32[1024]{0:T(1024)} %param.13) | copy-start | bytes 12292
  184.5 6.6 %collective-permute-start.4 = (f32[512,1040]{0,1:T(8,128)}, f32[512,1040]{0,1:T(8,128)S(1)}, u32[]{:S(2)}, u32[]{:S(2)}) collective-permute-start(f32[512,1040]{0,1:T(8,128)} %fusion.78), channel_id=1, source_target_pairs={{0,1},{1,0},{2,3},{3,2},{4,5},{5,4},{6,7},{7,6},{8,9},{9,8},{10,11... | collective-permute-start | bytes 6389768 | tf_op jit(solution)/shard_map/ppermute | solution.py:125
  197.6 15.1 %collective-permute-start.5 = (f32[256,1040]{0,1:T(8,128)S(1)}, f32[256,1040]{0,1:T(8,128)S(1)}, u32[]{:S(2)}, u32[]{:S(2)}) collective-permute-start(f32[256,1040]{0,1:T(8,128)S(1)} %pad_maximum_fusion.5), channel_id=1, source_target_pairs={{0,2},{1,9},{2,0},{3,11},{4,6},{5,13},{6,4},{7,15},{8,10},{9,1},{1... | collective-permute-start | bytes 3194888 | tf_op jit(solution)/shard_map/ppermute | solution.py:85
  214.5 9.4 %collective-permute-start.6 = (f32[128,1040]{0,1:T(8,128)S(1)}, f32[128,1040]{0,1:T(8,128)S(1)}, u32[]{:S(2)}, u32[]{:S(2)}) collective-permute-start(f32[128,1040]{0,1:T(8,128)S(1)} %bitcast.197), channel_id=1, source_target_pairs={{0,8},{1,3},{2,10},{3,1},{4,12},{5,7},{6,14},{7,5},{8,0},{9,11},{1... | collective-permute-start | bytes 1597448 | tf_op jit(solution)/shard_map/ppermute | solution.py:85
  224.3 6.8 %collective-permute-start.7 = (f32[64,1040]{1,0:T(8,128)S(1)}, f32[64,1040]{1,0:T(8,128)S(1)}, u32[]{:S(2)}, u32[]{:S(2)}) collective-permute-start(f32[64,1040]{1,0:T(8,128)S(1)} %pad_maximum_fusion.6), channel_id=1, source_target_pairs={{0,16},{1,5},{2,18},{3,7},{4,20},{5,1},{6,22},{7,3},{8,24},{9,13},... | collective-permute-start | bytes 798728 | tf_op jit(solution)/shard_map/ppermute | solution.py:85
  231.2 6.7 %collective-permute-start.8 = (f32[32,1040]{1,0:T(8,128)S(1)}, f32[32,1040]{1,0:T(8,128)S(1)}, u32[]{:S(2)}, u32[]{:S(2)}) collective-permute-start(f32[32,1040]{1,0:T(8,128)S(1)} %dynamic-slice_bitcast_fusion), channel_id=1, source_target_pairs={{0,4},{1,17},{2,6},{3,19},{4,0},{5,21},{6,2},{7,23},{8,12},{9,25},... | collective-permute-start | bytes 399368 | tf_op jit(solution)/shard_map/ppermute | solution.py:85
  238.0 6.4 %collective-permute-start.9 = (f32[16,1040]{1,0:T(8,128)S(1)}, f32[16,1040]{1,0:T(8,128)S(1)}, u32[]{:S(2)}, u32[]{:S(2)}) collective-permute-start(f32[16,1040]{1,0:T(8,128)S(1)} %pad_maximum_fusion.7), channel_id=1, source_target_pairs={{0,32},{1,129},{2,34},{3,131},{4,36},{5,133},{6,38},{7,135},{8,40}... | collective-permute-start | bytes 199688 | tf_op jit(solution)/shard_map/ppermute | solution.py:85
  244.4 5.5 %collective-permute-start.10 = (f32[8,1040]{1,0:T(8,128)S(1)}, f32[8,1040]{1,0:T(8,128)S(1)}, u32[]{:S(2)}, u32[]{:S(2)}) collective-permute-start(f32[8,1040]{1,0:T(8,128)S(1)} %dynamic-slice_bitcast_fusion.5), channel_id=1, source_target_pairs={{0,128},{1,33},{2,130},{3,35},{4,132},{5,37},{6,134},{7,39},{8,136... | collective-permute-start | bytes 99848 | tf_op jit(solution)/shard_map/ppermute | solution.py:85
  250.0 7.8 %collective-permute-start.11 = (f32[4,1040]{1,0:T(4,128)S(1)}, f32[4,1040]{1,0:T(4,128)S(1)}, u32[]{:S(2)}, u32[]{:S(2)}) collective-permute-start(f32[4,1040]{1,0:T(4,128)S(1)} %dynamic-slice_bitcast_fusion.10), channel_id=1, source_target_pairs={{0,64},{1,65},{2,66},{3,67},{4,68},{5,69},{6,70},{7,71},{8,72},{9,... | collective-permute-start | bytes 49928 | tf_op jit(solution)/shard_map/ppermute | solution.py:85
  (20 other events, 78.6 us)
Sparse Core Ops, SparseCore 0:
  9.8 67.4 all-gather.2
  79.0 62.7 all-gather.4

commit v2 on v1

--- a/solution.py
+++ b/solution.py
@@ -1,4 +1,5 @@
 import jax
+import numpy as np
 import jax.numpy as jnp
 from jax import lax
 from jax.sharding import PartitionSpec as P
@@ -29,9 +30,8 @@
 
 
 def expand(normed, piece):
-    return jax.nn.gelu(
-        jnp.dot(normed, piece, preferred_element_type=jnp.float32), approximate=False
-    ).astype(jnp.bfloat16)
+    pre = jnp.dot(normed, piece, preferred_element_type=jnp.float32)
+    return (0.5 * pre * (1.0 + lax.erf(pre * np.float32(np.sqrt(0.5))))).astype(jnp.bfloat16)
 
 
 def contract(hidden, piece):

time: 267 us -> 256 us (0.959); the launches traced: 266 us -> 251 us
  matrix products: 56.4 us -> 28.3 us
  waiting for transfers between devices: 64.1 us -> 74.9 us
    dot_general x1 -> x0, matrix products: 37.4 us -> none  [expand(): jnp.dot(normed, piece, preferred_element_type=jnp.float32)]
    all_gather x1, waiting for transfers between devices: 0.01 us -> 14.8 us  [on_device(): branch = contract(hidden, lax.all_gather(w_down, 'col', axis=1, tiled=True))]
    dot_general x1, matrix products: 12.5 us -> 21.8 us  [contract(): lax.dot_general(hidden, piece, (((1,), (1,)), ((), ())), preferred_elemen...]
    ppermute x7, starting transfers between devices: 7.33 us -> 11.9 us  [halving_sum(): part = keep + lax.ppermute(send, axes, pairs)]
    ppermute x7, waiting for transfers between devices: 49.3 us -> 45.3 us  [halving_sum(): part = keep + lax.ppermute(send, axes, pairs)]
  transfers between devices with their start and end apart: 14 -> 14, of which waited for: 11 -> 12; matrix products, arithmetic and copies ran while one was open for 50% -> 38% of each run, Pallas kernels for 0% -> 0%
where the time goes in v2:
time: 256 us; the launch traced here: 251 us
  other arithmetic  83.7 us (33%)
  waiting for transfers between devices  74.9 us (29%)
  matrix products  28.3 us (11%)
  local copies, waits for them, and re-layouts  25 us (10%)
  starting transfers between devices  24.7 us (10%)
  between operations  14.7 us (6%)
    reduce_sum x1, other arithmetic, apply_norm(): mean = jnp.mean(rows, axis=(-2, -1), keepdims=True)  62.4 us
    ppermute x7, waiting for transfers between devices, halving_sum(): part = keep + lax.ppermute(send, axes, pairs)  45.3 us
    dot_general x1, matrix products, contract(): lax.dot_general(hidden, piece, (((1,), (1,)), ((), ())), preferred_elemen...  21.8 us
    all_gather x1, waiting for transfers between devices, on_device(): branch = contract(hidden, lax.all_gather(w_down, 'col', axis=1, tiled=True))  14.8 us
    ppermute x7, starting transfers between devices, halving_sum(): part = keep + lax.ppermute(send, axes, pairs)  11.9 us
    reduce_sum x1, other arithmetic, apply_norm(): var = jnp.mean(centered * centered, axis=(-2, -1), keepdims=True)  11 us
    ppermute x2, starting transfers between devices, with_halo(): before = lax.ppermute(last, axis, up)  6.96 us
    ppermute x2, waiting for transfers between devices, with_halo(): before = lax.ppermute(last, axis, up)  6.95 us
  transfers between devices with their start and end apart: 14, of which 12 were waited for; matrix products, arithmetic and copies ran while one was open for 38% of the time, Pallas kernels for 0%

profile of v2, /device:TPU:120, one launch (start us, length us, event | category | flops | bytes accessed | tf_op | source)
XLA Modules:
  0.0 251.4 jit_solution(2399761944246311848)
XLA Ops:
  9.8 5.0 %collective-permute-start = (bf16[3,3,16,1024]{3,2,1,0:T(8,128)(2,1)S(1)}, bf16[3,3,16,1024]{3,2,1,0:T(8,128)(2,1)S(1)}, u32[]{:S(2)}, u32[]{:S(2)}) collective-permute-start(bf16[3,3,16,1024]{3,2,1,0:T(8,128)(2,1)S(1)} %get-tuple-element.10), channel_id=1, source_target_pairs={{0,16},{16,32},{32,48},{48,64},{64,80},{80,96},{96,112},{112,128},... | collective-permute-start | bytes 884744 | tf_op jit(solution)/shard_map/ppermute | solution.py:19
  21.6 4.9 %collective-permute-done.1 = bf16[3,3,16,1024]{3,2,1,0:T(8,128)(2,1)S(1)} collective-permute-done((bf16[3,3,16,1024]{3,2,1,0:T(8,128)(2,1)S(1)}, bf16[3,3,16,1024]{3,2,1,0:T(8,128)(2,1)S(1)}, u32[]{:S(2)}, u32[]{:S(2)}) %collective-permute-start.1) | collective-permute-done | bytes 294944 | tf_op jit(solution)/shard_map/ppermute | solution.py:20
  26.7 3.0 %pad_maximum_fusion.1 = bf16[3,22,16,1024]{3,1,2,0:T(8,128)(2,1)S(1)} fusion(bf16[3,3,16,1024]{3,1,2,0:T(4,128)(2,1)S(1)} %copy.62, bf16[3,16,16,1024]{3,1,2,0:T(8,128)(2,1)} %copy.61, bf16[3,3,16,1024]{3,1,2,0:T(4,128)(2,1)S(1)} %copy.60), kind=kLoop, calls=%fused_computation.108 | loop fusion | flops 6488064 | bytes 4325376 | tf_op jit(solution)/shard_map/concatenate | solution.py:21
  31.6 3.6 %collective-permute-start.3 = (bf16[3,22,3,1024]{3,1,2,0:T(8,128)(2,1)S(1)}, bf16[3,22,3,1024]{3,1,2,0:T(8,128)(2,1)}, u32[]{:S(2)}, u32[]{:S(2)}) collective-permute-start(bf16[3,22,3,1024]{3,1,2,0:T(8,128)(2,1)S(1)} %get-tuple-element.5), channel_id=1, source_target_pairs={{1,0},{2,1},{3,2},{4,3},{5,4},{6,5},{7,6},{8,7},{9,8},{10,9},{11,1... | collective-permute-start | bytes 1216520 | tf_op jit(solution)/shard_map/ppermute | solution.py:20
  36.6 2.8 %reshape.205 = bf16[3,22,16,8,128]{4,3,1,2,0:T(8,128)(2,1)} reshape(bf16[3,22,16,1024]{3,1,2,0:T(8,128)(2,1)S(1)} %pad_maximum_fusion.1) | data formatting | bytes 4325376 | tf_op jit(solution)/shard_map/concatenate | solution.py:21
  39.3 7.0 %collective-permute-done.2 = bf16[3,22,3,1024]{3,1,2,0:T(8,128)(2,1)} collective-permute-done((bf16[3,22,3,1024]{3,1,2,0:T(8,128)(2,1)S(1)}, bf16[3,22,3,1024]{3,1,2,0:T(8,128)(2,1)}, u32[]{:S(2)}, u32[]{:S(2)}) %collective-permute-start.2) | collective-permute-done | bytes 405536 | tf_op jit(solution)/shard_map/ppermute | solution.py:19
  49.3 4.0 %copy_convert_fusion = f32[3,22,22,8,128]{4,3,2,1,0:T(8,128)} fusion(bf16[3,22,3,8,128]{4,3,1,2,0:T(8,128)(2,1)S(1)} %concatenate.37, bf16[3,22,16,8,128]{4,3,1,2,0:T(8,128)(2,1)} %reshape.205, bf16[3,22,3,8,128]{4,3,1,2,0:T(8,128)(2,1)S(1)} %concatenate.35), kind=kLoop, calls=%fused_computation.107 | loop fusion | flops 4460544 | bytes 8921088 | tf_op jit(solution)/shard_map/convert_element_type | solution.py:98
  53.4 62.4 %fusion.77 = (f32[3,16,16]{2,1,0:T(8,128)S(1)}, f32[3,16,16,8,128]{4,3,2,1,0:T(8,128)S(1)}) fusion(f32[8,128]{1,0:T(8,128)S(1)} %get-tuple-element.19, f32[3,22,22,8,128]{4,3,2,1,0:T(8,128)} %copy_convert_fusion, f32[8,128]{1,0:T(8,128)S(1)} %get-tuple-element.20, f32[8,128]{1,0:T(8,128)S(1)} %get-tuple-element.21, f32[8,128]{1,0:T(8,128)S(1)} %get-tuple-element.22, ...), kind=kLoop, calls=%fused_computation.209 | loop fusion | flops 77069568 | bytes 157490176 | tf_op jit(solution)/shard_map/reduce_sum | solution.py:26
  116.0 11.0 %multiply_reduce_fusion = f32[3,16,16]{2,1,0:T(8,128)S(1)} fusion(f32[3,16,16,8,128]{4,3,2,1,0:T(8,128)S(1)} %get-tuple-element.3, f32[3,16,16]{2,1,0:T(8,128)S(1)} %broadcast_multiply_fusion.1), kind=kLoop, calls=%fused_computation.105 | loop fusion | flops 2358528 | bytes 3151872 | tf_op jit(solution)/shard_map/reduce_sum | solution.py:28
  127.1 14.8 %all-gather.5.cloned.1.call-done = bf16[1024,4096]{1,0:T(8,128)(2,1)} async-done(((bf16[1024,256]{1,0:T(8,128)(2,1)}), bf16[1024,4096]{1,0:T(8,128)(2,1)}) %all-gather.5.cloned.1.call-update) | async-done | bytes 8388624 | tf_op jit(solution)/shard_map/all_gather | solution.py:108
  141.8 21.8 %broadcast_multiply_fusion = (bf16[768,1024]{1,0:T(8,128)(2,1)}, bf16[768,1024]{1,0:T(8,128)(2,1)}) fusion(bf16[768]{0:T(1024)(128)(2,1)S(1)} %copy-done.27, bf16[1024,4096]{1,0:T(8,128)(2,1)} %all-gather.5.cloned.1.call-done, bf16[1024,4096]{1,0:T(8,128)(2,1)} %all-gather.3.cloned.1.call-done, f32[96,8,8,128]{3,2,1,0:T(8,128)S(1)} %bitcast.178, ...), kind=kOutput, calls=%fused_computation.120 | convolution fusion | flops 12910067712 | bytes 24657408 | tf_op jit(solution)/shard_map/dot_general | solution.py:38
  168.1 3.8 %fusion.65 = f32[512,1040]{0,1:T(8,128)} fusion(bf16[768,16]{1,0:T(8,128)(2,1)S(1)} %copy-done.2, bf16[768,1024]{1,0:T(8,128)(2,1)} %get-tuple-element.72, bf16[768,1024]{0,1:T(8,128)(2,1)S(1)} %reshape.182, s32[]{:T(128)S(6)} %select_n.201), kind=kOutput, calls=%fused_computation.114 | convolution fusion | flops 821084160 | bytes 4685828 | tf_op jit(solution)/shard_map/dot_general | solution.py:120
  172.1 2.7 %fusion.66 = f32[512,1040]{0,1:T(8,128)S(1)} fusion(bf16[768,16]{1,0:T(8,128)(2,1)S(1)} %copy-done.2, bf16[768,1024]{1,0:T(8,128)(2,1)} %get-tuple-element.72, bf16[768,1024]{0,1:T(8,128)(2,1)} %copy-done.1, s32[]{:T(128)S(6)} %select_n.200), kind=kOutput, calls=%fused_computation.115 | convolution fusion | flops 821084160 | bytes 4513796 | tf_op jit(solution)/shard_map/dot_general | solution.py:120
  178.1 2.7 %reshape.183 = f32[2,2,128,1040]{2,1,0,3:T(2,128)S(1)} reshape(f32[512,1040]{0,1:T(8,128)} %add.360) | data formatting | bytes 4259840 | tf_op jit(solution)/shard_map/reshape | solution.py:66
  184.1 13.8 %collective-permute-done.5 = f32[256,1040]{0,1:T(8,128)S(1)} collective-permute-done((f32[256,1040]{0,1:T(8,128)S(1)}, f32[256,1040]{0,1:T(8,128)S(1)}, u32[]{:S(2)}, u32[]{:S(2)}) %collective-permute-start.5) | collective-permute-done | bytes 1064992 | tf_op jit(solution)/shard_map/ppermute | solution.py:85
  201.4 7.7 %collective-permute-done.6 = f32[128,1040]{0,1:T(8,128)S(1)} collective-permute-done((f32[128,1040]{0,1:T(8,128)S(1)}, f32[128,1040]{0,1:T(8,128)S(1)}, u32[]{:S(2)}, u32[]{:S(2)}) %collective-permute-start.6) | collective-permute-done | bytes 532512 | tf_op jit(solution)/shard_map/ppermute | solution.py:85
  210.1 6.3 %collective-permute-done.7 = f32[64,1040]{1,0:T(8,128)S(1)} collective-permute-done((f32[64,1040]{1,0:T(8,128)S(1)}, f32[64,1040]{1,0:T(8,128)S(1)}, u32[]{:S(2)}, u32[]{:S(2)}) %collective-permute-start.7) | collective-permute-done | bytes 266272 | tf_op jit(solution)/shard_map/ppermute | solution.py:85
  216.4 2.5 collective-permute-start.8
  218.9 4.2 %collective-permute-done.8 = f32[32,1040]{1,0:T(8,128)S(1)} collective-permute-done((f32[32,1040]{1,0:T(8,128)S(1)}, f32[32,1040]{1,0:T(8,128)S(1)}, u32[]{:S(2)}, u32[]{:S(2)}) %collective-permute-start.8) | collective-permute-done | bytes 133152 | tf_op jit(solution)/shard_map/ppermute | solution.py:85
  223.7 6.3 %collective-permute-done.9 = f32[16,1040]{1,0:T(8,128)S(1)} collective-permute-done((f32[16,1040]{1,0:T(8,128)S(1)}, f32[16,1040]{1,0:T(8,128)S(1)}, u32[]{:S(2)}, u32[]{:S(2)}) %collective-permute-start.9) | collective-permute-done | bytes 66592 | tf_op jit(solution)/shard_map/ppermute | solution.py:85
  230.1 3.1 %collective-permute-start.10 = (f32[8,1040]{1,0:T(8,128)S(1)}, f32[8,1040]{1,0:T(8,128)S(1)}, u32[]{:S(2)}, u32[]{:S(2)}) collective-permute-start(f32[8,1040]{1,0:T(8,128)S(1)} %dynamic-slice_bitcast_fusion.5), channel_id=1, source_target_pairs={{0,128},{1,33},{2,130},{3,35},{4,132},{5,37},{6,134},{7,39},{8,136... | collective-permute-start | bytes 99848 | tf_op jit(solution)/shard_map/ppermute | solution.py:85
  233.1 2.5 collective-permute-done.10
  235.6 3.2 %collective-permute-start.11 = (f32[4,1040]{1,0:T(4,128)S(1)}, f32[4,1040]{1,0:T(4,128)S(1)}, u32[]{:S(2)}, u32[]{:S(2)}) collective-permute-start(f32[4,1040]{1,0:T(4,128)S(1)} %dynamic-slice_bitcast_fusion.10), channel_id=1, source_target_pairs={{0,64},{1,65},{2,66},{3,67},{4,68},{5,69},{6,70},{7,71},{8,72},{9,... | collective-permute-start | bytes 49928 | tf_op jit(solution)/shard_map/ppermute | solution.py:85
  238.8 4.6 %collective-permute-done.11 = f32[4,1040]{1,0:T(4,128)S(1)} collective-permute-done((f32[4,1040]{1,0:T(4,128)S(1)}, f32[4,1040]{1,0:T(4,128)S(1)}, u32[]{:S(2)}, u32[]{:S(2)}) %collective-permute-start.11) | collective-permute-done | bytes 16672 | tf_op jit(solution)/shard_map/ppermute | solution.py:85
  (123 shorter events, 33.3 us)
Async XLA Ops:
  7.2 10.4 %copy-start = (bf16[3,16,16,1024]{3,2,1,0:T(8,128)(2,1)S(1)}, bf16[3,16,16,1024]{3,2,1,0:T(8,128)(2,1)}, u32[]{:S(2)}) copy-start(bf16[3,16,16,1024]{3,2,1,0:T(8,128)(2,1)} %param.8) | copy-start | bytes 4718596
  7.2 12.5 %copy-start.3 = (bf16[7,7,1024]{2,1,0:T(8,128)(2,1)S(1)}, bf16[7,7,1024]{2,1,0:T(8,128)(2,1)}, u32[]{:S(2)}) copy-start(bf16[7,7,1024]{2,1,0:T(8,128)(2,1)} %param.9) | copy-start | bytes 301060
  7.2 12.6 %copy-start.4 = (s32[3,16,16]{2,1,0:T(8,128)S(1)}, s32[3,16,16]{2,1,0:T(8,128)}, u32[]{:S(2)}) copy-start(s32[3,16,16]{2,1,0:T(8,128)} %param.15) | copy-start | bytes 9220
  7.2 119.9 %all-gather.3.cloned.1.call-start = ((), (), s32[]{:S(2)}) async-start(), calls=%async_computation | async-start | bytes 8912896 | tf_op jit(solution)/shard_map/all_gather | solution.py:107
  7.9 133.9 %all-gather.5.cloned.1.call-start = ((), (), s32[]{:S(2)}) async-start(), calls=%async_computation.1 | async-start | bytes 8912896 | tf_op jit(solution)/shard_map/all_gather | solution.py:108
  9.8 11.5 %collective-permute-start = (bf16[3,3,16,1024]{3,2,1,0:T(8,128)(2,1)S(1)}, bf16[3,3,16,1024]{3,2,1,0:T(8,128)(2,1)S(1)}, u32[]{:S(2)}, u32[]{:S(2)}) collective-permute-start(bf16[3,3,16,1024]{3,2,1,0:T(8,128)(2,1)S(1)} %get-tuple-element.10), channel_id=1, source_target_pairs={{0,16},{16,32},{32,48},{48,64},{64,80},{80,96},{96,112},{112,128},... | collective-permute-start | bytes 884744 | tf_op jit(solution)/shard_map/ppermute | solution.py:19
  14.8 11.6 %collective-permute-start.1 = (bf16[3,3,16,1024]{3,2,1,0:T(8,128)(2,1)S(1)}, bf16[3,3,16,1024]{3,2,1,0:T(8,128)(2,1)S(1)}, u32[]{:S(2)}, u32[]{:S(2)}) collective-permute-start(bf16[3,3,16,1024]{3,2,1,0:T(8,128)(2,1)S(1)} %get-tuple-element.11), channel_id=1, source_target_pairs={{16,0},{32,16},{48,32},{64,48},{80,64},{96,80},{112,96},{128,112},... | collective-permute-start | bytes 884744 | tf_op jit(solution)/shard_map/ppermute | solution.py:20
  29.7 16.6 %collective-permute-start.2 = (bf16[3,22,3,1024]{3,1,2,0:T(8,128)(2,1)S(1)}, bf16[3,22,3,1024]{3,1,2,0:T(8,128)(2,1)}, u32[]{:S(2)}, u32[]{:S(2)}) collective-permute-start(bf16[3,22,3,1024]{3,1,2,0:T(8,128)(2,1)S(1)} %get-tuple-element.4), channel_id=1, source_target_pairs={{0,1},{1,2},{2,3},{3,4},{4,5},{5,6},{6,7},{7,8},{8,9},{9,10},{10,1... | collective-permute-start | bytes 1216520 | tf_op jit(solution)/shard_map/ppermute | solution.py:19
  31.6 16.1 %collective-permute-start.3 = (bf16[3,22,3,1024]{3,1,2,0:T(8,128)(2,1)S(1)}, bf16[3,22,3,1024]{3,1,2,0:T(8,128)(2,1)}, u32[]{:S(2)}, u32[]{:S(2)}) collective-permute-start(bf16[3,22,3,1024]{3,1,2,0:T(8,128)(2,1)S(1)} %get-tuple-element.5), channel_id=1, source_target_pairs={{1,0},{2,1},{3,2},{4,3},{5,4},{6,5},{7,6},{8,7},{9,8},{10,9},{11,1... | collective-permute-start | bytes 1216520 | tf_op jit(solution)/shard_map/ppermute | solution.py:20
  49.1 4.2 %copy-start.5 = (f32[8,128]{1,0:T(8,128)S(1)}, f32[8,128]{1,0:T(8,128)}, u32[]{:S(2)}) copy-start(f32[8,128]{1,0:T(8,128)} %get-tuple-element.64) | copy-start | bytes 12292
  49.1 4.2 %copy-start.6 = (f32[8,128]{1,0:T(8,128)S(1)}, f32[8,128]{1,0:T(8,128)}, u32[]{:S(2)}) copy-start(f32[8,128]{1,0:T(8,128)} %get-tuple-element.65) | copy-start | bytes 12292
  49.1 4.2 %copy-start.7 = (f32[8,128]{1,0:T(8,128)S(1)}, f32[8,128]{1,0:T(8,128)}, u32[]{:S(2)}) copy-start(f32[8,128]{1,0:T(8,128)} %get-tuple-element.66) | copy-start | bytes 12292
  49.1 4.2 %copy-start.8 = (f32[8,128]{1,0:T(8,128)S(1)}, f32[8,128]{1,0:T(8,128)}, u32[]{:S(2)}) copy-start(f32[8,128]{1,0:T(8,128)} %get-tuple-element.37) | copy-start | bytes 12292
  115.8 26.0 %copy-start.27 = (bf16[768]{0:T(1024)(128)(2,1)S(1)}, bf16[768]{0:T(1024)(128)(2,1)}, u32[]{:S(2)}) copy-start(bf16[768]{0:T(1024)(128)(2,1)} %convert_element_type.45) | copy-start | bytes 4612
  115.9 26.0 %copy-start.28 = (f32[1024]{0:T(1024)S(1)}, f32[1024]{0:T(1024)}, u32[]{:S(2)}) copy-start(f32[1024]{0:T(1024)} %param.10) | copy-start | bytes 12292
  115.9 25.9 %copy-start.29 = (f32[1024]{0:T(1024)S(1)}, f32[1024]{0:T(1024)}, u32[]{:S(2)}) copy-start(f32[1024]{0:T(1024)} %param.13) | copy-start | bytes 12292
  171.9 4.4 %collective-permute-start.4 = (f32[512,1040]{0,1:T(8,128)}, f32[512,1040]{0,1:T(8,128)S(1)}, u32[]{:S(2)}, u32[]{:S(2)}) collective-permute-start(f32[512,1040]{0,1:T(8,128)} %fusion.65), channel_id=1, source_target_pairs={{0,1},{1,0},{2,3},{3,2},{4,5},{5,4},{6,7},{7,6},{8,9},{9,8},{10,11... | collective-permute-start | bytes 6389768 | tf_op jit(solution)/shard_map/ppermute | solution.py:125
  182.8 15.1 %collective-permute-start.5 = (f32[256,1040]{0,1:T(8,128)S(1)}, f32[256,1040]{0,1:T(8,128)S(1)}, u32[]{:S(2)}, u32[]{:S(2)}) collective-permute-start(f32[256,1040]{0,1:T(8,128)S(1)} %pad_maximum_fusion.5), channel_id=1, source_target_pairs={{0,2},{1,9},{2,0},{3,11},{4,6},{5,13},{6,4},{7,15},{8,10},{9,1},{1... | collective-permute-start | bytes 3194888 | tf_op jit(solution)/shard_map/ppermute | solution.py:85
  199.7 9.4 %collective-permute-start.6 = (f32[128,1040]{0,1:T(8,128)S(1)}, f32[128,1040]{0,1:T(8,128)S(1)}, u32[]{:S(2)}, u32[]{:S(2)}) collective-permute-start(f32[128,1040]{0,1:T(8,128)S(1)} %bitcast.189), channel_id=1, source_target_pairs={{0,8},{1,3},{2,10},{3,1},{4,12},{5,7},{6,14},{7,5},{8,0},{9,11},{1... | collective-permute-start | bytes 1597448 | tf_op jit(solution)/shard_map/ppermute | solution.py:85
  209.5 6.8 %collective-permute-start.7 = (f32[64,1040]{1,0:T(8,128)S(1)}, f32[64,1040]{1,0:T(8,128)S(1)}, u32[]{:S(2)}, u32[]{:S(2)}) collective-permute-start(f32[64,1040]{1,0:T(8,128)S(1)} %pad_maximum_fusion.6), channel_id=1, source_target_pairs={{0,16},{1,5},{2,18},{3,7},{4,20},{5,1},{6,22},{7,3},{8,24},{9,13},... | collective-permute-start | bytes 798728 | tf_op jit(solution)/shard_map/ppermute | solution.py:85
  216.4 6.7 %collective-permute-start.8 = (f32[32,1040]{1,0:T(8,128)S(1)}, f32[32,1040]{1,0:T(8,128)S(1)}, u32[]{:S(2)}, u32[]{:S(2)}) collective-permute-start(f32[32,1040]{1,0:T(8,128)S(1)} %dynamic-slice_bitcast_fusion), channel_id=1, source_target_pairs={{0,4},{1,17},{2,6},{3,19},{4,0},{5,21},{6,2},{7,23},{8,12},{9,25},... | collective-permute-start | bytes 399368 | tf_op jit(solution)/shard_map/ppermute | solution.py:85
  223.2 6.8 %collective-permute-start.9 = (f32[16,1040]{1,0:T(8,128)S(1)}, f32[16,1040]{1,0:T(8,128)S(1)}, u32[]{:S(2)}, u32[]{:S(2)}) collective-permute-start(f32[16,1040]{1,0:T(8,128)S(1)} %pad_maximum_fusion.7), channel_id=1, source_target_pairs={{0,32},{1,129},{2,34},{3,131},{4,36},{5,133},{6,38},{7,135},{8,40}... | collective-permute-start | bytes 199688 | tf_op jit(solution)/shard_map/ppermute | solution.py:85
  230.1 5.5 %collective-permute-start.10 = (f32[8,1040]{1,0:T(8,128)S(1)}, f32[8,1040]{1,0:T(8,128)S(1)}, u32[]{:S(2)}, u32[]{:S(2)}) collective-permute-start(f32[8,1040]{1,0:T(8,128)S(1)} %dynamic-slice_bitcast_fusion.5), channel_id=1, source_target_pairs={{0,128},{1,33},{2,130},{3,35},{4,132},{5,37},{6,134},{7,39},{8,136... | collective-permute-start | bytes 99848 | tf_op jit(solution)/shard_map/ppermute | solution.py:85
  235.6 7.8 %collective-permute-start.11 = (f32[4,1040]{1,0:T(4,128)S(1)}, f32[4,1040]{1,0:T(4,128)S(1)}, u32[]{:S(2)}, u32[]{:S(2)}) collective-permute-start(f32[4,1040]{1,0:T(4,128)S(1)} %dynamic-slice_bitcast_fusion.10), channel_id=1, source_target_pairs={{0,64},{1,65},{2,66},{3,67},{4,68},{5,69},{6,70},{7,71},{8,72},{9,... | collective-permute-start | bytes 49928 | tf_op jit(solution)/shard_map/ppermute | solution.py:85
  (20 other events, 78.6 us)
Sparse Core Ops, SparseCore 0:
  9.8 67.4 all-gather.2
  79.0 62.7 all-gather.4

commit v3 on v2

--- a/solution.py
+++ b/solution.py
@@ -2,10 +2,11 @@
 import numpy as np
 import jax.numpy as jnp
 from jax import lax
-from jax.sharding import PartitionSpec as P
+from jax.sharding import Mesh, PartitionSpec as P
 
 NCLS = 16
 KSIZE = 7
+COL = ("chip", "core")
 LANES = 128
 
 
@@ -92,10 +93,15 @@
     return (onehot - 1.0 / NCLS).astype(jnp.bfloat16)
 
 
+def gather_hidden(piece):
+    across = lax.all_gather(piece, COL[0], axis=1, tiled=True)
+    return lax.all_gather(across, COL[1], axis=1, tiled=True)
+
+
 def on_device(features, dw_kernel, ln_gain, w_in, w_down, gamma, labels, valid):
     tiles, high, wide, width = features.shape
     tile = (width // LANES, LANES)
-    padded = with_halo(features, (("row", 1), ("col", 2)), 3).astype(jnp.float32)
+    padded = with_halo(features, (("row", 1), (COL, 2)), 3).astype(jnp.float32)
     padded = padded.reshape(padded.shape[:3] + tile)
     kernel = dw_kernel.astype(jnp.float32).reshape((KSIZE, KSIZE) + tile)
     conv = jnp.zeros((tiles, high, wide) + tile, jnp.float32)
@@ -104,12 +110,12 @@
             conv = conv + padded[:, i : i + high, j : j + wide] * kernel[i, j]
     count = tiles * high * wide
     normed = apply_norm(conv.reshape(count, *tile), ln_gain.reshape(tile)).reshape(count, width)
-    hidden = expand(normed, lax.all_gather(w_in, "col", axis=1, tiled=True))
-    branch = contract(hidden, lax.all_gather(w_down, "col", axis=1, tiled=True))
+    hidden = expand(normed, gather_hidden(w_in))
+    branch = contract(hidden, gather_hidden(w_down))
     out = (features.reshape(count, width).astype(jnp.float32) + gamma * branch).astype(jnp.bfloat16)
     keep = valid.reshape(count, 1)
     masked = out * keep.astype(jnp.bfloat16)
-    axes = ("row", "col")
+    axes = ("row",) + COL
     core = lax.axis_index(axes) & 1
     ordered = halving_order(masked)
     rhs = jnp.concatenate([out, targets_of(labels, count)], axis=1)
@@ -121,29 +127,31 @@
             lhs, rhs, (((0,), (0,)), ((), ())), preferred_element_type=jnp.float32
         )
 
-    size = lax.axis_size("row") * lax.axis_size("col")
+    size = lax.axis_size("row") * lax.axis_size(COL)
     sent = lax.ppermute(rows_of(1 - core), axes, [(i, i ^ 1) for i in range(size)])
     kept = lax.optimization_barrier(rows_of(core))
     summed = halving_sum(kept + sent, axes, 1)
     gram_sum, cross_sum = summed[:, :width], summed[:, width:]
-    total = float(tiles * high * lax.axis_size("row") * wide * lax.axis_size("col"))
+    total = float(tiles * high * lax.axis_size("row") * wide * lax.axis_size(COL))
     return (gram_sum / total, cross_sum / jnp.sqrt(jnp.float32(total)))
 
 
 def solution(mesh):
+    rows, cols = mesh.devices.shape
+    fine = Mesh(mesh.devices.reshape(rows, cols // 2, 2), ("row",) + COL)
     return jax.shard_map(
         on_device,
-        mesh=mesh,
+        mesh=fine,
         in_specs=(
-            P(None, "row", "col", None),
+            P(None, "row", COL, None),
             P(),
             P(),
-            P(None, "col"),
-            P(None, "col"),
+            P(None, COL),
+            P(None, COL),
             P(),
-            P(None, "row", "col"),
-            P(None, "row", "col"),
+            P(None, "row", COL),
+            P(None, "row", COL),
         ),
-        out_specs=(P(("row", "col"), None), P(("row", "col"), None)),
+        out_specs=(P(("row",) + COL, None), P(("row",) + COL, None)),
         check_vma=False,
     )

time: 256 us -> 363 us (1.42); the launches traced: 251 us -> 363 us
  waiting for transfers between devices: 74.9 us -> 187 us
    all_gather x2 -> x4, waiting for transfers between devices: 14.8 us -> 130 us  [the longest x2 130 us: gather_hidden(): across = lax.all_gather(piece, COL[0], axis=1, tiled=True)]
    ppermute x2, waiting for transfers between devices: 6.95 us -> 0.16 us  [with_halo(): before = lax.ppermute(last, axis, up)]
    ppermute x7, starting transfers between devices: 11.9 us -> 7.43 us  [halving_sum(): part = keep + lax.ppermute(send, axes, pairs)]
    ppermute x7, waiting for transfers between devices: 45.3 us -> 49.2 us  [halving_sum(): part = keep + lax.ppermute(send, axes, pairs)]
  transfers between devices with their start and end apart: 14 -> 16, of which waited for: 12 -> 13; matrix products, arithmetic and copies ran while one was open for 38% -> 27% of each run, Pallas kernels for 0% -> 0%
where the time goes in v3:
time: 363 us
  waiting for transfers between devices  187 us (52%)
  other arithmetic  86.4 us (24%)
  matrix products  28.3 us (8%)
  starting transfers between devices  23.4 us (6%)
  local copies, waits for them, and re-layouts  23.2 us (6%)
  between operations  14.6 us (4%)
    all_gather x2, waiting for transfers between devices, gather_hidden(): across = lax.all_gather(piece, COL[0], axis=1, tiled=True)  130 us
    reduce_sum x1, other arithmetic, apply_norm(): mean = jnp.mean(rows, axis=(-2, -1), keepdims=True)  64.9 us
    ppermute x7, waiting for transfers between devices, halving_sum(): part = keep + lax.ppermute(send, axes, pairs)  49.2 us
    dot_general x1, matrix products, contract(): lax.dot_general(hidden, piece, (((1,), (1,)), ((), ())), preferred_elemen...  21.8 us
    reduce_sum x1, other arithmetic, apply_norm(): var = jnp.mean(centered * centered, axis=(-2, -1), keepdims=True)  11 us
    ppermute x7, starting transfers between devices, halving_sum(): part = keep + lax.ppermute(send, axes, pairs)  7.43 us
  transfers between devices with their start and end apart: 16, of which 13 were waited for; matrix products, arithmetic and copies ran while one was open for 27% of the time, Pallas kernels for 0%

profile of v3, /device:TPU:120, one launch (start us, length us, event | category | flops | bytes accessed | tf_op | source)
XLA Modules:
  0.0 362.8 jit_solution(11651615008758052240)
XLA Ops:
  8.7 65.1 %all-gather.9.cloned.1.call-done = bf16[1024,2048]{1,0:T(8,128)(2,1)} async-done(((bf16[1024,256]{1,0:T(8,128)(2,1)}), bf16[1024,2048]{1,0:T(8,128)(2,1)}) %all-gather.9.cloned.1.call-update) | async-done | bytes 4194320 | tf_op jit(solution)/shard_map/all_gather | solution.py:97
  73.9 65.4 %all-gather.5.cloned.1.call-done = bf16[1024,2048]{1,0:T(8,128)(2,1)} async-done(((bf16[1024,256]{1,0:T(8,128)(2,1)}), bf16[1024,2048]{1,0:T(8,128)(2,1)}) %all-gather.5.cloned.1.call-update) | async-done | bytes 4194320 | tf_op jit(solution)/shard_map/all_gather | solution.py:97
  139.4 4.7 %collective-permute-start = (bf16[3,3,16,1024]{3,2,1,0:T(8,128)(2,1)S(1)}, bf16[3,3,16,1024]{3,2,1,0:T(8,128)(2,1)S(1)}, u32[]{:S(2)}, u32[]{:S(2)}) collective-permute-start(bf16[3,3,16,1024]{3,2,1,0:T(8,128)(2,1)S(1)} %get-tuple-element.10), channel_id=1, source_target_pairs={{0,16},{16,32},{32,48},{48,64},{64,80},{80,96},{96,112},{112,128},... | collective-permute-start | bytes 884744 | tf_op jit(solution)/shard_map/ppermute | solution.py:20
  150.1 3.8 %collective-permute-done.1 = bf16[3,3,16,1024]{3,2,1,0:T(8,128)(2,1)S(1)} collective-permute-done((bf16[3,3,16,1024]{3,2,1,0:T(8,128)(2,1)S(1)}, bf16[3,3,16,1024]{3,2,1,0:T(8,128)(2,1)S(1)}, u32[]{:S(2)}, u32[]{:S(2)}) %collective-permute-start.1) | collective-permute-done | bytes 294944 | tf_op jit(solution)/shard_map/ppermute | solution.py:21
  154.1 3.2 pad_maximum_fusion.1
  159.4 3.6 %collective-permute-start.3 = (bf16[3,22,3,1024]{3,1,2,0:T(8,128)(2,1)S(1)}, bf16[3,22,3,1024]{3,1,2,0:T(8,128)(2,1)}, u32[]{:S(2)}, u32[]{:S(2)}) collective-permute-start(bf16[3,22,3,1024]{3,1,2,0:T(8,128)(2,1)S(1)} %get-tuple-element.5), channel_id=1, source_target_pairs={{1,0},{2,1},{3,2},{4,3},{5,4},{6,5},{7,6},{8,7},{9,8},{10,9},{11,1... | collective-permute-start | bytes 1216520 | tf_op jit(solution)/shard_map/ppermute | solution.py:21
  164.3 2.7 reshape.205
  170.3 3.9 %copy_convert_fusion = f32[3,22,22,8,128]{4,3,2,1,0:T(8,128)} fusion(bf16[3,22,3,8,128]{4,3,1,2,0:T(8,128)(2,1)S(1)} %concatenate.37, bf16[3,22,16,8,128]{4,3,1,2,0:T(8,128)(2,1)} %reshape.205, bf16[3,22,3,8,128]{4,3,1,2,0:T(8,128)(2,1)S(1)} %concatenate.35), kind=kLoop, calls=%fused_computation.107 | loop fusion | flops 4460544 | bytes 8921088 | tf_op jit(solution)/shard_map/convert_element_type | solution.py:104
  174.4 64.9 %fusion.77 = (f32[3,16,16]{2,1,0:T(8,128)S(1)}, f32[3,16,16,8,128]{4,3,2,1,0:T(8,128)S(1)}) fusion(f32[8,128]{1,0:T(8,128)S(1)} %get-tuple-element.19, f32[3,22,22,8,128]{4,3,2,1,0:T(8,128)} %copy_convert_fusion, f32[8,128]{1,0:T(8,128)S(1)} %get-tuple-element.20, f32[8,128]{1,0:T(8,128)S(1)} %get-tuple-element.21, f32[8,128]{1,0:T(8,128)S(1)} %get-tuple-element.22, ...), kind=kLoop, calls=%fused_computation.209 | loop fusion | flops 77069568 | bytes 157490176 | tf_op jit(solution)/shard_map/reduce_sum | solution.py:27
  239.4 11.0 %multiply_reduce_fusion = f32[3,16,16]{2,1,0:T(8,128)S(1)} fusion(f32[3,16,16,8,128]{4,3,2,1,0:T(8,128)S(1)} %get-tuple-element.3, f32[3,16,16]{2,1,0:T(8,128)S(1)} %broadcast_multiply_fusion.1), kind=kLoop, calls=%fused_computation.105 | loop fusion | flops 2358528 | bytes 3151872 | tf_op jit(solution)/shard_map/reduce_sum | solution.py:29
  250.6 21.8 %broadcast_multiply_fusion = (bf16[768,1024]{1,0:T(8,128)(2,1)}, bf16[768,1024]{1,0:T(8,128)(2,1)}) fusion(bf16[768]{0:T(1024)(128)(2,1)S(1)} %copy-done.28, bf16[1024,4096]{1,0:T(8,128)(2,1)} %all-gather.11.cloned.1.call-done, bf16[1024,4096]{1,0:T(8,128)(2,1)} %all-gather.7.cloned.1.call-done, f32[96,8,8,128]{3,2,1,0:T(8,128)S(1)} %bitcast.178, ...), kind=kOutput, calls=%fused_computation.120 | convolution fusion | flops 12910067712 | bytes 24657408 | tf_op jit(solution)/shard_map/dot_general | solution.py:39
  276.9 3.8 %fusion.65 = f32[512,1040]{0,1:T(8,128)} fusion(bf16[768,16]{1,0:T(8,128)(2,1)S(1)} %copy-done.2, bf16[768,1024]{1,0:T(8,128)(2,1)} %get-tuple-element.72, bf16[768,1024]{0,1:T(8,128)(2,1)S(1)} %reshape.182, s32[]{:T(128)S(6)} %select_n.201), kind=kOutput, calls=%fused_computation.114 | convolution fusion | flops 821084160 | bytes 4685828 | tf_op jit(solution)/shard_map/dot_general | solution.py:126
  280.7 3.7 %collective-permute-start.4 = (f32[512,1040]{0,1:T(8,128)}, f32[512,1040]{0,1:T(8,128)S(1)}, u32[]{:S(2)}, u32[]{:S(2)}) collective-permute-start(f32[512,1040]{0,1:T(8,128)} %fusion.65), channel_id=1, source_target_pairs={{0,1},{1,0},{2,3},{3,2},{4,5},{5,4},{6,7},{7,6},{8,9},{9,8},{10,11... | collective-permute-start | bytes 6389768 | tf_op jit(solution)/shard_map/ppermute | solution.py:131
  284.4 2.7 fusion.66
  290.3 2.7 reshape.183
  295.1 14.9 %collective-permute-done.5 = f32[256,1040]{0,1:T(8,128)S(1)} collective-permute-done((f32[256,1040]{0,1:T(8,128)S(1)}, f32[256,1040]{0,1:T(8,128)S(1)}, u32[]{:S(2)}, u32[]{:S(2)}) %collective-permute-start.5) | collective-permute-done | bytes 1064992 | tf_op jit(solution)/shard_map/ppermute | solution.py:86
  312.9 8.3 %collective-permute-done.6 = f32[128,1040]{0,1:T(8,128)S(1)} collective-permute-done((f32[128,1040]{0,1:T(8,128)S(1)}, f32[128,1040]{0,1:T(8,128)S(1)}, u32[]{:S(2)}, u32[]{:S(2)}) %collective-permute-start.6) | collective-permute-done | bytes 532512 | tf_op jit(solution)/shard_map/ppermute | solution.py:86
  321.7 6.7 %collective-permute-done.7 = f32[64,1040]{1,0:T(8,128)S(1)} collective-permute-done((f32[64,1040]{1,0:T(8,128)S(1)}, f32[64,1040]{1,0:T(8,128)S(1)}, u32[]{:S(2)}, u32[]{:S(2)}) %collective-permute-start.7) | collective-permute-done | bytes 266272 | tf_op jit(solution)/shard_map/ppermute | solution.py:86
  328.6 6.6 %collective-permute-done.8 = f32[32,1040]{1,0:T(8,128)S(1)} collective-permute-done((f32[32,1040]{1,0:T(8,128)S(1)}, f32[32,1040]{1,0:T(8,128)S(1)}, u32[]{:S(2)}, u32[]{:S(2)}) %collective-permute-start.8) | collective-permute-done | bytes 133152 | tf_op jit(solution)/shard_map/ppermute | solution.py:86
  335.4 6.2 %collective-permute-done.9 = f32[16,1040]{1,0:T(8,128)S(1)} collective-permute-done((f32[16,1040]{1,0:T(8,128)S(1)}, f32[16,1040]{1,0:T(8,128)S(1)}, u32[]{:S(2)}, u32[]{:S(2)}) %collective-permute-start.9) | collective-permute-done | bytes 66592 | tf_op jit(solution)/shard_map/ppermute | solution.py:86
  341.7 2.8 collective-permute-start.10
  344.5 2.8 collective-permute-done.10
  347.3 4.2 %collective-permute-start.11 = (f32[4,1040]{1,0:T(4,128)S(1)}, f32[4,1040]{1,0:T(4,128)S(1)}, u32[]{:S(2)}, u32[]{:S(2)}) collective-permute-start(f32[4,1040]{1,0:T(4,128)S(1)} %dynamic-slice_bitcast_fusion.10), channel_id=1, source_target_pairs={{0,64},{1,65},{2,66},{3,67},{4,68},{5,69},{6,70},{7,71},{8,72},{9,... | collective-permute-start | bytes 49928 | tf_op jit(solution)/shard_map/ppermute | solution.py:86
  351.5 3.6 collective-permute-done.11
  (131 shorter events, 29.0 us)
Async XLA Ops:
  7.2 66.6 %all-gather.9.cloned.1.call-start = ((), (), s32[]{:S(2)}) async-start(), calls=%async_computation.2 | async-start | bytes 4718592 | tf_op jit(solution)/shard_map/all_gather | solution.py:97
  7.9 131.4 %all-gather.5.cloned.1.call-start = ((), (), s32[]{:S(2)}) async-start(), calls=%async_computation | async-start | bytes 4718592 | tf_op jit(solution)/shard_map/all_gather | solution.py:97
  8.6 241.9 %all-gather.11.cloned.1.call-start = ((), (), s32[]{:S(2)}) async-start(), calls=%async_computation.3 | async-start | bytes 12582912 | tf_op jit(solution)/shard_map/all_gather | solution.py:98
  73.8 65.5 %copy-start = (bf16[3,16,16,1024]{3,2,1,0:T(8,128)(2,1)S(1)}, bf16[3,16,16,1024]{3,2,1,0:T(8,128)(2,1)}, u32[]{:S(2)}) copy-start(bf16[3,16,16,1024]{3,2,1,0:T(8,128)(2,1)} %param.8) | copy-start | bytes 4718596
  73.8 72.2 %copy-start.4 = (s32[3,16,16]{2,1,0:T(8,128)S(1)}, s32[3,16,16]{2,1,0:T(8,128)}, u32[]{:S(2)}) copy-start(s32[3,16,16]{2,1,0:T(8,128)} %param.14) | copy-start | bytes 9220
  73.8 176.7 %all-gather.7.cloned.1.call-start = ((), (), s32[]{:S(2)}) async-start(), calls=%async_computation.1 | async-start | bytes 12582912 | tf_op jit(solution)/shard_map/all_gather | solution.py:98
  139.3 8.8 %copy-start.3 = (bf16[7,7,1024]{2,1,0:T(8,128)(2,1)S(1)}, bf16[7,7,1024]{2,1,0:T(8,128)(2,1)}, u32[]{:S(2)}) copy-start(bf16[7,7,1024]{2,1,0:T(8,128)(2,1)} %param.9) | copy-start | bytes 301060
  139.3 8.9 %copy-start.5 = (s32[3,16,16]{2,1,0:T(8,128)S(1)}, s32[3,16,16]{2,1,0:T(8,128)}, u32[]{:S(2)}) copy-start(s32[3,16,16]{2,1,0:T(8,128)} %param.15) | copy-start | bytes 9220
  139.4 10.4 %collective-permute-start = (bf16[3,3,16,1024]{3,2,1,0:T(8,128)(2,1)S(1)}, bf16[3,3,16,1024]{3,2,1,0:T(8,128)(2,1)S(1)}, u32[]{:S(2)}, u32[]{:S(2)}) collective-permute-start(bf16[3,3,16,1024]{3,2,1,0:T(8,128)(2,1)S(1)} %get-tuple-element.10), channel_id=1, source_target_pairs={{0,16},{16,32},{32,48},{48,64},{64,80},{80,96},{96,112},{112,128},... | collective-permute-start | bytes 884744 | tf_op jit(solution)/shard_map/ppermute | solution.py:20
  144.0 9.8 %collective-permute-start.1 = (bf16[3,3,16,1024]{3,2,1,0:T(8,128)(2,1)S(1)}, bf16[3,3,16,1024]{3,2,1,0:T(8,128)(2,1)S(1)}, u32[]{:S(2)}, u32[]{:S(2)}) collective-permute-start(bf16[3,3,16,1024]{3,2,1,0:T(8,128)(2,1)S(1)} %get-tuple-element.11), channel_id=1, source_target_pairs={{16,0},{32,16},{48,32},{64,48},{80,64},{96,80},{112,96},{128,112},... | collective-permute-start | bytes 884744 | tf_op jit(solution)/shard_map/ppermute | solution.py:21
  157.4 9.7 %collective-permute-start.2 = (bf16[3,22,3,1024]{3,1,2,0:T(8,128)(2,1)S(1)}, bf16[3,22,3,1024]{3,1,2,0:T(8,128)(2,1)}, u32[]{:S(2)}, u32[]{:S(2)}) collective-permute-start(bf16[3,22,3,1024]{3,1,2,0:T(8,128)(2,1)S(1)} %get-tuple-element.4), channel_id=1, source_target_pairs={{0,1},{1,2},{2,3},{3,4},{4,5},{5,6},{6,7},{7,8},{8,9},{9,10},{10,1... | collective-permute-start | bytes 1216520 | tf_op jit(solution)/shard_map/ppermute | solution.py:20
  159.4 9.5 %collective-permute-start.3 = (bf16[3,22,3,1024]{3,1,2,0:T(8,128)(2,1)S(1)}, bf16[3,22,3,1024]{3,1,2,0:T(8,128)(2,1)}, u32[]{:S(2)}, u32[]{:S(2)}) collective-permute-start(bf16[3,22,3,1024]{3,1,2,0:T(8,128)(2,1)S(1)} %get-tuple-element.5), channel_id=1, source_target_pairs={{1,0},{2,1},{3,2},{4,3},{5,4},{6,5},{7,6},{8,7},{9,8},{10,9},{11,1... | collective-permute-start | bytes 1216520 | tf_op jit(solution)/shard_map/ppermute | solution.py:21
  170.1 4.1 %copy-start.6 = (f32[8,128]{1,0:T(8,128)S(1)}, f32[8,128]{1,0:T(8,128)}, u32[]{:S(2)}) copy-start(f32[8,128]{1,0:T(8,128)} %get-tuple-element.64) | copy-start | bytes 12292
  239.3 11.2 %copy-start.28 = (bf16[768]{0:T(1024)(128)(2,1)S(1)}, bf16[768]{0:T(1024)(128)(2,1)}, u32[]{:S(2)}) copy-start(bf16[768]{0:T(1024)(128)(2,1)} %convert_element_type.45) | copy-start | bytes 4612
  239.3 11.2 %copy-start.29 = (f32[1024]{0:T(1024)S(1)}, f32[1024]{0:T(1024)}, u32[]{:S(2)}) copy-start(f32[1024]{0:T(1024)} %param.10) | copy-start | bytes 12292
  239.3 11.2 %copy-start.30 = (f32[1024]{0:T(1024)S(1)}, f32[1024]{0:T(1024)}, u32[]{:S(2)}) copy-start(f32[1024]{0:T(1024)} %param.13) | copy-start | bytes 12292
  280.7 7.7 %collective-permute-start.4 = (f32[512,1040]{0,1:T(8,128)}, f32[512,1040]{0,1:T(8,128)S(1)}, u32[]{:S(2)}, u32[]{:S(2)}) collective-permute-start(f32[512,1040]{0,1:T(8,128)} %fusion.65), channel_id=1, source_target_pairs={{0,1},{1,0},{2,3},{3,2},{4,5},{5,4},{6,7},{7,6},{8,9},{9,8},{10,11... | collective-permute-start | bytes 6389768 | tf_op jit(solution)/shard_map/ppermute | solution.py:131
  295.0 15.1 %collective-permute-start.5 = (f32[256,1040]{0,1:T(8,128)S(1)}, f32[256,1040]{0,1:T(8,128)S(1)}, u32[]{:S(2)}, u32[]{:S(2)}) collective-permute-start(f32[256,1040]{0,1:T(8,128)S(1)} %pad_maximum_fusion.5), channel_id=1, source_target_pairs={{0,2},{1,9},{2,0},{3,11},{4,6},{5,13},{6,4},{7,15},{8,10},{9,1},{1... | collective-permute-start | bytes 3194888 | tf_op jit(solution)/shard_map/ppermute | solution.py:86
  311.9 9.4 %collective-permute-start.6 = (f32[128,1040]{0,1:T(8,128)S(1)}, f32[128,1040]{0,1:T(8,128)S(1)}, u32[]{:S(2)}, u32[]{:S(2)}) collective-permute-start(f32[128,1040]{0,1:T(8,128)S(1)} %bitcast.189), channel_id=1, source_target_pairs={{0,8},{1,3},{2,10},{3,1},{4,12},{5,7},{6,14},{7,5},{8,0},{9,11},{1... | collective-permute-start | bytes 1597448 | tf_op jit(solution)/shard_map/ppermute | solution.py:86
  321.6 6.8 %collective-permute-start.7 = (f32[64,1040]{1,0:T(8,128)S(1)}, f32[64,1040]{1,0:T(8,128)S(1)}, u32[]{:S(2)}, u32[]{:S(2)}) collective-permute-start(f32[64,1040]{1,0:T(8,128)S(1)} %pad_maximum_fusion.6), channel_id=1, source_target_pairs={{0,16},{1,5},{2,18},{3,7},{4,20},{5,1},{6,22},{7,3},{8,24},{9,13},... | collective-permute-start | bytes 798728 | tf_op jit(solution)/shard_map/ppermute | solution.py:86
  328.5 6.7 %collective-permute-start.8 = (f32[32,1040]{1,0:T(8,128)S(1)}, f32[32,1040]{1,0:T(8,128)S(1)}, u32[]{:S(2)}, u32[]{:S(2)}) collective-permute-start(f32[32,1040]{1,0:T(8,128)S(1)} %dynamic-slice_bitcast_fusion), channel_id=1, source_target_pairs={{0,4},{1,17},{2,6},{3,19},{4,0},{5,21},{6,2},{7,23},{8,12},{9,25},... | collective-permute-start | bytes 399368 | tf_op jit(solution)/shard_map/ppermute | solution.py:86
  335.3 6.4 %collective-permute-start.9 = (f32[16,1040]{1,0:T(8,128)S(1)}, f32[16,1040]{1,0:T(8,128)S(1)}, u32[]{:S(2)}, u32[]{:S(2)}) collective-permute-start(f32[16,1040]{1,0:T(8,128)S(1)} %pad_maximum_fusion.7), channel_id=1, source_target_pairs={{0,32},{1,129},{2,34},{3,131},{4,36},{5,133},{6,38},{7,135},{8,40}... | collective-permute-start | bytes 199688 | tf_op jit(solution)/shard_map/ppermute | solution.py:86
  341.7 5.5 %collective-permute-start.10 = (f32[8,1040]{1,0:T(8,128)S(1)}, f32[8,1040]{1,0:T(8,128)S(1)}, u32[]{:S(2)}, u32[]{:S(2)}) collective-permute-start(f32[8,1040]{1,0:T(8,128)S(1)} %dynamic-slice_bitcast_fusion.5), channel_id=1, source_target_pairs={{0,128},{1,33},{2,130},{3,35},{4,132},{5,37},{6,134},{7,39},{8,136... | collective-permute-start | bytes 99848 | tf_op jit(solution)/shard_map/ppermute | solution.py:86
  347.3 7.8 %collective-permute-start.11 = (f32[4,1040]{1,0:T(4,128)S(1)}, f32[4,1040]{1,0:T(4,128)S(1)}, u32[]{:S(2)}, u32[]{:S(2)}) collective-permute-start(f32[4,1040]{1,0:T(4,128)S(1)} %dynamic-slice_bitcast_fusion.10), channel_id=1, source_target_pairs={{0,64},{1,65},{2,66},{3,67},{4,68},{5,69},{6,70},{7,71},{8,72},{9,... | collective-permute-start | bytes 49928 | tf_op jit(solution)/shard_map/ppermute | solution.py:86
  (23 other events, 90.2 us)
Sparse Core Ops, SparseCore 0:
  9.7 64.0 all-gather.8
  75.5 63.7 all-gather.4
  141.1 27.0 all-gather.10
  169.8 25.8 all-gather.6

commit v4 on v2

--- a/solution.py
+++ b/solution.py
@@ -104,8 +104,11 @@
             conv = conv + padded[:, i : i + high, j : j + wide] * kernel[i, j]
     count = tiles * high * wide
     normed = apply_norm(conv.reshape(count, *tile), ln_gain.reshape(tile)).reshape(count, width)
-    hidden = expand(normed, lax.all_gather(w_in, "col", axis=1, tiled=True))
-    branch = contract(hidden, lax.all_gather(w_down, "col", axis=1, tiled=True))
+    w_in_all, w_down_all = lax.all_gather(
+        jnp.stack([w_in, w_down]), "col", axis=2, tiled=True
+    )
+    hidden = expand(normed, w_in_all)
+    branch = contract(hidden, w_down_all)
     out = (features.reshape(count, width).astype(jnp.float32) + gamma * branch).astype(jnp.bfloat16)
     keep = valid.reshape(count, 1)
     masked = out * keep.astype(jnp.bfloat16)

time: 256 us -> 246 us (0.961); the launches traced: 251 us -> 246 us
  waiting for transfers between devices: 74.9 us -> 65.2 us
  other arithmetic: 83.7 us -> 91.7 us
  local copies, waits for them, and re-layouts: 25 us -> 22.1 us
    all_gather x2 -> x1, waiting for transfers between devices: 14.8 us -> 0.01 us  [on_device(): lax.all_gather(jnp.stack([w_in, w_down]), 'col', axis=2, tiled=True)]
    ppermute x7, starting transfers between devices: 11.9 us -> 7.28 us  [halving_sum(): part = keep + lax.ppermute(send, axes, pairs)]
    ppermute x7, waiting for transfers between devices: 45.3 us -> 49.5 us  [halving_sum(): part = keep + lax.ppermute(send, axes, pairs)]
    ppermute x1, starting transfers between devices: 0.26 us -> 4.39 us  [on_device(): lax.ppermute(rows_of(1 - core), axes, [(i, i ^ 1) for i in range(size)])]
    convert_element_type x0 -> x1, other arithmetic: none -> 2.96 us  [apply_norm(): return (centered * lax.rsqrt(var + 1e-06) * ln_gain).astype(jnp.bfloat16)]
    ppermute x2, waiting for transfers between devices: 5.05 us -> 7.93 us  [with_halo(): after = lax.ppermute(leading, axis, down)]
  transfers between devices with their start and end apart: 14 -> 13, of which waited for: 12 -> 12; matrix products, arithmetic and copies ran while one was open for 38% -> 41% of each run, Pallas kernels for 0% -> 0%
where the time goes in v4:
time: 246 us
  other arithmetic  91.7 us (37%)
  waiting for transfers between devices  65.2 us (27%)
  matrix products  27.6 us (11%)
  starting transfers between devices  24.2 us (10%)
  local copies, waits for them, and re-layouts  22.1 us (9%)
  between operations  14.9 us (6%)
    reduce_sum x1, other arithmetic, apply_norm(): mean = jnp.mean(rows, axis=(-2, -1), keepdims=True)  64.9 us
    ppermute x7, waiting for transfers between devices, halving_sum(): part = keep + lax.ppermute(send, axes, pairs)  49.5 us
    dot_general x1, matrix products, contract(): lax.dot_general(hidden, piece, (((1,), (1,)), ((), ())), preferred_elemen...  21.1 us
    reduce_sum x1, other arithmetic, apply_norm(): var = jnp.mean(centered * centered, axis=(-2, -1), keepdims=True)  11 us
    ppermute x2, waiting for transfers between devices, with_halo(): after = lax.ppermute(leading, axis, down)  7.93 us
    ppermute x7, starting transfers between devices, halving_sum(): part = keep + lax.ppermute(send, axes, pairs)  7.28 us
    ppermute x2, starting transfers between devices, with_halo(): before = lax.ppermute(last, axis, up)  6.96 us
    dot_general x2, matrix products, rows_of(): lax.dot_general(lhs, rhs, (((0,), (0,)), ((), ())), preferred_element_typ...  6.49 us
  transfers between devices with their start and end apart: 13, of which 12 were waited for; matrix products, arithmetic and copies ran while one was open for 41% of the time, Pallas kernels for 0%

profile of v4, /device:TPU:120, one launch (start us, length us, event | category | flops | bytes accessed | tf_op | source)
XLA Modules:
  0.0 245.8 jit_solution(3611785644545125164)
XLA Ops:
  9.8 5.0 %collective-permute-start = (bf16[3,3,16,1024]{3,2,1,0:T(8,128)(2,1)S(1)}, bf16[3,3,16,1024]{3,2,1,0:T(8,128)(2,1)S(1)}, u32[]{:S(2)}, u32[]{:S(2)}) collective-permute-start(bf16[3,3,16,1024]{3,2,1,0:T(8,128)(2,1)S(1)} %get-tuple-element.10), channel_id=1, source_target_pairs={{0,16},{16,32},{32,48},{48,64},{64,80},{80,96},{96,112},{112,128},... | collective-permute-start | bytes 884744 | tf_op jit(solution)/shard_map/ppermute | solution.py:19
  21.3 5.1 %collective-permute-done.1 = bf16[3,3,16,1024]{3,2,1,0:T(8,128)(2,1)S(1)} collective-permute-done((bf16[3,3,16,1024]{3,2,1,0:T(8,128)(2,1)S(1)}, bf16[3,3,16,1024]{3,2,1,0:T(8,128)(2,1)S(1)}, u32[]{:S(2)}, u32[]{:S(2)}) %collective-permute-start.1) | collective-permute-done | bytes 294944 | tf_op jit(solution)/shard_map/ppermute | solution.py:20
  26.6 3.0 %pad_maximum_fusion.1 = bf16[3,22,16,1024]{3,1,2,0:T(8,128)(2,1)S(1)} fusion(bf16[3,3,16,1024]{3,1,2,0:T(4,128)(2,1)S(1)} %copy.62, bf16[3,16,16,1024]{3,1,2,0:T(8,128)(2,1)} %copy.61, bf16[3,3,16,1024]{3,1,2,0:T(4,128)(2,1)S(1)} %copy.60), kind=kLoop, calls=%fused_computation.108 | loop fusion | flops 6488064 | bytes 4325376 | tf_op jit(solution)/shard_map/concatenate | solution.py:21
  31.6 3.6 %collective-permute-start.3 = (bf16[3,22,3,1024]{3,1,2,0:T(8,128)(2,1)S(1)}, bf16[3,22,3,1024]{3,1,2,0:T(8,128)(2,1)}, u32[]{:S(2)}, u32[]{:S(2)}) collective-permute-start(bf16[3,22,3,1024]{3,1,2,0:T(8,128)(2,1)S(1)} %get-tuple-element.5), channel_id=1, source_target_pairs={{1,0},{2,1},{3,2},{4,3},{5,4},{6,5},{7,6},{8,7},{9,8},{10,9},{11,1... | collective-permute-start | bytes 1216520 | tf_op jit(solution)/shard_map/ppermute | solution.py:20
  36.6 2.8 %reshape.209 = bf16[3,22,16,8,128]{4,3,1,2,0:T(8,128)(2,1)} reshape(bf16[3,22,16,1024]{3,1,2,0:T(8,128)(2,1)S(1)} %pad_maximum_fusion.1) | data formatting | bytes 4325376 | tf_op jit(solution)/shard_map/concatenate | solution.py:21
  39.3 5.9 %collective-permute-done.2 = bf16[3,22,3,1024]{3,1,2,0:T(8,128)(2,1)} collective-permute-done((bf16[3,22,3,1024]{3,1,2,0:T(8,128)(2,1)S(1)}, bf16[3,22,3,1024]{3,1,2,0:T(8,128)(2,1)}, u32[]{:S(2)}, u32[]{:S(2)}) %collective-permute-start.2) | collective-permute-done | bytes 405536 | tf_op jit(solution)/shard_map/ppermute | solution.py:19
  46.5 2.9 %collective-permute-done.3 = bf16[3,22,3,1024]{3,1,2,0:T(8,128)(2,1)} collective-permute-done((bf16[3,22,3,1024]{3,1,2,0:T(8,128)(2,1)S(1)}, bf16[3,22,3,1024]{3,1,2,0:T(8,128)(2,1)}, u32[]{:S(2)}, u32[]{:S(2)}) %collective-permute-start.3) | collective-permute-done | bytes 405536 | tf_op jit(solution)/shard_map/ppermute | solution.py:20
  50.9 4.0 %copy_convert_fusion = f32[3,22,22,8,128]{4,3,2,1,0:T(8,128)} fusion(bf16[3,22,3,8,128]{4,3,1,2,0:T(8,128)(2,1)S(1)} %concatenate.37, bf16[3,22,16,8,128]{4,3,1,2,0:T(8,128)(2,1)} %reshape.209, bf16[3,22,3,8,128]{4,3,1,2,0:T(8,128)(2,1)S(1)} %concatenate.35), kind=kLoop, calls=%fused_computation.107 | loop fusion | flops 4460544 | bytes 8921088 | tf_op jit(solution)/shard_map/convert_element_type | solution.py:98
  55.1 64.9 %fusion.67 = (f32[3,16,16]{2,1,0:T(8,128)S(1)}, f32[3,16,16,8,128]{4,3,2,1,0:T(8,128)S(1)}) fusion(f32[8,128]{1,0:T(8,128)S(1)} %get-tuple-element.19, f32[3,22,22,8,128]{4,3,2,1,0:T(8,128)} %copy_convert_fusion, f32[8,128]{1,0:T(8,128)S(1)} %get-tuple-element.20, f32[8,128]{1,0:T(8,128)S(1)} %get-tuple-element.21, f32[8,128]{1,0:T(8,128)S(1)} %get-tuple-element.22, ...), kind=kLoop, calls=%fused_computation.208 | loop fusion | flops 77069568 | bytes 157490176 | tf_op jit(solution)/shard_map/reduce_sum | solution.py:26
  120.1 11.0 %multiply_reduce_fusion = f32[3,16,16]{2,1,0:T(8,128)S(1)} fusion(f32[3,16,16,8,128]{4,3,2,1,0:T(8,128)S(1)} %get-tuple-element.3, f32[3,16,16]{2,1,0:T(8,128)S(1)} %broadcast_multiply_fusion.1), kind=kLoop, calls=%fused_computation.105 | loop fusion | flops 2358528 | bytes 3151872 | tf_op jit(solution)/shard_map/reduce_sum | solution.py:28
  131.1 3.0 %multiply_convert_fusion.1 = bf16[3,16,16,8,128]{4,3,2,1,0:T(8,128)(2,1)} fusion(f32[3,16,16,8,128]{4,3,2,1,0:T(8,128)S(1)} %get-tuple-element.3, f32[8,128]{1,0:T(8,128)S(1)} %bitcast.200, f32[3,16,16]{2,1,0:T(8,128)S(1)} %add_rsqrt_fusion, f32[3,16,16]{2,1,0:T(8,128)S(1)} %broadcast_multiply_fusion.1), kind=kLoop, calls=%fused_computation.104 | loop fusion | flops 3145728 | bytes 4728832 | tf_op jit(solution)/shard_map/convert_element_type | solution.py:29
  134.1 21.1 %broadcast_multiply_fusion = (bf16[768,1024]{1,0:T(8,128)(2,1)S(1)}, bf16[768,1024]{1,0:T(8,128)(2,1)}) fusion(bf16[768]{0:T(1024)(128)(2,1)S(1)} %copy-done.29, bf16[2,1024,4096]{2,1,0:T(8,128)(2,1)} %all-gather.2.cloned.1.call-done, bf16[96,8,8,128]{3,2,1,0:T(8,128)(2,1)} %bitcast.193, f32[1024]{0:T(1024)S(1)} %copy-done.30, bf16[768,1024]{1,0:T(8,128)(2,1)} %bitcast.187), kind=kOutput, calls=%fused_computation.119 | convolution fusion | flops 12906921984 | bytes 23074304 | tf_op jit(solution)/shard_map/dot_general | solution.py:38
  158.7 3.8 %fusion.55 = f32[512,1040]{0,1:T(8,128)} fusion(bf16[768,16]{1,0:T(8,128)(2,1)S(1)} %copy-done.2, bf16[768,1024]{1,0:T(8,128)(2,1)} %get-tuple-element.72, bf16[768,1024]{0,1:T(8,128)(2,1)S(1)} %reshape.186, s32[]{:T(128)S(6)} %select_n.201), kind=kOutput, calls=%fused_computation.112 | convolution fusion | flops 821084160 | bytes 4685828 | tf_op jit(solution)/shard_map/dot_general | solution.py:123
  162.5 4.4 %collective-permute-start.4 = (f32[512,1040]{0,1:T(8,128)}, f32[512,1040]{0,1:T(8,128)S(1)}, u32[]{:S(2)}, u32[]{:S(2)}) collective-permute-start(f32[512,1040]{0,1:T(8,128)} %fusion.55), channel_id=1, source_target_pairs={{0,1},{1,0},{2,3},{3,2},{4,5},{5,4},{6,7},{7,6},{8,9},{9,8},{10,11... | collective-permute-start | bytes 6389768 | tf_op jit(solution)/shard_map/ppermute | solution.py:128
  166.9 2.7 %fusion.56 = f32[512,1040]{0,1:T(8,128)S(1)} fusion(bf16[768,16]{1,0:T(8,128)(2,1)S(1)} %copy-done.2, bf16[768,1024]{1,0:T(8,128)(2,1)} %get-tuple-element.72, bf16[768,1024]{0,1:T(8,128)(2,1)} %copy-done.1, s32[]{:T(128)S(6)} %select_n.200), kind=kOutput, calls=%fused_computation.113 | convolution fusion | flops 821084160 | bytes 4513796 | tf_op jit(solution)/shard_map/dot_general | solution.py:123
  177.8 14.9 %collective-permute-done.5 = f32[256,1040]{0,1:T(8,128)S(1)} collective-permute-done((f32[256,1040]{0,1:T(8,128)S(1)}, f32[256,1040]{0,1:T(8,128)S(1)}, u32[]{:S(2)}, u32[]{:S(2)}) %collective-permute-start.5) | collective-permute-done | bytes 1064992 | tf_op jit(solution)/shard_map/ppermute | solution.py:85
  195.6 8.3 %collective-permute-done.6 = f32[128,1040]{0,1:T(8,128)S(1)} collective-permute-done((f32[128,1040]{0,1:T(8,128)S(1)}, f32[128,1040]{0,1:T(8,128)S(1)}, u32[]{:S(2)}, u32[]{:S(2)}) %collective-permute-start.6) | collective-permute-done | bytes 532512 | tf_op jit(solution)/shard_map/ppermute | solution.py:85
  204.4 6.7 %collective-permute-done.7 = f32[64,1040]{1,0:T(8,128)S(1)} collective-permute-done((f32[64,1040]{1,0:T(8,128)S(1)}, f32[64,1040]{1,0:T(8,128)S(1)}, u32[]{:S(2)}, u32[]{:S(2)}) %collective-permute-start.7) | collective-permute-done | bytes 266272 | tf_op jit(solution)/shard_map/ppermute | solution.py:85
  211.3 6.6 %collective-permute-done.8 = f32[32,1040]{1,0:T(8,128)S(1)} collective-permute-done((f32[32,1040]{1,0:T(8,128)S(1)}, f32[32,1040]{1,0:T(8,128)S(1)}, u32[]{:S(2)}, u32[]{:S(2)}) %collective-permute-start.8) | collective-permute-done | bytes 133152 | tf_op jit(solution)/shard_map/ppermute | solution.py:85
  218.1 6.2 %collective-permute-done.9 = f32[16,1040]{1,0:T(8,128)S(1)} collective-permute-done((f32[16,1040]{1,0:T(8,128)S(1)}, f32[16,1040]{1,0:T(8,128)S(1)}, u32[]{:S(2)}, u32[]{:S(2)}) %collective-permute-start.9) | collective-permute-done | bytes 66592 | tf_op jit(solution)/shard_map/ppermute | solution.py:85
  224.4 2.8 %collective-permute-start.10 = (f32[8,1040]{1,0:T(8,128)S(1)}, f32[8,1040]{1,0:T(8,128)S(1)}, u32[]{:S(2)}, u32[]{:S(2)}) collective-permute-start(f32[8,1040]{1,0:T(8,128)S(1)} %dynamic-slice_bitcast_fusion.5), channel_id=1, source_target_pairs={{0,128},{1,33},{2,130},{3,35},{4,132},{5,37},{6,134},{7,39},{8,136... | collective-permute-start | bytes 99848 | tf_op jit(solution)/shard_map/ppermute | solution.py:85
  227.2 2.7 %collective-permute-done.10 = f32[8,1040]{1,0:T(8,128)S(1)} collective-permute-done((f32[8,1040]{1,0:T(8,128)S(1)}, f32[8,1040]{1,0:T(8,128)S(1)}, u32[]{:S(2)}, u32[]{:S(2)}) %collective-permute-start.10) | collective-permute-done | bytes 33312 | tf_op jit(solution)/shard_map/ppermute | solution.py:85
  230.0 3.8 %collective-permute-start.11 = (f32[4,1040]{1,0:T(4,128)S(1)}, f32[4,1040]{1,0:T(4,128)S(1)}, u32[]{:S(2)}, u32[]{:S(2)}) collective-permute-start(f32[4,1040]{1,0:T(4,128)S(1)} %dynamic-slice_bitcast_fusion.10), channel_id=1, source_target_pairs={{0,64},{1,65},{2,66},{3,67},{4,68},{5,69},{6,70},{7,71},{8,72},{9,... | collective-permute-start | bytes 49928 | tf_op jit(solution)/shard_map/ppermute | solution.py:85
  233.8 4.0 %collective-permute-done.11 = f32[4,1040]{1,0:T(4,128)S(1)} collective-permute-done((f32[4,1040]{1,0:T(4,128)S(1)}, f32[4,1040]{1,0:T(4,128)S(1)}, u32[]{:S(2)}, u32[]{:S(2)}) %collective-permute-start.11) | collective-permute-done | bytes 16672 | tf_op jit(solution)/shard_map/ppermute | solution.py:85
  (122 shorter events, 31.7 us)
Async XLA Ops:
  7.2 9.6 %copy-start.4 = (s32[3,16,16]{2,1,0:T(8,128)S(1)}, s32[3,16,16]{2,1,0:T(8,128)}, u32[]{:S(2)}) copy-start(s32[3,16,16]{2,1,0:T(8,128)} %param.14) | copy-start | bytes 9220
  7.2 126.9 %all-gather.2.cloned.1.call-start = ((), (), s32[]{:S(2)}) async-start(), calls=%async_computation | async-start | bytes 17825792 | tf_op jit(solution)/shard_map/all_gather | solution.py:107
  9.7 9.2 %copy-start.3 = (bf16[7,7,1024]{2,1,0:T(8,128)(2,1)S(1)}, bf16[7,7,1024]{2,1,0:T(8,128)(2,1)}, u32[]{:S(2)}) copy-start(bf16[7,7,1024]{2,1,0:T(8,128)(2,1)} %param.9) | copy-start | bytes 301060
  9.7 9.3 %copy-start.5 = (s32[3,16,16]{2,1,0:T(8,128)S(1)}, s32[3,16,16]{2,1,0:T(8,128)}, u32[]{:S(2)}) copy-start(s32[3,16,16]{2,1,0:T(8,128)} %param.15) | copy-start | bytes 9220
  9.8 11.3 %collective-permute-start = (bf16[3,3,16,1024]{3,2,1,0:T(8,128)(2,1)S(1)}, bf16[3,3,16,1024]{3,2,1,0:T(8,128)(2,1)S(1)}, u32[]{:S(2)}, u32[]{:S(2)}) collective-permute-start(bf16[3,3,16,1024]{3,2,1,0:T(8,128)(2,1)S(1)} %get-tuple-element.10), channel_id=1, source_target_pairs={{0,16},{16,32},{32,48},{48,64},{64,80},{80,96},{96,112},{112,128},... | collective-permute-start | bytes 884744 | tf_op jit(solution)/shard_map/ppermute | solution.py:19
  14.8 11.6 %collective-permute-start.1 = (bf16[3,3,16,1024]{3,2,1,0:T(8,128)(2,1)S(1)}, bf16[3,3,16,1024]{3,2,1,0:T(8,128)(2,1)S(1)}, u32[]{:S(2)}, u32[]{:S(2)}) collective-permute-start(bf16[3,3,16,1024]{3,2,1,0:T(8,128)(2,1)S(1)} %get-tuple-element.11), channel_id=1, source_target_pairs={{16,0},{32,16},{48,32},{64,48},{80,64},{96,80},{112,96},{128,112},... | collective-permute-start | bytes 884744 | tf_op jit(solution)/shard_map/ppermute | solution.py:20
  29.7 15.5 %collective-permute-start.2 = (bf16[3,22,3,1024]{3,1,2,0:T(8,128)(2,1)S(1)}, bf16[3,22,3,1024]{3,1,2,0:T(8,128)(2,1)}, u32[]{:S(2)}, u32[]{:S(2)}) collective-permute-start(bf16[3,22,3,1024]{3,1,2,0:T(8,128)(2,1)S(1)} %get-tuple-element.4), channel_id=1, source_target_pairs={{0,1},{1,2},{2,3},{3,4},{4,5},{5,6},{6,7},{7,8},{8,9},{9,10},{10,1... | collective-permute-start | bytes 1216520 | tf_op jit(solution)/shard_map/ppermute | solution.py:19
  31.6 17.7 %collective-permute-start.3 = (bf16[3,22,3,1024]{3,1,2,0:T(8,128)(2,1)S(1)}, bf16[3,22,3,1024]{3,1,2,0:T(8,128)(2,1)}, u32[]{:S(2)}, u32[]{:S(2)}) collective-permute-start(bf16[3,22,3,1024]{3,1,2,0:T(8,128)(2,1)S(1)} %get-tuple-element.5), channel_id=1, source_target_pairs={{1,0},{2,1},{3,2},{4,3},{5,4},{6,5},{7,6},{8,7},{9,8},{10,9},{11,1... | collective-permute-start | bytes 1216520 | tf_op jit(solution)/shard_map/ppermute | solution.py:20
  50.7 4.3 %copy-start.6 = (f32[8,128]{1,0:T(8,128)S(1)}, f32[8,128]{1,0:T(8,128)}, u32[]{:S(2)}) copy-start(f32[8,128]{1,0:T(8,128)} %get-tuple-element.64) | copy-start | bytes 12292
  50.7 4.2 %copy-start.7 = (f32[8,128]{1,0:T(8,128)S(1)}, f32[8,128]{1,0:T(8,128)}, u32[]{:S(2)}) copy-start(f32[8,128]{1,0:T(8,128)} %get-tuple-element.65) | copy-start | bytes 12292
  50.7 4.2 %copy-start.8 = (f32[8,128]{1,0:T(8,128)S(1)}, f32[8,128]{1,0:T(8,128)}, u32[]{:S(2)}) copy-start(f32[8,128]{1,0:T(8,128)} %get-tuple-element.66) | copy-start | bytes 12292
  50.7 4.2 %copy-start.9 = (f32[8,128]{1,0:T(8,128)S(1)}, f32[8,128]{1,0:T(8,128)}, u32[]{:S(2)}) copy-start(f32[8,128]{1,0:T(8,128)} %get-tuple-element.37) | copy-start | bytes 12292
  50.7 4.2 %copy-start.10 = (f32[8,128]{1,0:T(8,128)S(1)}, f32[8,128]{1,0:T(8,128)}, u32[]{:S(2)}) copy-start(f32[8,128]{1,0:T(8,128)} %get-tuple-element.38) | copy-start | bytes 12292
  50.7 4.2 %copy-start.11 = (f32[8,128]{1,0:T(8,128)S(1)}, f32[8,128]{1,0:T(8,128)}, u32[]{:S(2)}) copy-start(f32[8,128]{1,0:T(8,128)} %get-tuple-element.39) | copy-start | bytes 12292
  50.7 4.2 %copy-start.12 = (f32[8,128]{1,0:T(8,128)S(1)}, f32[8,128]{1,0:T(8,128)}, u32[]{:S(2)}) copy-start(f32[8,128]{1,0:T(8,128)} %get-tuple-element.40) | copy-start | bytes 12292
  120.0 11.1 %copy-start.28 = (f32[1024]{0:T(1024)S(1)}, f32[1024]{0:T(1024)}, u32[]{:S(2)}) copy-start(f32[1024]{0:T(1024)} %param.10) | copy-start | bytes 12292
  162.5 8.4 %collective-permute-start.4 = (f32[512,1040]{0,1:T(8,128)}, f32[512,1040]{0,1:T(8,128)S(1)}, u32[]{:S(2)}, u32[]{:S(2)}) collective-permute-start(f32[512,1040]{0,1:T(8,128)} %fusion.55), channel_id=1, source_target_pairs={{0,1},{1,0},{2,3},{3,2},{4,5},{5,4},{6,7},{7,6},{8,9},{9,8},{10,11... | collective-permute-start | bytes 6389768 | tf_op jit(solution)/shard_map/ppermute | solution.py:128
  177.4 15.3 %collective-permute-start.5 = (f32[256,1040]{0,1:T(8,128)S(1)}, f32[256,1040]{0,1:T(8,128)S(1)}, u32[]{:S(2)}, u32[]{:S(2)}) collective-permute-start(f32[256,1040]{0,1:T(8,128)S(1)} %pad_maximum_fusion.5), channel_id=1, source_target_pairs={{0,2},{1,9},{2,0},{3,11},{4,6},{5,13},{6,4},{7,15},{8,10},{9,1},{1... | collective-permute-start | bytes 3194888 | tf_op jit(solution)/shard_map/ppermute | solution.py:85
  194.6 9.4 %collective-permute-start.6 = (f32[128,1040]{0,1:T(8,128)S(1)}, f32[128,1040]{0,1:T(8,128)S(1)}, u32[]{:S(2)}, u32[]{:S(2)}) collective-permute-start(f32[128,1040]{0,1:T(8,128)S(1)} %bitcast.197), channel_id=1, source_target_pairs={{0,8},{1,3},{2,10},{3,1},{4,12},{5,7},{6,14},{7,5},{8,0},{9,11},{1... | collective-permute-start | bytes 1597448 | tf_op jit(solution)/shard_map/ppermute | solution.py:85
  204.3 6.8 %collective-permute-start.7 = (f32[64,1040]{1,0:T(8,128)S(1)}, f32[64,1040]{1,0:T(8,128)S(1)}, u32[]{:S(2)}, u32[]{:S(2)}) collective-permute-start(f32[64,1040]{1,0:T(8,128)S(1)} %pad_maximum_fusion.7), channel_id=1, source_target_pairs={{0,16},{1,5},{2,18},{3,7},{4,20},{5,1},{6,22},{7,3},{8,24},{9,13},... | collective-permute-start | bytes 798728 | tf_op jit(solution)/shard_map/ppermute | solution.py:85
  211.2 6.7 %collective-permute-start.8 = (f32[32,1040]{1,0:T(8,128)S(1)}, f32[32,1040]{1,0:T(8,128)S(1)}, u32[]{:S(2)}, u32[]{:S(2)}) collective-permute-start(f32[32,1040]{1,0:T(8,128)S(1)} %dynamic-slice_bitcast_fusion), channel_id=1, source_target_pairs={{0,4},{1,17},{2,6},{3,19},{4,0},{5,21},{6,2},{7,23},{8,12},{9,25},... | collective-permute-start | bytes 399368 | tf_op jit(solution)/shard_map/ppermute | solution.py:85
  218.0 6.4 %collective-permute-start.9 = (f32[16,1040]{1,0:T(8,128)S(1)}, f32[16,1040]{1,0:T(8,128)S(1)}, u32[]{:S(2)}, u32[]{:S(2)}) collective-permute-start(f32[16,1040]{1,0:T(8,128)S(1)} %pad_maximum_fusion.8), channel_id=1, source_target_pairs={{0,32},{1,129},{2,34},{3,131},{4,36},{5,133},{6,38},{7,135},{8,40}... | collective-permute-start | bytes 199688 | tf_op jit(solution)/shard_map/ppermute | solution.py:85
  224.4 5.5 %collective-permute-start.10 = (f32[8,1040]{1,0:T(8,128)S(1)}, f32[8,1040]{1,0:T(8,128)S(1)}, u32[]{:S(2)}, u32[]{:S(2)}) collective-permute-start(f32[8,1040]{1,0:T(8,128)S(1)} %dynamic-slice_bitcast_fusion.5), channel_id=1, source_target_pairs={{0,128},{1,33},{2,130},{3,35},{4,132},{5,37},{6,134},{7,39},{8,136... | collective-permute-start | bytes 99848 | tf_op jit(solution)/shard_map/ppermute | solution.py:85
  230.0 7.8 %collective-permute-start.11 = (f32[4,1040]{1,0:T(4,128)S(1)}, f32[4,1040]{1,0:T(4,128)S(1)}, u32[]{:S(2)}, u32[]{:S(2)}) collective-permute-start(f32[4,1040]{1,0:T(4,128)S(1)} %dynamic-slice_bitcast_fusion.10), channel_id=1, source_target_pairs={{0,64},{1,65},{2,66},{3,67},{4,68},{5,69},{6,70},{7,71},{8,72},{9,... | collective-permute-start | bytes 49928 | tf_op jit(solution)/shard_map/ppermute | solution.py:85
  (20 other events, 75.5 us)
Sparse Core Ops, SparseCore 0:
  9.8 105.7 all-gather.1

commit v5 on v4

--- a/solution.py
+++ b/solution.py
@@ -51,7 +51,7 @@
     return split.transpose(order).reshape(count, width)
 
 
-def halving_sum(part, axes, begin):
+def halving_sum(addends, axes, begin):
     size = 1
     for axis in axes:
         size *= lax.axis_size(axis)
@@ -60,30 +60,32 @@
     for step in range(begin, len(HALVING_BITS[0])):
         bit = jnp.where(core, HALVING_BITS[1][step], HALVING_BITS[0][step])
         mine = (me >> bit) & 1
-        if HALVING_BITS[0][step] != HALVING_BITS[1][step] and (
-            HALVING_BITS[0][step] == HALVING_BITS[1][step + 1]
-        ):
-            quarters = part.reshape((2, 2, part.shape[0] // 4) + part.shape[1:])
-            rest = quarters.shape[2:]
+        keep, send = 0, 0
+        for part in addends:
+            if HALVING_BITS[0][step] != HALVING_BITS[1][step] and (
+                HALVING_BITS[0][step] == HALVING_BITS[1][step + 1]
+            ):
+                quarters = part.reshape((2, 2, part.shape[0] // 4) + part.shape[1:])
+                rest = quarters.shape[2:]
 
-            def half(value):
-                pieces = []
-                for other in (0, 1):
-                    first = jnp.where(core, other, value)
-                    second = jnp.where(core, value, other)
-                    start = (first, second) + (0,) * len(rest)
-                    piece = lax.dynamic_slice(quarters, start, (1, 1) + rest)
-                    pieces.append(piece.reshape(rest))
-                return jnp.concatenate(pieces, axis=0)
+                def half(value):
+                    pieces = []
+                    for other in (0, 1):
+                        first = jnp.where(core, other, value)
+                        second = jnp.where(core, value, other)
+                        start = (first, second) + (0,) * len(rest)
+                        piece = lax.dynamic_slice(quarters, start, (1, 1) + rest)
+                        pieces.append(piece.reshape(rest))
+                    return jnp.concatenate(pieces, axis=0)
 
-            keep, send = half(mine), half(1 - mine)
-        else:
-            halves = part.reshape((2, part.shape[0] // 2) + part.shape[1:])
-            keep = lax.dynamic_index_in_dim(halves, mine, 0, keepdims=False)
-            send = lax.dynamic_index_in_dim(halves, 1 - mine, 0, keepdims=False)
+                keep, send = keep + half(mine), send + half(1 - mine)
+            else:
+                halves = part.reshape((2, part.shape[0] // 2) + part.shape[1:])
+                keep = keep + lax.dynamic_index_in_dim(halves, mine, 0, keepdims=False)
+                send = send + lax.dynamic_index_in_dim(halves, 1 - mine, 0, keepdims=False)
         pairs = [(i, i ^ (1 << HALVING_BITS[i & 1][step])) for i in range(size)]
-        part = keep + lax.ppermute(send, axes, pairs)
-    return part
+        addends = [keep + lax.ppermute(send, axes, pairs)]
+    return addends[0]
 
 
 def targets_of(labels, count):
@@ -127,7 +129,7 @@
     size = lax.axis_size("row") * lax.axis_size("col")
     sent = lax.ppermute(rows_of(1 - core), axes, [(i, i ^ 1) for i in range(size)])
     kept = lax.optimization_barrier(rows_of(core))
-    summed = halving_sum(kept + sent, axes, 1)
+    summed = halving_sum([kept, sent], axes, 1)
     gram_sum, cross_sum = summed[:, :width], summed[:, width:]
     total = float(tiles * high * lax.axis_size("row") * wide * lax.axis_size("col"))
     return (gram_sum / total, cross_sum / jnp.sqrt(jnp.float32(total)))

time: 246 us -> 248 us (level)
  local copies, waits for them, and re-layouts: 22.1 us -> 28.8 us
  other arithmetic: 91.7 us -> 88.8 us
    dynamic_slice x1, local copies, waits for them, and re-layouts: 1.9 us -> 6.12 us  [half(): piece = lax.dynamic_slice(quarters, start, (1, 1) + rest)]
    reshape x1 -> x2, local copies, waits for them, and re-layouts: 2.69 us -> 6.26 us  [halving_sum(): quarters = part.reshape((2, 2, part.shape[0] // 4) + part.shape[1:])]
    reduce_sum x1, other arithmetic: 64.9 us -> 62.4 us  [apply_norm(): mean = jnp.mean(rows, axis=(-2, -1), keepdims=True)]
  transfers between devices with their start and end apart: 13 -> 13, of which waited for: 12 -> 11; matrix products, arithmetic and copies ran while one was open for 41% -> 40% of each run, Pallas kernels for 0% -> 0%
where the time goes in v5:
time: 248 us
  other arithmetic  88.8 us (36%)
  waiting for transfers between devices  64 us (26%)
  local copies, waits for them, and re-layouts  28.8 us (12%)
  matrix products  27.5 us (11%)
  starting transfers between devices  24 us (10%)
  between operations  14.9 us (6%)
    reduce_sum x1, other arithmetic, apply_norm(): mean = jnp.mean(rows, axis=(-2, -1), keepdims=True)  62.4 us
    ppermute x7, waiting for transfers between devices, halving_sum(): addends = [keep + lax.ppermute(send, axes, pairs)]  49.7 us
    dot_general x1, matrix products, contract(): lax.dot_general(hidden, piece, (((1,), (1,)), ((), ())), preferred_elemen...  21.1 us
    reduce_sum x1, other arithmetic, apply_norm(): var = jnp.mean(centered * centered, axis=(-2, -1), keepdims=True)  11 us
    ppermute x2, waiting for transfers between devices, with_halo(): after = lax.ppermute(leading, axis, down)  7.93 us
    ppermute x7, starting transfers between devices, halving_sum(): addends = [keep + lax.ppermute(send, axes, pairs)]  7.06 us
    ppermute x2, starting transfers between devices, with_halo(): before = lax.ppermute(last, axis, up)  6.96 us
    ppermute x2, waiting for transfers between devices, with_halo(): before = lax.ppermute(last, axis, up)  6.42 us
  transfers between devices with their start and end apart: 13, of which 11 were waited for; matrix products, arithmetic and copies ran while one was open for 40% of the time, Pallas kernels for 0%

profile of v5, /device:TPU:120, one launch (start us, length us, event | category | flops | bytes accessed | tf_op | source)
XLA Modules:
  0.0 247.9 jit_solution(3314003724736680664)
XLA Ops:
  9.7 5.0 %collective-permute-start = (bf16[3,3,16,1024]{3,2,1,0:T(8,128)(2,1)S(1)}, bf16[3,3,16,1024]{3,2,1,0:T(8,128)(2,1)S(1)}, u32[]{:S(2)}, u32[]{:S(2)}) collective-permute-start(bf16[3,3,16,1024]{3,2,1,0:T(8,128)(2,1)S(1)} %get-tuple-element.14), channel_id=1, source_target_pairs={{0,16},{16,32},{32,48},{48,64},{64,80},{80,96},{96,112},{112,128},... | collective-permute-start | bytes 884744 | tf_op jit(solution)/shard_map/ppermute | solution.py:19
  21.3 5.1 %collective-permute-done.1 = bf16[3,3,16,1024]{3,2,1,0:T(8,128)(2,1)S(1)} collective-permute-done((bf16[3,3,16,1024]{3,2,1,0:T(8,128)(2,1)S(1)}, bf16[3,3,16,1024]{3,2,1,0:T(8,128)(2,1)S(1)}, u32[]{:S(2)}, u32[]{:S(2)}) %collective-permute-start.1) | collective-permute-done | bytes 294944 | tf_op jit(solution)/shard_map/ppermute | solution.py:20
  26.6 3.0 %pad_maximum_fusion.1 = bf16[3,22,16,1024]{3,1,2,0:T(8,128)(2,1)S(1)} fusion(bf16[3,3,16,1024]{3,1,2,0:T(4,128)(2,1)S(1)} %copy.63, bf16[3,16,16,1024]{3,1,2,0:T(8,128)(2,1)} %copy.62, bf16[3,3,16,1024]{3,1,2,0:T(4,128)(2,1)S(1)} %copy.61), kind=kLoop, calls=%fused_computation.108 | loop fusion | flops 6488064 | bytes 4325376 | tf_op jit(solution)/shard_map/concatenate | solution.py:21
  31.6 3.6 %collective-permute-start.3 = (bf16[3,22,3,1024]{3,1,2,0:T(8,128)(2,1)S(1)}, bf16[3,22,3,1024]{3,1,2,0:T(8,128)(2,1)}, u32[]{:S(2)}, u32[]{:S(2)}) collective-permute-start(bf16[3,22,3,1024]{3,1,2,0:T(8,128)(2,1)S(1)} %get-tuple-element.5), channel_id=1, source_target_pairs={{1,0},{2,1},{3,2},{4,3},{5,4},{6,5},{7,6},{8,7},{9,8},{10,9},{11,1... | collective-permute-start | bytes 1216520 | tf_op jit(solution)/shard_map/ppermute | solution.py:20
  36.5 2.8 %reshape.229 = bf16[3,22,16,8,128]{4,3,1,2,0:T(8,128)(2,1)} reshape(bf16[3,22,16,1024]{3,1,2,0:T(8,128)(2,1)S(1)} %pad_maximum_fusion.1) | data formatting | bytes 4325376 | tf_op jit(solution)/shard_map/concatenate | solution.py:21
  39.3 5.9 %collective-permute-done.2 = bf16[3,22,3,1024]{3,1,2,0:T(8,128)(2,1)} collective-permute-done((bf16[3,22,3,1024]{3,1,2,0:T(8,128)(2,1)S(1)}, bf16[3,22,3,1024]{3,1,2,0:T(8,128)(2,1)}, u32[]{:S(2)}, u32[]{:S(2)}) %collective-permute-start.2) | collective-permute-done | bytes 405536 | tf_op jit(solution)/shard_map/ppermute | solution.py:19
  46.5 2.9 %collective-permute-done.3 = bf16[3,22,3,1024]{3,1,2,0:T(8,128)(2,1)} collective-permute-done((bf16[3,22,3,1024]{3,1,2,0:T(8,128)(2,1)S(1)}, bf16[3,22,3,1024]{3,1,2,0:T(8,128)(2,1)}, u32[]{:S(2)}, u32[]{:S(2)}) %collective-permute-start.3) | collective-permute-done | bytes 405536 | tf_op jit(solution)/shard_map/ppermute | solution.py:20
  50.9 4.0 %copy_convert_fusion = f32[3,22,22,8,128]{4,3,2,1,0:T(8,128)} fusion(bf16[3,22,3,8,128]{4,3,1,2,0:T(8,128)(2,1)S(1)} %concatenate.43, bf16[3,22,16,8,128]{4,3,1,2,0:T(8,128)(2,1)} %reshape.229, bf16[3,22,3,8,128]{4,3,1,2,0:T(8,128)(2,1)S(1)} %concatenate.41), kind=kLoop, calls=%fused_computation.107 | loop fusion | flops 4460544 | bytes 8921088 | tf_op jit(solution)/shard_map/convert_element_type | solution.py:100
  55.1 62.4 %fusion.68 = (f32[3,16,16]{2,1,0:T(8,128)S(1)}, f32[3,16,16,8,128]{4,3,2,1,0:T(8,128)S(1)}) fusion(f32[8,128]{1,0:T(8,128)S(1)} %get-tuple-element.23, f32[3,22,22,8,128]{4,3,2,1,0:T(8,128)} %copy_convert_fusion, f32[8,128]{1,0:T(8,128)S(1)} %get-tuple-element.24, f32[8,128]{1,0:T(8,128)S(1)} %get-tuple-element.25, f32[8,128]{1,0:T(8,128)S(1)} %get-tuple-element.26, ...), kind=kLoop, calls=%fused_computation.213 | loop fusion | flops 77069568 | bytes 157490176 | tf_op jit(solution)/shard_map/reduce_sum | solution.py:26
  117.6 11.0 %multiply_reduce_fusion = f32[3,16,16]{2,1,0:T(8,128)S(1)} fusion(f32[3,16,16,8,128]{4,3,2,1,0:T(8,128)S(1)} %get-tuple-element.3, f32[3,16,16]{2,1,0:T(8,128)S(1)} %broadcast_multiply_fusion.1), kind=kLoop, calls=%fused_computation.105 | loop fusion | flops 2358528 | bytes 3151872 | tf_op jit(solution)/shard_map/reduce_sum | solution.py:28
  128.6 3.0 %multiply_convert_fusion.1 = bf16[3,16,16,8,128]{4,3,2,1,0:T(8,128)(2,1)} fusion(f32[3,16,16,8,128]{4,3,2,1,0:T(8,128)S(1)} %get-tuple-element.3, f32[8,128]{1,0:T(8,128)S(1)} %bitcast.210, f32[3,16,16]{2,1,0:T(8,128)S(1)} %add_rsqrt_fusion, f32[3,16,16]{2,1,0:T(8,128)S(1)} %broadcast_multiply_fusion.1), kind=kLoop, calls=%fused_computation.104 | loop fusion | flops 3145728 | bytes 4728832 | tf_op jit(solution)/shard_map/convert_element_type | solution.py:29
  131.6 21.1 %broadcast_multiply_fusion = (bf16[768,1024]{1,0:T(8,128)(2,1)S(1)}, bf16[768,1024]{1,0:T(8,128)(2,1)}) fusion(bf16[768]{0:T(1024)(128)(2,1)S(1)} %copy-done.30, bf16[2,1024,4096]{2,1,0:T(8,128)(2,1)} %all-gather.2.cloned.1.call-done, bf16[96,8,8,128]{3,2,1,0:T(8,128)(2,1)} %bitcast.203, f32[1024]{0:T(1024)S(1)} %copy-done.31, bf16[768,1024]{1,0:T(8,128)(2,1)} %bitcast.193), kind=kOutput, calls=%fused_computation.120 | convolution fusion | flops 12906921984 | bytes 23074304 | tf_op jit(solution)/shard_map/dot_general | solution.py:38
  155.0 3.9 %fusion.55 = f32[512,1040]{0,1:T(8,128)} fusion(bf16[768,16]{1,0:T(8,128)(2,1)S(1)} %copy-done.3, bf16[768,1024]{1,0:T(8,128)(2,1)} %get-tuple-element.76, bf16[768,1024]{0,1:T(8,128)(2,1)S(1)} %reshape.201, s32[]{:T(128)S(6)} %select_n.226), kind=kOutput, calls=%fused_computation.112 | convolution fusion | flops 821084160 | bytes 4685828 | tf_op jit(solution)/shard_map/dot_general | solution.py:125
  159.0 4.4 %collective-permute-start.4 = (f32[512,1040]{0,1:T(8,128)}, f32[512,1040]{0,1:T(8,128)}, u32[]{:S(2)}, u32[]{:S(2)}) collective-permute-start(f32[512,1040]{0,1:T(8,128)} %fusion.55), channel_id=1, source_target_pairs={{0,1},{1,0},{2,3},{3,2},{4,5},{5,4},{6,7},{7,6},{8,9},{9,8},{10,11... | collective-permute-start | bytes 6389768 | tf_op jit(solution)/shard_map/ppermute | solution.py:130
  168.5 3.6 %reshape.205 = f32[2,2,128,1040]{2,1,0,3:T(2,128)} reshape(f32[512,1040]{0,1:T(8,128)} %collective-permute-done.4) | data formatting | bytes 4259840 | tf_op jit(solution)/shard_map/reshape | solution.py:68
  172.1 6.1 %constant_dynamic-slice_fusion.7 = (f32[1,1,128,1040]{2,1,0,3:T(1,128)S(1)}, f32[1,1,128,1040]{2,1,0,3:T(1,128)S(1)}, f32[1,1,128,1040]{2,1,0,3:T(1,128)S(1)}, f...) fusion(f32[2,2,128,1040]{2,1,0,3:T(2,128)} %reshape.205, ...), kind=kLoop, calls=%fused_computation.153 | loop fusion | bytes 8519712 | tf_op jit(solution)/shard_map/dynamic_slice | solution.py:77
  178.4 15.1 %collective-permute-done.5 = f32[256,1040]{0,1:T(8,128)} collective-permute-done((f32[256,1040]{0,1:T(8,128)S(1)}, f32[256,1040]{0,1:T(8,128)}, u32[]{:S(2)}, u32[]{:S(2)}) %collective-permute-start.5) | collective-permute-done | bytes 1064992 | tf_op jit(solution)/shard_map/ppermute | solution.py:87
  197.7 8.3 %collective-permute-done.6 = f32[128,1040]{0,1:T(8,128)S(1)} collective-permute-done((f32[128,1040]{0,1:T(8,128)S(1)}, f32[128,1040]{0,1:T(8,128)S(1)}, u32[]{:S(2)}, u32[]{:S(2)}) %collective-permute-start.6) | collective-permute-done | bytes 532512 | tf_op jit(solution)/shard_map/ppermute | solution.py:87
  206.5 6.7 %collective-permute-done.7 = f32[64,1040]{1,0:T(8,128)S(1)} collective-permute-done((f32[64,1040]{1,0:T(8,128)S(1)}, f32[64,1040]{1,0:T(8,128)S(1)}, u32[]{:S(2)}, u32[]{:S(2)}) %collective-permute-start.7) | collective-permute-done | bytes 266272 | tf_op jit(solution)/shard_map/ppermute | solution.py:87
  213.4 6.6 %collective-permute-done.8 = f32[32,1040]{1,0:T(8,128)S(1)} collective-permute-done((f32[32,1040]{1,0:T(8,128)S(1)}, f32[32,1040]{1,0:T(8,128)S(1)}, u32[]{:S(2)}, u32[]{:S(2)}) %collective-permute-start.8) | collective-permute-done | bytes 133152 | tf_op jit(solution)/shard_map/ppermute | solution.py:87
  220.2 6.2 %collective-permute-done.9 = f32[16,1040]{1,0:T(8,128)S(1)} collective-permute-done((f32[16,1040]{1,0:T(8,128)S(1)}, f32[16,1040]{1,0:T(8,128)S(1)}, u32[]{:S(2)}, u32[]{:S(2)}) %collective-permute-start.9) | collective-permute-done | bytes 66592 | tf_op jit(solution)/shard_map/ppermute | solution.py:87
  226.5 2.8 %collective-permute-start.10 = (f32[8,1040]{1,0:T(8,128)S(1)}, f32[8,1040]{1,0:T(8,128)S(1)}, u32[]{:S(2)}, u32[]{:S(2)}) collective-permute-start(f32[8,1040]{1,0:T(8,128)S(1)} %dynamic-slice_bitcast_fusion.5), channel_id=1, source_target_pairs={{0,128},{1,33},{2,130},{3,35},{4,132},{5,37},{6,134},{7,39},{8,136... | collective-permute-start | bytes 99848 | tf_op jit(solution)/shard_map/ppermute | solution.py:87
  232.1 3.8 %collective-permute-start.11 = (f32[4,1040]{1,0:T(4,128)S(1)}, f32[4,1040]{1,0:T(4,128)S(1)}, u32[]{:S(2)}, u32[]{:S(2)}) collective-permute-start(f32[4,1040]{1,0:T(4,128)S(1)} %dynamic-slice_bitcast_fusion.10), channel_id=1, source_target_pairs={{0,64},{1,65},{2,66},{3,67},{4,68},{5,69},{6,70},{7,71},{8,72},{9,... | collective-permute-start | bytes 49928 | tf_op jit(solution)/shard_map/ppermute | solution.py:87
  235.9 4.0 %collective-permute-done.11 = f32[4,1040]{1,0:T(4,128)S(1)} collective-permute-done((f32[4,1040]{1,0:T(4,128)S(1)}, f32[4,1040]{1,0:T(4,128)S(1)}, u32[]{:S(2)}, u32[]{:S(2)}) %collective-permute-start.11) | collective-permute-done | bytes 16672 | tf_op jit(solution)/shard_map/ppermute | solution.py:87
  (126 shorter events, 31.7 us)
Async XLA Ops:
  7.2 9.5 %copy-start.5 = (s32[3,16,16]{2,1,0:T(8,128)S(1)}, s32[3,16,16]{2,1,0:T(8,128)}, u32[]{:S(2)}) copy-start(s32[3,16,16]{2,1,0:T(8,128)} %param.14) | copy-start | bytes 9220
  7.2 124.4 %all-gather.2.cloned.1.call-start = ((), (), s32[]{:S(2)}) async-start(), calls=%async_computation | async-start | bytes 17825792 | tf_op jit(solution)/shard_map/all_gather | solution.py:109
  9.7 9.2 %copy-start.4 = (bf16[7,7,1024]{2,1,0:T(8,128)(2,1)S(1)}, bf16[7,7,1024]{2,1,0:T(8,128)(2,1)}, u32[]{:S(2)}) copy-start(bf16[7,7,1024]{2,1,0:T(8,128)(2,1)} %param.9) | copy-start | bytes 301060
  9.7 9.3 %copy-start.6 = (s32[3,16,16]{2,1,0:T(8,128)S(1)}, s32[3,16,16]{2,1,0:T(8,128)}, u32[]{:S(2)}) copy-start(s32[3,16,16]{2,1,0:T(8,128)} %param.15) | copy-start | bytes 9220
  9.7 11.3 %collective-permute-start = (bf16[3,3,16,1024]{3,2,1,0:T(8,128)(2,1)S(1)}, bf16[3,3,16,1024]{3,2,1,0:T(8,128)(2,1)S(1)}, u32[]{:S(2)}, u32[]{:S(2)}) collective-permute-start(bf16[3,3,16,1024]{3,2,1,0:T(8,128)(2,1)S(1)} %get-tuple-element.14), channel_id=1, source_target_pairs={{0,16},{16,32},{32,48},{48,64},{64,80},{80,96},{96,112},{112,128},... | collective-permute-start | bytes 884744 | tf_op jit(solution)/shard_map/ppermute | solution.py:19
  14.8 11.6 %collective-permute-start.1 = (bf16[3,3,16,1024]{3,2,1,0:T(8,128)(2,1)S(1)}, bf16[3,3,16,1024]{3,2,1,0:T(8,128)(2,1)S(1)}, u32[]{:S(2)}, u32[]{:S(2)}) collective-permute-start(bf16[3,3,16,1024]{3,2,1,0:T(8,128)(2,1)S(1)} %get-tuple-element.15), channel_id=1, source_target_pairs={{16,0},{32,16},{48,32},{64,48},{80,64},{96,80},{112,96},{128,112},... | collective-permute-start | bytes 884744 | tf_op jit(solution)/shard_map/ppermute | solution.py:20
  29.7 15.5 %collective-permute-start.2 = (bf16[3,22,3,1024]{3,1,2,0:T(8,128)(2,1)S(1)}, bf16[3,22,3,1024]{3,1,2,0:T(8,128)(2,1)}, u32[]{:S(2)}, u32[]{:S(2)}) collective-permute-start(bf16[3,22,3,1024]{3,1,2,0:T(8,128)(2,1)S(1)} %get-tuple-element.4), channel_id=1, source_target_pairs={{0,1},{1,2},{2,3},{3,4},{4,5},{5,6},{6,7},{7,8},{8,9},{9,10},{10,1... | collective-permute-start | bytes 1216520 | tf_op jit(solution)/shard_map/ppermute | solution.py:19
  31.6 17.7 %collective-permute-start.3 = (bf16[3,22,3,1024]{3,1,2,0:T(8,128)(2,1)S(1)}, bf16[3,22,3,1024]{3,1,2,0:T(8,128)(2,1)}, u32[]{:S(2)}, u32[]{:S(2)}) collective-permute-start(bf16[3,22,3,1024]{3,1,2,0:T(8,128)(2,1)S(1)} %get-tuple-element.5), channel_id=1, source_target_pairs={{1,0},{2,1},{3,2},{4,3},{5,4},{6,5},{7,6},{8,7},{9,8},{10,9},{11,1... | collective-permute-start | bytes 1216520 | tf_op jit(solution)/shard_map/ppermute | solution.py:20
  50.6 4.3 %copy-start.7 = (f32[8,128]{1,0:T(8,128)S(1)}, f32[8,128]{1,0:T(8,128)}, u32[]{:S(2)}) copy-start(f32[8,128]{1,0:T(8,128)} %get-tuple-element.68) | copy-start | bytes 12292
  50.7 4.3 %copy-start.8 = (f32[8,128]{1,0:T(8,128)S(1)}, f32[8,128]{1,0:T(8,128)}, u32[]{:S(2)}) copy-start(f32[8,128]{1,0:T(8,128)} %get-tuple-element.69) | copy-start | bytes 12292
  50.7 4.2 %copy-start.9 = (f32[8,128]{1,0:T(8,128)S(1)}, f32[8,128]{1,0:T(8,128)}, u32[]{:S(2)}) copy-start(f32[8,128]{1,0:T(8,128)} %get-tuple-element.70) | copy-start | bytes 12292
  50.7 4.2 %copy-start.10 = (f32[8,128]{1,0:T(8,128)S(1)}, f32[8,128]{1,0:T(8,128)}, u32[]{:S(2)}) copy-start(f32[8,128]{1,0:T(8,128)} %get-tuple-element.41) | copy-start | bytes 12292
  117.5 11.1 %copy-start.29 = (f32[1024]{0:T(1024)S(1)}, f32[1024]{0:T(1024)}, u32[]{:S(2)}) copy-start(f32[1024]{0:T(1024)} %param.10) | copy-start | bytes 12292
  155.0 8.4 %copy-start.32 = (bf16[768,1024]{1,0:T(8,128)(2,1)S(1)}, bf16[768,1024]{1,0:T(8,128)(2,1)}, u32[]{:S(2)}) copy-start(bf16[768,1024]{1,0:T(8,128)(2,1)} %get-tuple-element.76) | copy-start | bytes 4718596
  159.0 9.5 %collective-permute-start.4 = (f32[512,1040]{0,1:T(8,128)}, f32[512,1040]{0,1:T(8,128)}, u32[]{:S(2)}, u32[]{:S(2)}) collective-permute-start(f32[512,1040]{0,1:T(8,128)} %fusion.55), channel_id=1, source_target_pairs={{0,1},{1,0},{2,3},{3,2},{4,5},{5,4},{6,7},{7,6},{8,9},{9,8},{10,11... | collective-permute-start | bytes 6389768 | tf_op jit(solution)/shard_map/ppermute | solution.py:130
  178.2 15.3 %copy-start.1 = (f32[1,1,128,1040]{2,1,0,3:T(1,128)S(1)}, f32[1,1,128,1040]{2,1,0,3:T(1,128)}, u32[]{:S(2)}) copy-start(f32[1,1,128,1040]{2,1,0,3:T(1,128)} %get-tuple-element.77) | copy-start | bytes 1597444
  178.2 15.3 %copy-start.2 = (f32[1,1,128,1040]{2,1,0,3:T(1,128)S(1)}, f32[1,1,128,1040]{2,1,0,3:T(1,128)}, u32[]{:S(2)}) copy-start(f32[1,1,128,1040]{2,1,0,3:T(1,128)} %get-tuple-element.80) | copy-start | bytes 1597444
  178.3 15.2 %collective-permute-start.5 = (f32[256,1040]{0,1:T(8,128)S(1)}, f32[256,1040]{0,1:T(8,128)}, u32[]{:S(2)}, u32[]{:S(2)}) collective-permute-start(f32[256,1040]{0,1:T(8,128)S(1)} %maximum_add_fusion.1), channel_id=1, source_target_pairs={{0,2},{1,9},{2,0},{3,11},{4,6},{5,13},{6,4},{7,15},{8,10},{9,1},{1... | collective-permute-start | bytes 3194888 | tf_op jit(solution)/shard_map/ppermute | solution.py:87
  196.7 9.4 %collective-permute-start.6 = (f32[128,1040]{0,1:T(8,128)S(1)}, f32[128,1040]{0,1:T(8,128)S(1)}, u32[]{:S(2)}, u32[]{:S(2)}) collective-permute-start(f32[128,1040]{0,1:T(8,128)S(1)} %bitcast.207), channel_id=1, source_target_pairs={{0,8},{1,3},{2,10},{3,1},{4,12},{5,7},{6,14},{7,5},{8,0},{9,11},{1... | collective-permute-start | bytes 1597448 | tf_op jit(solution)/shard_map/ppermute | solution.py:87
  206.4 6.8 %collective-permute-start.7 = (f32[64,1040]{1,0:T(8,128)S(1)}, f32[64,1040]{1,0:T(8,128)S(1)}, u32[]{:S(2)}, u32[]{:S(2)}) collective-permute-start(f32[64,1040]{1,0:T(8,128)S(1)} %pad_maximum_fusion.6), channel_id=1, source_target_pairs={{0,16},{1,5},{2,18},{3,7},{4,20},{5,1},{6,22},{7,3},{8,24},{9,13},... | collective-permute-start | bytes 798728 | tf_op jit(solution)/shard_map/ppermute | solution.py:87
  213.3 6.7 %collective-permute-start.8 = (f32[32,1040]{1,0:T(8,128)S(1)}, f32[32,1040]{1,0:T(8,128)S(1)}, u32[]{:S(2)}, u32[]{:S(2)}) collective-permute-start(f32[32,1040]{1,0:T(8,128)S(1)} %dynamic-slice_bitcast_fusion), channel_id=1, source_target_pairs={{0,4},{1,17},{2,6},{3,19},{4,0},{5,21},{6,2},{7,23},{8,12},{9,25},... | collective-permute-start | bytes 399368 | tf_op jit(solution)/shard_map/ppermute | solution.py:87
  220.1 6.4 %collective-permute-start.9 = (f32[16,1040]{1,0:T(8,128)S(1)}, f32[16,1040]{1,0:T(8,128)S(1)}, u32[]{:S(2)}, u32[]{:S(2)}) collective-permute-start(f32[16,1040]{1,0:T(8,128)S(1)} %pad_maximum_fusion.7), channel_id=1, source_target_pairs={{0,32},{1,129},{2,34},{3,131},{4,36},{5,133},{6,38},{7,135},{8,40}... | collective-permute-start | bytes 199688 | tf_op jit(solution)/shard_map/ppermute | solution.py:87
  226.5 5.5 %collective-permute-start.10 = (f32[8,1040]{1,0:T(8,128)S(1)}, f32[8,1040]{1,0:T(8,128)S(1)}, u32[]{:S(2)}, u32[]{:S(2)}) collective-permute-start(f32[8,1040]{1,0:T(8,128)S(1)} %dynamic-slice_bitcast_fusion.5), channel_id=1, source_target_pairs={{0,128},{1,33},{2,130},{3,35},{4,132},{5,37},{6,134},{7,39},{8,136... | collective-permute-start | bytes 99848 | tf_op jit(solution)/shard_map/ppermute | solution.py:87
  232.1 7.8 %collective-permute-start.11 = (f32[4,1040]{1,0:T(4,128)S(1)}, f32[4,1040]{1,0:T(4,128)S(1)}, u32[]{:S(2)}, u32[]{:S(2)}) collective-permute-start(f32[4,1040]{1,0:T(4,128)S(1)} %dynamic-slice_bitcast_fusion.10), channel_id=1, source_target_pairs={{0,64},{1,65},{2,66},{3,67},{4,68},{5,69},{6,70},{7,71},{8,72},{9,... | collective-permute-start | bytes 49928 | tf_op jit(solution)/shard_map/ppermute | solution.py:87
  (22 other events, 86.1 us)
Sparse Core Ops, SparseCore 0:
  9.8 105.7 all-gather.1

commit v6 on v4

--- a/solution.py
+++ b/solution.py
@@ -57,7 +57,7 @@
         size *= lax.axis_size(axis)
     me = lax.axis_index(axes)
     core = me & 1
-    for step in range(begin, len(HALVING_BITS[0])):
+    for step in range(begin, len(HALVING_BITS[0]) - 2):
         bit = jnp.where(core, HALVING_BITS[1][step], HALVING_BITS[0][step])
         mine = (me >> bit) & 1
         if HALVING_BITS[0][step] != HALVING_BITS[1][step] and (
@@ -83,7 +83,25 @@
             send = lax.dynamic_index_in_dim(halves, 1 - mine, 0, keepdims=False)
         pairs = [(i, i ^ (1 << HALVING_BITS[i & 1][step])) for i in range(size)]
         part = keep + lax.ppermute(send, axes, pairs)
-    return part
+    last, final = len(HALVING_BITS[0]) - 2, len(HALVING_BITS[0]) - 1
+    quarters = part.reshape((2, 2, part.shape[0] // 4) + part.shape[1:])
+    rest = quarters.shape[2:]
+    upper = (me >> jnp.where(core, HALVING_BITS[1][last], HALVING_BITS[0][last])) & 1
+    lower = (me >> jnp.where(core, HALVING_BITS[1][final], HALVING_BITS[0][final])) & 1
+
+    def quarter(first, second):
+        start = (first, second) + (0,) * len(rest)
+        return lax.dynamic_slice(quarters, start, (1, 1) + rest).reshape(rest)
+
+    total = quarter(upper, lower)
+    for flip_upper, flip_lower in ((1, 0), (0, 1), (1, 1)):
+        pairs = [
+            (i, i ^ (flip_upper << HALVING_BITS[i & 1][last]) ^ (flip_lower << HALVING_BITS[i & 1][final]))
+            for i in range(size)
+        ]
+        piece = quarter(upper ^ flip_upper, lower ^ flip_lower)
+        total = total + lax.ppermute(piece, axes, pairs)
+    return total
 
 
 def targets_of(labels, count):

time: 246 us -> 245 us (level)
  other arithmetic: 91.7 us -> 89.2 us
    ppermute x0 -> x3, starting transfers between devices: none -> 8.99 us  [halving_sum(): total = total + lax.ppermute(piece, axes, pairs)]
    ppermute x7 -> x5, waiting for transfers between devices: 49.5 us -> 42.4 us  [halving_sum(): part = keep + lax.ppermute(send, axes, pairs)]
    ppermute x7 -> x5, starting transfers between devices: 7.28 us -> 0.68 us  [halving_sum(): part = keep + lax.ppermute(send, axes, pairs)]
    ppermute x0 -> x3, waiting for transfers between devices: none -> 4.97 us  [halving_sum(): total = total + lax.ppermute(piece, axes, pairs)]
    reduce_sum x1, other arithmetic: 64.9 us -> 62.4 us  [apply_norm(): mean = jnp.mean(rows, axis=(-2, -1), keepdims=True)]
  transfers between devices with their start and end apart: 13 -> 14, of which waited for: 12 -> 12; matrix products, arithmetic and copies ran while one was open for 41% -> 40% of each run, Pallas kernels for 0% -> 0%
where the time goes in v6:
time: 245 us; the launch traced here: 244 us
  other arithmetic  89.2 us (36%)
  waiting for transfers between devices  63.1 us (26%)
  matrix products  27.6 us (11%)
  starting transfers between devices  26.6 us (11%)
  local copies, waits for them, and re-layouts  22.1 us (9%)
  between operations  14.9 us (6%)
    reduce_sum x1, other arithmetic, apply_norm(): mean = jnp.mean(rows, axis=(-2, -1), keepdims=True)  62.4 us
    ppermute x5, waiting for transfers between devices, halving_sum(): part = keep + lax.ppermute(send, axes, pairs)  42.4 us
    dot_general x1, matrix products, contract(): lax.dot_general(hidden, piece, (((1,), (1,)), ((), ())), preferred_elemen...  21.1 us
    reduce_sum x1, other arithmetic, apply_norm(): var = jnp.mean(centered * centered, axis=(-2, -1), keepdims=True)  11 us
    ppermute x3, starting transfers between devices, halving_sum(): total = total + lax.ppermute(piece, axes, pairs)  8.99 us
    ppermute x2, waiting for transfers between devices, with_halo(): after = lax.ppermute(leading, axis, down)  7.93 us
    ppermute x2, starting transfers between devices, with_halo(): before = lax.ppermute(last, axis, up)  6.96 us
    dot_general x2, matrix products, rows_of(): lax.dot_general(lhs, rhs, (((0,), (0,)), ((), ())), preferred_element_typ...  6.49 us
  transfers between devices with their start and end apart: 14, of which 12 were waited for; matrix products, arithmetic and copies ran while one was open for 40% of the time, Pallas kernels for 0%

profile of v6, /device:TPU:120, one launch (start us, length us, event | category | flops | bytes accessed | tf_op | source)
XLA Modules:
  0.0 243.6 jit_solution(14761394302346821358)
XLA Ops:
  9.7 5.0 %collective-permute-start = (bf16[3,3,16,1024]{3,2,1,0:T(8,128)(2,1)S(1)}, bf16[3,3,16,1024]{3,2,1,0:T(8,128)(2,1)S(1)}, u32[]{:S(2)}, u32[]{:S(2)}) collective-permute-start(bf16[3,3,16,1024]{3,2,1,0:T(8,128)(2,1)S(1)} %get-tuple-element.10), channel_id=1, source_target_pairs={{0,16},{16,32},{32,48},{48,64},{64,80},{80,96},{96,112},{112,128},... | collective-permute-start | bytes 884744 | tf_op jit(solution)/shard_map/ppermute | solution.py:19
  21.3 5.1 %collective-permute-done.1 = bf16[3,3,16,1024]{3,2,1,0:T(8,128)(2,1)S(1)} collective-permute-done((bf16[3,3,16,1024]{3,2,1,0:T(8,128)(2,1)S(1)}, bf16[3,3,16,1024]{3,2,1,0:T(8,128)(2,1)S(1)}, u32[]{:S(2)}, u32[]{:S(2)}) %collective-permute-start.1) | collective-permute-done | bytes 294944 | tf_op jit(solution)/shard_map/ppermute | solution.py:20
  26.6 3.0 %pad_maximum_fusion.1 = bf16[3,22,16,1024]{3,1,2,0:T(8,128)(2,1)S(1)} fusion(bf16[3,3,16,1024]{3,1,2,0:T(4,128)(2,1)S(1)} %copy.63, bf16[3,16,16,1024]{3,1,2,0:T(8,128)(2,1)} %copy.62, bf16[3,3,16,1024]{3,1,2,0:T(4,128)(2,1)S(1)} %copy.61), kind=kLoop, calls=%fused_computation.108 | loop fusion | flops 6488064 | bytes 4325376 | tf_op jit(solution)/shard_map/concatenate | solution.py:21
  31.6 3.6 %collective-permute-start.3 = (bf16[3,22,3,1024]{3,1,2,0:T(8,128)(2,1)S(1)}, bf16[3,22,3,1024]{3,1,2,0:T(8,128)(2,1)}, u32[]{:S(2)}, u32[]{:S(2)}) collective-permute-start(bf16[3,22,3,1024]{3,1,2,0:T(8,128)(2,1)S(1)} %get-tuple-element.5), channel_id=1, source_target_pairs={{1,0},{2,1},{3,2},{4,3},{5,4},{6,5},{7,6},{8,7},{9,8},{10,9},{11,1... | collective-permute-start | bytes 1216520 | tf_op jit(solution)/shard_map/ppermute | solution.py:20
  36.5 2.8 %reshape.221 = bf16[3,22,16,8,128]{4,3,1,2,0:T(8,128)(2,1)} reshape(bf16[3,22,16,1024]{3,1,2,0:T(8,128)(2,1)S(1)} %pad_maximum_fusion.1) | data formatting | bytes 4325376 | tf_op jit(solution)/shard_map/concatenate | solution.py:21
  39.3 5.9 %collective-permute-done.2 = bf16[3,22,3,1024]{3,1,2,0:T(8,128)(2,1)} collective-permute-done((bf16[3,22,3,1024]{3,1,2,0:T(8,128)(2,1)S(1)}, bf16[3,22,3,1024]{3,1,2,0:T(8,128)(2,1)}, u32[]{:S(2)}, u32[]{:S(2)}) %collective-permute-start.2) | collective-permute-done | bytes 405536 | tf_op jit(solution)/shard_map/ppermute | solution.py:19
  46.5 2.9 %collective-permute-done.3 = bf16[3,22,3,1024]{3,1,2,0:T(8,128)(2,1)} collective-permute-done((bf16[3,22,3,1024]{3,1,2,0:T(8,128)(2,1)S(1)}, bf16[3,22,3,1024]{3,1,2,0:T(8,128)(2,1)}, u32[]{:S(2)}, u32[]{:S(2)}) %collective-permute-start.3) | collective-permute-done | bytes 405536 | tf_op jit(solution)/shard_map/ppermute | solution.py:20
  50.9 4.0 %copy_convert_fusion = f32[3,22,22,8,128]{4,3,2,1,0:T(8,128)} fusion(bf16[3,22,3,8,128]{4,3,1,2,0:T(8,128)(2,1)S(1)} %concatenate.37, bf16[3,22,16,8,128]{4,3,1,2,0:T(8,128)(2,1)} %reshape.221, bf16[3,22,3,8,128]{4,3,1,2,0:T(8,128)(2,1)S(1)} %concatenate.35), kind=kLoop, calls=%fused_computation.107 | loop fusion | flops 4460544 | bytes 8921088 | tf_op jit(solution)/shard_map/convert_element_type | solution.py:116
  55.1 62.4 %fusion.68 = (f32[3,16,16]{2,1,0:T(8,128)S(1)}, f32[3,16,16,8,128]{4,3,2,1,0:T(8,128)S(1)}) fusion(f32[8,128]{1,0:T(8,128)S(1)} %get-tuple-element.19, f32[3,22,22,8,128]{4,3,2,1,0:T(8,128)} %copy_convert_fusion, f32[8,128]{1,0:T(8,128)S(1)} %get-tuple-element.20, f32[8,128]{1,0:T(8,128)S(1)} %get-tuple-element.21, f32[8,128]{1,0:T(8,128)S(1)} %get-tuple-element.22, ...), kind=kLoop, calls=%fused_computation.209 | loop fusion | flops 77069568 | bytes 157490176 | tf_op jit(solution)/shard_map/reduce_sum | solution.py:26
  117.6 11.0 %multiply_reduce_fusion = f32[3,16,16]{2,1,0:T(8,128)S(1)} fusion(f32[3,16,16,8,128]{4,3,2,1,0:T(8,128)S(1)} %get-tuple-element.3, f32[3,16,16]{2,1,0:T(8,128)S(1)} %broadcast_multiply_fusion.1), kind=kLoop, calls=%fused_computation.105 | loop fusion | flops 2358528 | bytes 3151872 | tf_op jit(solution)/shard_map/reduce_sum | solution.py:28
  128.6 3.0 %multiply_convert_fusion.1 = bf16[3,16,16,8,128]{4,3,2,1,0:T(8,128)(2,1)} fusion(f32[3,16,16,8,128]{4,3,2,1,0:T(8,128)S(1)} %get-tuple-element.3, f32[8,128]{1,0:T(8,128)S(1)} %bitcast.202, f32[3,16,16]{2,1,0:T(8,128)S(1)} %add_rsqrt_fusion, f32[3,16,16]{2,1,0:T(8,128)S(1)} %broadcast_multiply_fusion.1), kind=kLoop, calls=%fused_computation.104 | loop fusion | flops 3145728 | bytes 4728832 | tf_op jit(solution)/shard_map/convert_element_type | solution.py:29
  131.6 21.1 %broadcast_multiply_fusion = (bf16[768,1024]{1,0:T(8,128)(2,1)S(1)}, bf16[768,1024]{1,0:T(8,128)(2,1)}) fusion(bf16[768]{0:T(1024)(128)(2,1)S(1)} %copy-done.29, bf16[2,1024,4096]{2,1,0:T(8,128)(2,1)} %all-gather.2.cloned.1.call-done, bf16[96,8,8,128]{3,2,1,0:T(8,128)(2,1)} %bitcast.195, f32[1024]{0:T(1024)S(1)} %copy-done.30, bf16[768,1024]{1,0:T(8,128)(2,1)} %bitcast.189), kind=kOutput, calls=%fused_computation.119 | convolution fusion | flops 12906921984 | bytes 23074304 | tf_op jit(solution)/shard_map/dot_general | solution.py:38
  156.2 3.8 %fusion.55 = f32[512,1040]{0,1:T(8,128)} fusion(bf16[768,16]{1,0:T(8,128)(2,1)S(1)} %copy-done.2, bf16[768,1024]{1,0:T(8,128)(2,1)} %get-tuple-element.75, bf16[768,1024]{0,1:T(8,128)(2,1)S(1)} %reshape.195, s32[]{:T(128)S(6)} %select_n.203), kind=kOutput, calls=%fused_computation.112 | convolution fusion | flops 821084160 | bytes 4685828 | tf_op jit(solution)/shard_map/dot_general | solution.py:141
  160.0 4.4 %collective-permute-start.4 = (f32[512,1040]{0,1:T(8,128)}, f32[512,1040]{0,1:T(8,128)S(1)}, u32[]{:S(2)}, u32[]{:S(2)}) collective-permute-start(f32[512,1040]{0,1:T(8,128)} %fusion.55), channel_id=1, source_target_pairs={{0,1},{1,0},{2,3},{3,2},{4,5},{5,4},{6,7},{7,6},{8,9},{9,8},{10,11... | collective-permute-start | bytes 6389768 | tf_op jit(solution)/shard_map/ppermute | solution.py:146
  164.3 2.7 %fusion.56 = f32[512,1040]{0,1:T(8,128)S(1)} fusion(bf16[768,16]{1,0:T(8,128)(2,1)S(1)} %copy-done.2, bf16[768,1024]{1,0:T(8,128)(2,1)} %get-tuple-element.75, bf16[768,1024]{0,1:T(8,128)(2,1)} %copy-done.1, s32[]{:T(128)S(6)} %select_n.202), kind=kOutput, calls=%fused_computation.113 | convolution fusion | flops 821084160 | bytes 4513796 | tf_op jit(solution)/shard_map/dot_general | solution.py:141
  170.2 2.7 %reshape.196 = f32[2,2,128,1040]{2,1,0,3:T(2,128)S(1)} reshape(f32[512,1040]{0,1:T(8,128)} %add.362) | data formatting | bytes 4259840 | tf_op jit(solution)/shard_map/reshape | solution.py:66
  175.3 14.9 %collective-permute-done.5 = f32[256,1040]{0,1:T(8,128)S(1)} collective-permute-done((f32[256,1040]{0,1:T(8,128)S(1)}, f32[256,1040]{0,1:T(8,128)S(1)}, u32[]{:S(2)}, u32[]{:S(2)}) %collective-permute-start.5) | collective-permute-done | bytes 1064992 | tf_op jit(solution)/shard_map/ppermute | solution.py:85
  193.1 8.3 %collective-permute-done.6 = f32[128,1040]{0,1:T(8,128)S(1)} collective-permute-done((f32[128,1040]{0,1:T(8,128)S(1)}, f32[128,1040]{0,1:T(8,128)S(1)}, u32[]{:S(2)}, u32[]{:S(2)}) %collective-permute-start.6) | collective-permute-done | bytes 532512 | tf_op jit(solution)/shard_map/ppermute | solution.py:85
  201.9 6.7 %collective-permute-done.7 = f32[64,1040]{1,0:T(8,128)S(1)} collective-permute-done((f32[64,1040]{1,0:T(8,128)S(1)}, f32[64,1040]{1,0:T(8,128)S(1)}, u32[]{:S(2)}, u32[]{:S(2)}) %collective-permute-start.7) | collective-permute-done | bytes 266272 | tf_op jit(solution)/shard_map/ppermute | solution.py:85
  208.8 6.6 %collective-permute-done.8 = f32[32,1040]{1,0:T(8,128)S(1)} collective-permute-done((f32[32,1040]{1,0:T(8,128)S(1)}, f32[32,1040]{1,0:T(8,128)S(1)}, u32[]{:S(2)}, u32[]{:S(2)}) %collective-permute-start.8) | collective-permute-done | bytes 133152 | tf_op jit(solution)/shard_map/ppermute | solution.py:85
  215.6 5.8 %collective-permute-done.9 = f32[16,1040]{1,0:T(8,128)S(1)} collective-permute-done((f32[16,1040]{1,0:T(8,128)S(1)}, f32[16,1040]{1,0:T(8,128)S(1)}, u32[]{:S(2)}, u32[]{:S(2)}) %collective-permute-start.9) | collective-permute-done | bytes 66592 | tf_op jit(solution)/shard_map/ppermute | solution.py:85
  221.5 3.0 %collective-permute-start.10 = (f32[4,1040]{1,0:T(4,128)S(1)}, f32[4,1040]{1,0:T(4,128)S(1)}, u32[]{:S(2)}, u32[]{:S(2)}) collective-permute-start(f32[4,1040]{1,0:T(4,128)S(1)} %get-tuple-element.71), channel_id=1, source_target_pairs={{0,128},{1,33},{2,130},{3,35},{4,132},{5,37},{6,134},{7,39},{8,136... | collective-permute-start | bytes 49928 | tf_op jit(solution)/shard_map/ppermute | solution.py:103
  225.4 5.1 %collective-permute-start.12 = (f32[4,1040]{1,0:T(4,128)S(1)}, f32[4,1040]{1,0:T(4,128)S(1)}, u32[]{:S(2)}, u32[]{:S(2)}) collective-permute-start(f32[4,1040]{1,0:T(4,128)S(1)} %get-tuple-element.72), channel_id=1, source_target_pairs={{0,192},{1,97},{2,194},{3,99},{4,196},{5,101},{6,198},{7,103},{8,2... | collective-permute-start | bytes 49928 | tf_op jit(solution)/shard_map/ppermute | solution.py:103
  232.2 3.3 %collective-permute-done.12 = f32[4,1040]{1,0:T(4,128)S(1)} collective-permute-done((f32[4,1040]{1,0:T(4,128)S(1)}, f32[4,1040]{1,0:T(4,128)S(1)}, u32[]{:S(2)}, u32[]{:S(2)}) %collective-permute-start.12) | collective-permute-done | bytes 16672 | tf_op jit(solution)/shard_map/ppermute | solution.py:103
  (122 shorter events, 31.5 us)
Async XLA Ops:
  7.2 9.5 %copy-start.4 = (s32[3,16,16]{2,1,0:T(8,128)S(1)}, s32[3,16,16]{2,1,0:T(8,128)}, u32[]{:S(2)}) copy-start(s32[3,16,16]{2,1,0:T(8,128)} %param.14) | copy-start | bytes 9220
  7.2 124.4 %all-gather.2.cloned.1.call-start = ((), (), s32[]{:S(2)}) async-start(), calls=%async_computation | async-start | bytes 17825792 | tf_op jit(solution)/shard_map/all_gather | solution.py:125
  9.7 9.2 %copy-start.3 = (bf16[7,7,1024]{2,1,0:T(8,128)(2,1)S(1)}, bf16[7,7,1024]{2,1,0:T(8,128)(2,1)}, u32[]{:S(2)}) copy-start(bf16[7,7,1024]{2,1,0:T(8,128)(2,1)} %param.9) | copy-start | bytes 301060
  9.7 9.3 %copy-start.5 = (s32[3,16,16]{2,1,0:T(8,128)S(1)}, s32[3,16,16]{2,1,0:T(8,128)}, u32[]{:S(2)}) copy-start(s32[3,16,16]{2,1,0:T(8,128)} %param.15) | copy-start | bytes 9220
  9.7 11.3 %collective-permute-start = (bf16[3,3,16,1024]{3,2,1,0:T(8,128)(2,1)S(1)}, bf16[3,3,16,1024]{3,2,1,0:T(8,128)(2,1)S(1)}, u32[]{:S(2)}, u32[]{:S(2)}) collective-permute-start(bf16[3,3,16,1024]{3,2,1,0:T(8,128)(2,1)S(1)} %get-tuple-element.10), channel_id=1, source_target_pairs={{0,16},{16,32},{32,48},{48,64},{64,80},{80,96},{96,112},{112,128},... | collective-permute-start | bytes 884744 | tf_op jit(solution)/shard_map/ppermute | solution.py:19
  14.8 11.6 %collective-permute-start.1 = (bf16[3,3,16,1024]{3,2,1,0:T(8,128)(2,1)S(1)}, bf16[3,3,16,1024]{3,2,1,0:T(8,128)(2,1)S(1)}, u32[]{:S(2)}, u32[]{:S(2)}) collective-permute-start(bf16[3,3,16,1024]{3,2,1,0:T(8,128)(2,1)S(1)} %get-tuple-element.11), channel_id=1, source_target_pairs={{16,0},{32,16},{48,32},{64,48},{80,64},{96,80},{112,96},{128,112},... | collective-permute-start | bytes 884744 | tf_op jit(solution)/shard_map/ppermute | solution.py:20
  29.7 15.5 %collective-permute-start.2 = (bf16[3,22,3,1024]{3,1,2,0:T(8,128)(2,1)S(1)}, bf16[3,22,3,1024]{3,1,2,0:T(8,128)(2,1)}, u32[]{:S(2)}, u32[]{:S(2)}) collective-permute-start(bf16[3,22,3,1024]{3,1,2,0:T(8,128)(2,1)S(1)} %get-tuple-element.4), channel_id=1, source_target_pairs={{0,1},{1,2},{2,3},{3,4},{4,5},{5,6},{6,7},{7,8},{8,9},{9,10},{10,1... | collective-permute-start | bytes 1216520 | tf_op jit(solution)/shard_map/ppermute | solution.py:19
  31.6 17.7 %collective-permute-start.3 = (bf16[3,22,3,1024]{3,1,2,0:T(8,128)(2,1)S(1)}, bf16[3,22,3,1024]{3,1,2,0:T(8,128)(2,1)}, u32[]{:S(2)}, u32[]{:S(2)}) collective-permute-start(bf16[3,22,3,1024]{3,1,2,0:T(8,128)(2,1)S(1)} %get-tuple-element.5), channel_id=1, source_target_pairs={{1,0},{2,1},{3,2},{4,3},{5,4},{6,5},{7,6},{8,7},{9,8},{10,9},{11,1... | collective-permute-start | bytes 1216520 | tf_op jit(solution)/shard_map/ppermute | solution.py:20
  50.6 4.3 %copy-start.6 = (f32[8,128]{1,0:T(8,128)S(1)}, f32[8,128]{1,0:T(8,128)}, u32[]{:S(2)}) copy-start(f32[8,128]{1,0:T(8,128)} %get-tuple-element.64) | copy-start | bytes 12292
  50.7 4.3 %copy-start.7 = (f32[8,128]{1,0:T(8,128)S(1)}, f32[8,128]{1,0:T(8,128)}, u32[]{:S(2)}) copy-start(f32[8,128]{1,0:T(8,128)} %get-tuple-element.65) | copy-start | bytes 12292
  50.7 4.2 %copy-start.8 = (f32[8,128]{1,0:T(8,128)S(1)}, f32[8,128]{1,0:T(8,128)}, u32[]{:S(2)}) copy-start(f32[8,128]{1,0:T(8,128)} %get-tuple-element.66) | copy-start | bytes 12292
  50.7 4.2 %copy-start.9 = (f32[8,128]{1,0:T(8,128)S(1)}, f32[8,128]{1,0:T(8,128)}, u32[]{:S(2)}) copy-start(f32[8,128]{1,0:T(8,128)} %get-tuple-element.37) | copy-start | bytes 12292
  50.7 4.2 %copy-start.10 = (f32[8,128]{1,0:T(8,128)S(1)}, f32[8,128]{1,0:T(8,128)}, u32[]{:S(2)}) copy-start(f32[8,128]{1,0:T(8,128)} %get-tuple-element.38) | copy-start | bytes 12292
  50.7 4.2 %copy-start.11 = (f32[8,128]{1,0:T(8,128)S(1)}, f32[8,128]{1,0:T(8,128)}, u32[]{:S(2)}) copy-start(f32[8,128]{1,0:T(8,128)} %get-tuple-element.39) | copy-start | bytes 12292
  117.5 11.1 %copy-start.28 = (f32[1024]{0:T(1024)S(1)}, f32[1024]{0:T(1024)}, u32[]{:S(2)}) copy-start(f32[1024]{0:T(1024)} %param.10) | copy-start | bytes 12292
  160.0 8.4 %collective-permute-start.4 = (f32[512,1040]{0,1:T(8,128)}, f32[512,1040]{0,1:T(8,128)S(1)}, u32[]{:S(2)}, u32[]{:S(2)}) collective-permute-start(f32[512,1040]{0,1:T(8,128)} %fusion.55), channel_id=1, source_target_pairs={{0,1},{1,0},{2,3},{3,2},{4,5},{5,4},{6,7},{7,6},{8,9},{9,8},{10,11... | collective-permute-start | bytes 6389768 | tf_op jit(solution)/shard_map/ppermute | solution.py:146
  174.9 15.3 %collective-permute-start.5 = (f32[256,1040]{0,1:T(8,128)S(1)}, f32[256,1040]{0,1:T(8,128)S(1)}, u32[]{:S(2)}, u32[]{:S(2)}) collective-permute-start(f32[256,1040]{0,1:T(8,128)S(1)} %pad_maximum_fusion.5), channel_id=1, source_target_pairs={{0,2},{1,9},{2,0},{3,11},{4,6},{5,13},{6,4},{7,15},{8,10},{9,1},{1... | collective-permute-start | bytes 3194888 | tf_op jit(solution)/shard_map/ppermute | solution.py:85
  192.0 9.4 %collective-permute-start.6 = (f32[128,1040]{0,1:T(8,128)S(1)}, f32[128,1040]{0,1:T(8,128)S(1)}, u32[]{:S(2)}, u32[]{:S(2)}) collective-permute-start(f32[128,1040]{0,1:T(8,128)S(1)} %bitcast.199), channel_id=1, source_target_pairs={{0,8},{1,3},{2,10},{3,1},{4,12},{5,7},{6,14},{7,5},{8,0},{9,11},{1... | collective-permute-start | bytes 1597448 | tf_op jit(solution)/shard_map/ppermute | solution.py:85
  201.8 6.8 %collective-permute-start.7 = (f32[64,1040]{1,0:T(8,128)S(1)}, f32[64,1040]{1,0:T(8,128)S(1)}, u32[]{:S(2)}, u32[]{:S(2)}) collective-permute-start(f32[64,1040]{1,0:T(8,128)S(1)} %pad_maximum_fusion.7), channel_id=1, source_target_pairs={{0,16},{1,5},{2,18},{3,7},{4,20},{5,1},{6,22},{7,3},{8,24},{9,13},... | collective-permute-start | bytes 798728 | tf_op jit(solution)/shard_map/ppermute | solution.py:85
  208.7 6.7 %collective-permute-start.8 = (f32[32,1040]{1,0:T(8,128)S(1)}, f32[32,1040]{1,0:T(8,128)S(1)}, u32[]{:S(2)}, u32[]{:S(2)}) collective-permute-start(f32[32,1040]{1,0:T(8,128)S(1)} %dynamic-slice_bitcast_fusion), channel_id=1, source_target_pairs={{0,4},{1,17},{2,6},{3,19},{4,0},{5,21},{6,2},{7,23},{8,12},{9,25},... | collective-permute-start | bytes 399368 | tf_op jit(solution)/shard_map/ppermute | solution.py:85
  215.5 6.0 %collective-permute-start.9 = (f32[16,1040]{1,0:T(8,128)S(1)}, f32[16,1040]{1,0:T(8,128)S(1)}, u32[]{:S(2)}, u32[]{:S(2)}) collective-permute-start(f32[16,1040]{1,0:T(8,128)S(1)} %pad_maximum_fusion.8), channel_id=1, source_target_pairs={{0,32},{1,129},{2,34},{3,131},{4,36},{5,133},{6,38},{7,135},{8,40}... | collective-permute-start | bytes 199688 | tf_op jit(solution)/shard_map/ppermute | solution.py:85
  221.5 9.0 %collective-permute-start.10 = (f32[4,1040]{1,0:T(4,128)S(1)}, f32[4,1040]{1,0:T(4,128)S(1)}, u32[]{:S(2)}, u32[]{:S(2)}) collective-permute-start(f32[4,1040]{1,0:T(4,128)S(1)} %get-tuple-element.71), channel_id=1, source_target_pairs={{0,128},{1,33},{2,130},{3,35},{4,132},{5,37},{6,134},{7,39},{8,136... | collective-permute-start | bytes 49928 | tf_op jit(solution)/shard_map/ppermute | solution.py:103
  224.6 7.7 %collective-permute-start.11 = (f32[4,1040]{1,0:T(4,128)S(1)}, f32[4,1040]{1,0:T(4,128)S(1)}, u32[]{:S(2)}, u32[]{:S(2)}) collective-permute-start(f32[4,1040]{1,0:T(4,128)S(1)} %get-tuple-element.73), channel_id=1, source_target_pairs={{0,64},{1,65},{2,66},{3,67},{4,68},{5,69},{6,70},{7,71},{8,72},{9,... | collective-permute-start | bytes 49928 | tf_op jit(solution)/shard_map/ppermute | solution.py:103
  225.4 10.1 %collective-permute-start.12 = (f32[4,1040]{1,0:T(4,128)S(1)}, f32[4,1040]{1,0:T(4,128)S(1)}, u32[]{:S(2)}, u32[]{:S(2)}) collective-permute-start(f32[4,1040]{1,0:T(4,128)S(1)} %get-tuple-element.72), channel_id=1, source_target_pairs={{0,192},{1,97},{2,194},{3,99},{4,196},{5,101},{6,198},{7,103},{8,2... | collective-permute-start | bytes 49928 | tf_op jit(solution)/shard_map/ppermute | solution.py:103
  (21 other events, 79.9 us)
Sparse Core Ops, SparseCore 0:
  9.8 105.7 all-gather.1

commit v7 on v6

--- a/solution.py
+++ b/solution.py
@@ -51,13 +51,13 @@
     return split.transpose(order).reshape(count, width)
 
 
-def halving_sum(part, axes, begin):
+def halving_sum(part, axes, steps):
     size = 1
     for axis in axes:
         size *= lax.axis_size(axis)
     me = lax.axis_index(axes)
     core = me & 1
-    for step in range(begin, len(HALVING_BITS[0]) - 2):
+    for step in steps:
         bit = jnp.where(core, HALVING_BITS[1][step], HALVING_BITS[0][step])
         mine = (me >> bit) & 1
         if HALVING_BITS[0][step] != HALVING_BITS[1][step] and (
@@ -83,11 +83,19 @@
             send = lax.dynamic_index_in_dim(halves, 1 - mine, 0, keepdims=False)
         pairs = [(i, i ^ (1 << HALVING_BITS[i & 1][step])) for i in range(size)]
         part = keep + lax.ppermute(send, axes, pairs)
-    last, final = len(HALVING_BITS[0]) - 2, len(HALVING_BITS[0]) - 1
+    return part
+
+
+def radix4(part, axes, upper_bits, lower_bits):
+    size = 1
+    for axis in axes:
+        size *= lax.axis_size(axis)
+    me = lax.axis_index(axes)
+    core = me & 1
     quarters = part.reshape((2, 2, part.shape[0] // 4) + part.shape[1:])
     rest = quarters.shape[2:]
-    upper = (me >> jnp.where(core, HALVING_BITS[1][last], HALVING_BITS[0][last])) & 1
-    lower = (me >> jnp.where(core, HALVING_BITS[1][final], HALVING_BITS[0][final])) & 1
+    upper = (me >> jnp.where(core, upper_bits[1], upper_bits[0])) & 1
+    lower = (me >> jnp.where(core, lower_bits[1], lower_bits[0])) & 1
 
     def quarter(first, second):
         start = (first, second) + (0,) * len(rest)
@@ -96,7 +104,7 @@
     total = quarter(upper, lower)
     for flip_upper, flip_lower in ((1, 0), (0, 1), (1, 1)):
         pairs = [
-            (i, i ^ (flip_upper << HALVING_BITS[i & 1][last]) ^ (flip_lower << HALVING_BITS[i & 1][final]))
+            (i, i ^ (flip_upper << upper_bits[i & 1]) ^ (flip_lower << lower_bits[i & 1]))
             for i in range(size)
         ]
         piece = quarter(upper ^ flip_upper, lower ^ flip_lower)
@@ -145,7 +153,10 @@
     size = lax.axis_size("row") * lax.axis_size("col")
     sent = lax.ppermute(rows_of(1 - core), axes, [(i, i ^ 1) for i in range(size)])
     kept = lax.optimization_barrier(rows_of(core))
-    summed = halving_sum(kept + sent, axes, 1)
+    summed = halving_sum(kept + sent, axes, (1, 2))
+    summed = radix4(summed, axes, (HALVING_BITS[0][3],) * 2, (HALVING_BITS[0][4],) * 2)
+    summed = halving_sum(summed, axes, (5,))
+    summed = radix4(summed, axes, tuple(b[6] for b in HALVING_BITS), tuple(b[7] for b in HALVING_BITS))
     gram_sum, cross_sum = summed[:, :width], summed[:, width:]
     total = float(tiles * high * lax.axis_size("row") * wide * lax.axis_size("col"))
     return (gram_sum / total, cross_sum / jnp.sqrt(jnp.float32(total)))

time: 245 us -> 247 us (level); the launches traced: 244 us -> 242 us
  waiting for transfers between devices: 63.1 us -> 53.6 us
  starting transfers between devices: 26.6 us -> 31.5 us
  other arithmetic: 89.2 us -> 92.3 us
    ppermute x5 -> x3, waiting for transfers between devices: 42.4 us -> 28.5 us  [halving_sum(): part = keep + lax.ppermute(send, axes, pairs)]
    ppermute x3 -> x6, starting transfers between devices: 8.99 us -> 14.1 us  [radix4(): total = total + lax.ppermute(piece, axes, pairs)]
    ppermute x3 -> x6, waiting for transfers between devices: 4.97 us -> 9.33 us  [radix4(): total = total + lax.ppermute(piece, axes, pairs)]
    reduce_sum x1, other arithmetic: 62.4 us -> 65.5 us  [apply_norm(): mean = jnp.mean(rows, axis=(-2, -1), keepdims=True)]
  transfers between devices with their start and end apart: 14 -> 15, of which waited for: 12 -> 12; matrix products, arithmetic and copies ran while one was open for 40% -> 42% of each run, Pallas kernels for 0% -> 0%
where the time goes in v7:
time: 247 us; the launch traced here: 242 us
  other arithmetic  92.3 us (37%)
  waiting for transfers between devices  53.6 us (22%)
  starting transfers between devices  31.5 us (13%)
  matrix products  27.6 us (11%)
  local copies, waits for them, and re-layouts  22.1 us (9%)
  between operations  14.8 us (6%)
    reduce_sum x1, other arithmetic, apply_norm(): mean = jnp.mean(rows, axis=(-2, -1), keepdims=True)  65.5 us
    ppermute x3, waiting for transfers between devices, halving_sum(): part = keep + lax.ppermute(send, axes, pairs)  28.5 us
    dot_general x1, matrix products, contract(): lax.dot_general(hidden, piece, (((1,), (1,)), ((), ())), preferred_elemen...  21.1 us
    ppermute x6, starting transfers between devices, radix4(): total = total + lax.ppermute(piece, axes, pairs)  14.1 us
    reduce_sum x1, other arithmetic, apply_norm(): var = jnp.mean(centered * centered, axis=(-2, -1), keepdims=True)  11 us
    ppermute x6, waiting for transfers between devices, radix4(): total = total + lax.ppermute(piece, axes, pairs)  9.33 us
    ppermute x2, waiting for transfers between devices, with_halo(): after = lax.ppermute(leading, axis, down)  7.92 us
    ppermute x2, starting transfers between devices, with_halo(): before = lax.ppermute(last, axis, up)  6.96 us
  transfers between devices with their start and end apart: 15, of which 12 were waited for; matrix products, arithmetic and copies ran while one was open for 42% of the time, Pallas kernels for 0%

profile of v7, /device:TPU:120, one launch (start us, length us, event | category | flops | bytes accessed | tf_op | source)
XLA Modules:
  0.0 241.8 jit_solution(4995667333226711712)
XLA Ops:
  9.7 5.0 %collective-permute-start = (bf16[3,3,16,1024]{3,2,1,0:T(8,128)(2,1)S(1)}, bf16[3,3,16,1024]{3,2,1,0:T(8,128)(2,1)S(1)}, u32[]{:S(2)}, u32[]{:S(2)}) collective-permute-start(bf16[3,3,16,1024]{3,2,1,0:T(8,128)(2,1)S(1)} %get-tuple-element.10), channel_id=1, source_target_pairs={{0,16},{16,32},{32,48},{48,64},{64,80},{80,96},{96,112},{112,128},... | collective-permute-start | bytes 884744 | tf_op jit(solution)/shard_map/ppermute | solution.py:19
  21.3 5.1 %collective-permute-done.1 = bf16[3,3,16,1024]{3,2,1,0:T(8,128)(2,1)S(1)} collective-permute-done((bf16[3,3,16,1024]{3,2,1,0:T(8,128)(2,1)S(1)}, bf16[3,3,16,1024]{3,2,1,0:T(8,128)(2,1)S(1)}, u32[]{:S(2)}, u32[]{:S(2)}) %collective-permute-start.1) | collective-permute-done | bytes 294944 | tf_op jit(solution)/shard_map/ppermute | solution.py:20
  26.6 3.0 %pad_maximum_fusion.1 = bf16[3,22,16,1024]{3,1,2,0:T(8,128)(2,1)S(1)} fusion(bf16[3,3,16,1024]{3,1,2,0:T(4,128)(2,1)S(1)} %copy.62, bf16[3,16,16,1024]{3,1,2,0:T(8,128)(2,1)} %copy.61, bf16[3,3,16,1024]{3,1,2,0:T(4,128)(2,1)S(1)} %copy.60), kind=kLoop, calls=%fused_computation.108 | loop fusion | flops 6488064 | bytes 4325376 | tf_op jit(solution)/shard_map/concatenate | solution.py:21
  31.6 3.6 %collective-permute-start.3 = (bf16[3,22,3,1024]{3,1,2,0:T(8,128)(2,1)S(1)}, bf16[3,22,3,1024]{3,1,2,0:T(8,128)(2,1)}, u32[]{:S(2)}, u32[]{:S(2)}) collective-permute-start(bf16[3,22,3,1024]{3,1,2,0:T(8,128)(2,1)S(1)} %get-tuple-element.5), channel_id=1, source_target_pairs={{1,0},{2,1},{3,2},{4,3},{5,4},{6,5},{7,6},{8,7},{9,8},{10,9},{11,1... | collective-permute-start | bytes 1216520 | tf_op jit(solution)/shard_map/ppermute | solution.py:20
  36.6 2.7 %reshape.217 = bf16[3,22,16,8,128]{4,3,1,2,0:T(8,128)(2,1)} reshape(bf16[3,22,16,1024]{3,1,2,0:T(8,128)(2,1)S(1)} %pad_maximum_fusion.1) | data formatting | bytes 4325376 | tf_op jit(solution)/shard_map/concatenate | solution.py:21
  39.3 5.9 %collective-permute-done.2 = bf16[3,22,3,1024]{3,1,2,0:T(8,128)(2,1)} collective-permute-done((bf16[3,22,3,1024]{3,1,2,0:T(8,128)(2,1)S(1)}, bf16[3,22,3,1024]{3,1,2,0:T(8,128)(2,1)}, u32[]{:S(2)}, u32[]{:S(2)}) %collective-permute-start.2) | collective-permute-done | bytes 405536 | tf_op jit(solution)/shard_map/ppermute | solution.py:19
  46.5 2.9 %collective-permute-done.3 = bf16[3,22,3,1024]{3,1,2,0:T(8,128)(2,1)} collective-permute-done((bf16[3,22,3,1024]{3,1,2,0:T(8,128)(2,1)S(1)}, bf16[3,22,3,1024]{3,1,2,0:T(8,128)(2,1)}, u32[]{:S(2)}, u32[]{:S(2)}) %collective-permute-start.3) | collective-permute-done | bytes 405536 | tf_op jit(solution)/shard_map/ppermute | solution.py:20
  50.9 4.0 %copy_convert_fusion = f32[3,22,22,8,128]{4,3,2,1,0:T(8,128)} fusion(bf16[3,22,3,8,128]{4,3,1,2,0:T(8,128)(2,1)S(1)} %concatenate.31, bf16[3,22,16,8,128]{4,3,1,2,0:T(8,128)(2,1)} %reshape.217, bf16[3,22,3,8,128]{4,3,1,2,0:T(8,128)(2,1)S(1)} %concatenate.29), kind=kLoop, calls=%fused_computation.107 | loop fusion | flops 4460544 | bytes 8921088 | tf_op jit(solution)/shard_map/convert_element_type | solution.py:124
  55.1 65.5 %fusion.70 = (f32[3,16,16]{2,1,0:T(8,128)S(1)}, f32[3,16,16,8,128]{4,3,2,1,0:T(8,128)S(1)}) fusion(f32[8,128]{1,0:T(8,128)S(1)} %get-tuple-element.18, f32[3,22,22,8,128]{4,3,2,1,0:T(8,128)} %copy_convert_fusion, f32[8,128]{1,0:T(8,128)S(1)} %get-tuple-element.19, f32[8,128]{1,0:T(8,128)S(1)} %get-tuple-element.20, f32[8,128]{1,0:T(8,128)S(1)} %get-tuple-element.21, ...), kind=kLoop, calls=%fused_computation.207 | loop fusion | flops 77069568 | bytes 157490176 | tf_op jit(solution)/shard_map/reduce_sum | solution.py:26
  120.6 11.0 %multiply_reduce_fusion = f32[3,16,16]{2,1,0:T(8,128)S(1)} fusion(f32[3,16,16,8,128]{4,3,2,1,0:T(8,128)S(1)} %get-tuple-element.3, f32[3,16,16]{2,1,0:T(8,128)S(1)} %broadcast_multiply_fusion.1), kind=kLoop, calls=%fused_computation.105 | loop fusion | flops 2358528 | bytes 3151872 | tf_op jit(solution)/shard_map/reduce_sum | solution.py:28
  131.6 3.0 %multiply_convert_fusion.1 = bf16[3,16,16,8,128]{4,3,2,1,0:T(8,128)(2,1)} fusion(f32[3,16,16,8,128]{4,3,2,1,0:T(8,128)S(1)} %get-tuple-element.3, f32[8,128]{1,0:T(8,128)S(1)} %bitcast.200, f32[3,16,16]{2,1,0:T(8,128)S(1)} %add_rsqrt_fusion, f32[3,16,16]{2,1,0:T(8,128)S(1)} %broadcast_multiply_fusion.1), kind=kLoop, calls=%fused_computation.104 | loop fusion | flops 3145728 | bytes 4728832 | tf_op jit(solution)/shard_map/convert_element_type | solution.py:29
  134.6 21.1 %broadcast_multiply_fusion = (bf16[768,1024]{1,0:T(8,128)(2,1)S(1)}, bf16[768,1024]{1,0:T(8,128)(2,1)}) fusion(bf16[768]{0:T(1024)(128)(2,1)S(1)} %copy-done.29, bf16[2,1024,4096]{2,1,0:T(8,128)(2,1)} %all-gather.2.cloned.1.call-done, bf16[96,8,8,128]{3,2,1,0:T(8,128)(2,1)} %bitcast.195, f32[1024]{0:T(1024)S(1)} %copy-done.30, bf16[768,1024]{1,0:T(8,128)(2,1)} %bitcast.188), kind=kOutput, calls=%fused_computation.119 | convolution fusion | flops 12906921984 | bytes 23074304 | tf_op jit(solution)/shard_map/dot_general | solution.py:38
  159.2 3.8 %fusion.55 = f32[512,1040]{0,1:T(8,128)} fusion(bf16[768,16]{1,0:T(8,128)(2,1)S(1)} %copy-done.2, bf16[768,1024]{1,0:T(8,128)(2,1)} %get-tuple-element.74, bf16[768,1024]{0,1:T(8,128)(2,1)S(1)} %reshape.192, s32[]{:T(128)S(6)} %select_n.160), kind=kOutput, calls=%fused_computation.112 | convolution fusion | flops 821084160 | bytes 4685828 | tf_op jit(solution)/shard_map/dot_general | solution.py:149
  163.0 4.4 %collective-permute-start.4 = (f32[512,1040]{0,1:T(8,128)}, f32[512,1040]{0,1:T(8,128)S(1)}, u32[]{:S(2)}, u32[]{:S(2)}) collective-permute-start(f32[512,1040]{0,1:T(8,128)} %fusion.55), channel_id=1, source_target_pairs={{0,1},{1,0},{2,3},{3,2},{4,5},{5,4},{6,7},{7,6},{8,9},{9,8},{10,11... | collective-permute-start | bytes 6389768 | tf_op jit(solution)/shard_map/ppermute | solution.py:154
  167.4 2.7 %fusion.56 = f32[512,1040]{0,1:T(8,128)S(1)} fusion(bf16[768,16]{1,0:T(8,128)(2,1)S(1)} %copy-done.2, bf16[768,1024]{1,0:T(8,128)(2,1)} %get-tuple-element.74, bf16[768,1024]{0,1:T(8,128)(2,1)} %copy-done.1, s32[]{:T(128)S(6)} %select_n.159), kind=kOutput, calls=%fused_computation.113 | convolution fusion | flops 821084160 | bytes 4513796 | tf_op jit(solution)/shard_map/dot_general | solution.py:149
  173.3 2.7 %reshape.193 = f32[2,2,128,1040]{2,1,0,3:T(2,128)S(1)} reshape(f32[512,1040]{0,1:T(8,128)} %add.352) | data formatting | bytes 4259840 | tf_op jit(solution)/shard_map/reshape | solution.py:66
  178.3 14.9 %collective-permute-done.5 = f32[256,1040]{0,1:T(8,128)S(1)} collective-permute-done((f32[256,1040]{0,1:T(8,128)S(1)}, f32[256,1040]{0,1:T(8,128)S(1)}, u32[]{:S(2)}, u32[]{:S(2)}) %collective-permute-start.5) | collective-permute-done | bytes 1064992 | tf_op jit(solution)/shard_map/ppermute | solution.py:85
  196.1 8.4 %collective-permute-done.6 = f32[128,1040]{0,1:T(8,128)S(1)} collective-permute-done((f32[128,1040]{0,1:T(8,128)S(1)}, f32[128,1040]{0,1:T(8,128)S(1)}, u32[]{:S(2)}, u32[]{:S(2)}) %collective-permute-start.6) | collective-permute-done | bytes 532512 | tf_op jit(solution)/shard_map/ppermute | solution.py:85
  205.0 4.9 %collective-permute-start.9 = (f32[32,1040]{1,0:T(8,128)S(1)}, f32[32,1040]{1,0:T(8,128)S(1)}, u32[]{:S(2)}, u32[]{:S(2)}) collective-permute-start(f32[32,1040]{1,0:T(8,128)S(1)} %get-tuple-element.15), channel_id=1, source_target_pairs={{0,20},{1,21},{2,22},{3,23},{4,16},{5,17},{6,18},{7,19},{8,28},{9,... | collective-permute-start | bytes 399368 | tf_op jit(solution)/shard_map/ppermute | solution.py:111
  211.2 2.9 %collective-permute-done.8 = f32[32,1040]{1,0:T(8,128)S(1)} collective-permute-done((f32[32,1040]{1,0:T(8,128)S(1)}, f32[32,1040]{1,0:T(8,128)S(1)}, u32[]{:S(2)}, u32[]{:S(2)}) %collective-permute-start.8) | collective-permute-done | bytes 133152 | tf_op jit(solution)/shard_map/ppermute | solution.py:111
  214.3 5.2 %collective-permute-done.10 = f32[16,1040]{1,0:T(8,128)S(1)} collective-permute-done((f32[16,1040]{1,0:T(8,128)S(1)}, f32[16,1040]{1,0:T(8,128)S(1)}, u32[]{:S(2)}, u32[]{:S(2)}) %collective-permute-start.10) | collective-permute-done | bytes 66592 | tf_op jit(solution)/shard_map/ppermute | solution.py:85
  219.6 2.9 %collective-permute-start.11 = (f32[4,1040]{1,0:T(4,128)S(1)}, f32[4,1040]{1,0:T(4,128)S(1)}, u32[]{:S(2)}, u32[]{:S(2)}) collective-permute-start(f32[4,1040]{1,0:T(4,128)S(1)} %get-tuple-element.70), channel_id=1, source_target_pairs={{0,128},{1,33},{2,130},{3,35},{4,132},{5,37},{6,134},{7,39},{8,136... | collective-permute-start | bytes 49928 | tf_op jit(solution)/shard_map/ppermute | solution.py:111
  223.7 4.9 %collective-permute-start.13 = (f32[4,1040]{1,0:T(4,128)S(1)}, f32[4,1040]{1,0:T(4,128)S(1)}, u32[]{:S(2)}, u32[]{:S(2)}) collective-permute-start(f32[4,1040]{1,0:T(4,128)S(1)} %get-tuple-element.71), channel_id=1, source_target_pairs={{0,192},{1,97},{2,194},{3,99},{4,196},{5,101},{6,198},{7,103},{8,2... | collective-permute-start | bytes 49928 | tf_op jit(solution)/shard_map/ppermute | solution.py:111
  230.2 3.5 %collective-permute-done.13 = f32[4,1040]{1,0:T(4,128)S(1)} collective-permute-done((f32[4,1040]{1,0:T(4,128)S(1)}, f32[4,1040]{1,0:T(4,128)S(1)}, u32[]{:S(2)}, u32[]{:S(2)}) %collective-permute-start.13) | collective-permute-done | bytes 16672 | tf_op jit(solution)/shard_map/ppermute | solution.py:111
  (121 shorter events, 32.9 us)
Async XLA Ops:
  7.2 9.5 %copy-start.4 = (s32[3,16,16]{2,1,0:T(8,128)S(1)}, s32[3,16,16]{2,1,0:T(8,128)}, u32[]{:S(2)}) copy-start(s32[3,16,16]{2,1,0:T(8,128)} %param.14) | copy-start | bytes 9220
  7.2 127.4 %all-gather.2.cloned.1.call-start = ((), (), s32[]{:S(2)}) async-start(), calls=%async_computation | async-start | bytes 17825792 | tf_op jit(solution)/shard_map/all_gather | solution.py:133
  9.6 9.2 %copy-start.3 = (bf16[7,7,1024]{2,1,0:T(8,128)(2,1)S(1)}, bf16[7,7,1024]{2,1,0:T(8,128)(2,1)}, u32[]{:S(2)}) copy-start(bf16[7,7,1024]{2,1,0:T(8,128)(2,1)} %param.9) | copy-start | bytes 301060
  9.7 9.3 %copy-start.5 = (s32[3,16,16]{2,1,0:T(8,128)S(1)}, s32[3,16,16]{2,1,0:T(8,128)}, u32[]{:S(2)}) copy-start(s32[3,16,16]{2,1,0:T(8,128)} %param.15) | copy-start | bytes 9220
  9.7 11.3 %collective-permute-start = (bf16[3,3,16,1024]{3,2,1,0:T(8,128)(2,1)S(1)}, bf16[3,3,16,1024]{3,2,1,0:T(8,128)(2,1)S(1)}, u32[]{:S(2)}, u32[]{:S(2)}) collective-permute-start(bf16[3,3,16,1024]{3,2,1,0:T(8,128)(2,1)S(1)} %get-tuple-element.10), channel_id=1, source_target_pairs={{0,16},{16,32},{32,48},{48,64},{64,80},{80,96},{96,112},{112,128},... | collective-permute-start | bytes 884744 | tf_op jit(solution)/shard_map/ppermute | solution.py:19
  14.8 11.6 %collective-permute-start.1 = (bf16[3,3,16,1024]{3,2,1,0:T(8,128)(2,1)S(1)}, bf16[3,3,16,1024]{3,2,1,0:T(8,128)(2,1)S(1)}, u32[]{:S(2)}, u32[]{:S(2)}) collective-permute-start(bf16[3,3,16,1024]{3,2,1,0:T(8,128)(2,1)S(1)} %get-tuple-element.11), channel_id=1, source_target_pairs={{16,0},{32,16},{48,32},{64,48},{80,64},{96,80},{112,96},{128,112},... | collective-permute-start | bytes 884744 | tf_op jit(solution)/shard_map/ppermute | solution.py:20
  29.7 15.5 %collective-permute-start.2 = (bf16[3,22,3,1024]{3,1,2,0:T(8,128)(2,1)S(1)}, bf16[3,22,3,1024]{3,1,2,0:T(8,128)(2,1)}, u32[]{:S(2)}, u32[]{:S(2)}) collective-permute-start(bf16[3,22,3,1024]{3,1,2,0:T(8,128)(2,1)S(1)} %get-tuple-element.4), channel_id=1, source_target_pairs={{0,1},{1,2},{2,3},{3,4},{4,5},{5,6},{6,7},{7,8},{8,9},{9,10},{10,1... | collective-permute-start | bytes 1216520 | tf_op jit(solution)/shard_map/ppermute | solution.py:19
  31.6 17.7 %collective-permute-start.3 = (bf16[3,22,3,1024]{3,1,2,0:T(8,128)(2,1)S(1)}, bf16[3,22,3,1024]{3,1,2,0:T(8,128)(2,1)}, u32[]{:S(2)}, u32[]{:S(2)}) collective-permute-start(bf16[3,22,3,1024]{3,1,2,0:T(8,128)(2,1)S(1)} %get-tuple-element.5), channel_id=1, source_target_pairs={{1,0},{2,1},{3,2},{4,3},{5,4},{6,5},{7,6},{8,7},{9,8},{10,9},{11,1... | collective-permute-start | bytes 1216520 | tf_op jit(solution)/shard_map/ppermute | solution.py:20
  50.6 4.3 %copy-start.6 = (f32[8,128]{1,0:T(8,128)S(1)}, f32[8,128]{1,0:T(8,128)}, u32[]{:S(2)}) copy-start(f32[8,128]{1,0:T(8,128)} %get-tuple-element.63) | copy-start | bytes 12292
  50.6 4.2 %copy-start.7 = (f32[8,128]{1,0:T(8,128)S(1)}, f32[8,128]{1,0:T(8,128)}, u32[]{:S(2)}) copy-start(f32[8,128]{1,0:T(8,128)} %get-tuple-element.64) | copy-start | bytes 12292
  50.7 4.2 %copy-start.8 = (f32[8,128]{1,0:T(8,128)S(1)}, f32[8,128]{1,0:T(8,128)}, u32[]{:S(2)}) copy-start(f32[8,128]{1,0:T(8,128)} %get-tuple-element.65) | copy-start | bytes 12292
  50.7 4.2 %copy-start.9 = (f32[8,128]{1,0:T(8,128)S(1)}, f32[8,128]{1,0:T(8,128)}, u32[]{:S(2)}) copy-start(f32[8,128]{1,0:T(8,128)} %get-tuple-element.36) | copy-start | bytes 12292
  50.7 4.2 %copy-start.10 = (f32[8,128]{1,0:T(8,128)S(1)}, f32[8,128]{1,0:T(8,128)}, u32[]{:S(2)}) copy-start(f32[8,128]{1,0:T(8,128)} %get-tuple-element.37) | copy-start | bytes 12292
  120.6 11.1 %copy-start.28 = (f32[1024]{0:T(1024)S(1)}, f32[1024]{0:T(1024)}, u32[]{:S(2)}) copy-start(f32[1024]{0:T(1024)} %param.10) | copy-start | bytes 12292
  163.0 8.4 %collective-permute-start.4 = (f32[512,1040]{0,1:T(8,128)}, f32[512,1040]{0,1:T(8,128)S(1)}, u32[]{:S(2)}, u32[]{:S(2)}) collective-permute-start(f32[512,1040]{0,1:T(8,128)} %fusion.55), channel_id=1, source_target_pairs={{0,1},{1,0},{2,3},{3,2},{4,5},{5,4},{6,7},{7,6},{8,9},{9,8},{10,11... | collective-permute-start | bytes 6389768 | tf_op jit(solution)/shard_map/ppermute | solution.py:154
  178.0 15.3 %collective-permute-start.5 = (f32[256,1040]{0,1:T(8,128)S(1)}, f32[256,1040]{0,1:T(8,128)S(1)}, u32[]{:S(2)}, u32[]{:S(2)}) collective-permute-start(f32[256,1040]{0,1:T(8,128)S(1)} %pad_maximum_fusion.5), channel_id=1, source_target_pairs={{0,2},{1,9},{2,0},{3,11},{4,6},{5,13},{6,4},{7,15},{8,10},{9,1},{1... | collective-permute-start | bytes 3194888 | tf_op jit(solution)/shard_map/ppermute | solution.py:85
  195.1 9.4 %collective-permute-start.6 = (f32[128,1040]{0,1:T(8,128)S(1)}, f32[128,1040]{0,1:T(8,128)S(1)}, u32[]{:S(2)}, u32[]{:S(2)}) collective-permute-start(f32[128,1040]{0,1:T(8,128)S(1)} %bitcast.197), channel_id=1, source_target_pairs={{0,8},{1,3},{2,10},{3,1},{4,12},{5,7},{6,14},{7,5},{8,0},{9,11},{1... | collective-permute-start | bytes 1597448 | tf_op jit(solution)/shard_map/ppermute | solution.py:85
  204.8 6.3 %collective-permute-start.7 = (f32[32,1040]{1,0:T(8,128)S(1)}, f32[32,1040]{1,0:T(8,128)S(1)}, u32[]{:S(2)}, u32[]{:S(2)}) collective-permute-start(f32[32,1040]{1,0:T(8,128)S(1)} %get-tuple-element.14), channel_id=1, source_target_pairs={{0,16},{1,17},{2,18},{3,19},{4,20},{5,21},{6,22},{7,23},{8,24},{9,... | collective-permute-start | bytes 399368 | tf_op jit(solution)/shard_map/ppermute | solution.py:111
  204.9 9.2 %collective-permute-start.8 = (f32[32,1040]{1,0:T(8,128)S(1)}, f32[32,1040]{1,0:T(8,128)S(1)}, u32[]{:S(2)}, u32[]{:S(2)}) collective-permute-start(f32[32,1040]{1,0:T(8,128)S(1)} %get-tuple-element.16), channel_id=1, source_target_pairs={{0,4},{1,5},{2,6},{3,7},{4,0},{5,1},{6,2},{7,3},{8,12},{9,13},{10,... | collective-permute-start | bytes 399368 | tf_op jit(solution)/shard_map/ppermute | solution.py:111
  205.0 9.1 %collective-permute-start.9 = (f32[32,1040]{1,0:T(8,128)S(1)}, f32[32,1040]{1,0:T(8,128)S(1)}, u32[]{:S(2)}, u32[]{:S(2)}) collective-permute-start(f32[32,1040]{1,0:T(8,128)S(1)} %get-tuple-element.15), channel_id=1, source_target_pairs={{0,20},{1,21},{2,22},{3,23},{4,16},{5,17},{6,18},{7,19},{8,28},{9,... | collective-permute-start | bytes 399368 | tf_op jit(solution)/shard_map/ppermute | solution.py:111
  214.2 5.3 %collective-permute-start.10 = (f32[16,1040]{1,0:T(8,128)S(1)}, f32[16,1040]{1,0:T(8,128)S(1)}, u32[]{:S(2)}, u32[]{:S(2)}) collective-permute-start(f32[16,1040]{1,0:T(8,128)S(1)} %pad_maximum_fusion.7), channel_id=1, source_target_pairs={{0,32},{1,129},{2,34},{3,131},{4,36},{5,133},{6,38},{7,135},{8,40}... | collective-permute-start | bytes 199688 | tf_op jit(solution)/shard_map/ppermute | solution.py:85
  219.6 9.0 %collective-permute-start.11 = (f32[4,1040]{1,0:T(4,128)S(1)}, f32[4,1040]{1,0:T(4,128)S(1)}, u32[]{:S(2)}, u32[]{:S(2)}) collective-permute-start(f32[4,1040]{1,0:T(4,128)S(1)} %get-tuple-element.70), channel_id=1, source_target_pairs={{0,128},{1,33},{2,130},{3,35},{4,132},{5,37},{6,134},{7,39},{8,136... | collective-permute-start | bytes 49928 | tf_op jit(solution)/shard_map/ppermute | solution.py:111
  222.6 7.7 %collective-permute-start.12 = (f32[4,1040]{1,0:T(4,128)S(1)}, f32[4,1040]{1,0:T(4,128)S(1)}, u32[]{:S(2)}, u32[]{:S(2)}) collective-permute-start(f32[4,1040]{1,0:T(4,128)S(1)} %get-tuple-element.72), channel_id=1, source_target_pairs={{0,64},{1,65},{2,66},{3,67},{4,68},{5,69},{6,70},{7,71},{8,72},{9,... | collective-permute-start | bytes 49928 | tf_op jit(solution)/shard_map/ppermute | solution.py:111
  223.7 10.1 %collective-permute-start.13 = (f32[4,1040]{1,0:T(4,128)S(1)}, f32[4,1040]{1,0:T(4,128)S(1)}, u32[]{:S(2)}, u32[]{:S(2)}) collective-permute-start(f32[4,1040]{1,0:T(4,128)S(1)} %get-tuple-element.71), channel_id=1, source_target_pairs={{0,192},{1,97},{2,194},{3,99},{4,196},{5,101},{6,198},{7,103},{8,2... | collective-permute-start | bytes 49928 | tf_op jit(solution)/shard_map/ppermute | solution.py:111
  (22 other events, 84.1 us)
Sparse Core Ops, SparseCore 0:
  9.8 105.7 all-gather.1

commit v8 on v7

--- a/solution.py
+++ b/solution.py
@@ -153,9 +153,8 @@
     size = lax.axis_size("row") * lax.axis_size("col")
     sent = lax.ppermute(rows_of(1 - core), axes, [(i, i ^ 1) for i in range(size)])
     kept = lax.optimization_barrier(rows_of(core))
-    summed = halving_sum(kept + sent, axes, (1, 2))
-    summed = radix4(summed, axes, (HALVING_BITS[0][3],) * 2, (HALVING_BITS[0][4],) * 2)
-    summed = halving_sum(summed, axes, (5,))
+    summed = radix4(kept + sent, axes, (HALVING_BITS[0][1],) * 2, (HALVING_BITS[0][2],) * 2)
+    summed = halving_sum(summed, axes, (3, 4, 5))
     summed = radix4(summed, axes, tuple(b[6] for b in HALVING_BITS), tuple(b[7] for b in HALVING_BITS))
     gram_sum, cross_sum = summed[:, :width], summed[:, width:]
     total = float(tiles * high * lax.axis_size("row") * wide * lax.axis_size("col"))

time: 247 us -> 247 us (level); the launches traced: 242 us -> 246 us
  waiting for transfers between devices: 53.6 us -> 64 us
  other arithmetic: 92.3 us -> 89.3 us
    ppermute x6, waiting for transfers between devices: 9.33 us -> 27.3 us  [radix4(): total = total + lax.ppermute(piece, axes, pairs)]
    ppermute x3, waiting for transfers between devices: 28.5 us -> 19.1 us  [halving_sum(): part = keep + lax.ppermute(send, axes, pairs)]
    reshape x2 -> x0, local copies, waits for them, and re-layouts: 3.24 us -> none  [the longest x1 2.69 us: halving_sum(): quarters = part.reshape((2, 2, part.shape[0] // 4) + part.shape[1:])]
    reduce_sum x1, other arithmetic: 65.5 us -> 62.4 us  [apply_norm(): mean = jnp.mean(rows, axis=(-2, -1), keepdims=True)]
    reshape x1 -> x2, local copies, waits for them, and re-layouts: 0.03 us -> 2.63 us  [radix4(): quarters = part.reshape((2, 2, part.shape[0] // 4) + part.shape[1:])]
    dynamic_slice x3 -> x2, local copies, waits for them, and re-layouts: 3.92 us -> 5.39 us  [quarter(): return lax.dynamic_slice(quarters, start, (1, 1) + rest).reshape(rest)]
  transfers between devices with their start and end apart: 15 -> 15, of which waited for: 12 -> 13; matrix products, arithmetic and copies ran while one was open for 42% -> 39% of each run, Pallas kernels for 0% -> 0%
where the time goes in v8:
time: 247 us; the launch traced here: 246 us
  other arithmetic  89.3 us (36%)
  waiting for transfers between devices  64 us (26%)
  starting transfers between devices  29.7 us (12%)
  matrix products  26.1 us (11%)
  local copies, waits for them, and re-layouts  22.2 us (9%)
  between operations  14.8 us (6%)
    reduce_sum x1, other arithmetic, apply_norm(): mean = jnp.mean(rows, axis=(-2, -1), keepdims=True)  62.4 us
    ppermute x6, waiting for transfers between devices, radix4(): total = total + lax.ppermute(piece, axes, pairs)  27.3 us
    dot_general x1, matrix products, contract(): lax.dot_general(hidden, piece, (((1,), (1,)), ((), ())), preferred_elemen...  21.1 us
    ppermute x3, waiting for transfers between devices, halving_sum(): part = keep + lax.ppermute(send, axes, pairs)  19.1 us
    ppermute x6, starting transfers between devices, radix4(): total = total + lax.ppermute(piece, axes, pairs)  12.5 us
    reduce_sum x1, other arithmetic, apply_norm(): var = jnp.mean(centered * centered, axis=(-2, -1), keepdims=True)  11 us
    ppermute x2, waiting for transfers between devices, with_halo(): after = lax.ppermute(leading, axis, down)  7.93 us
    ppermute x2, starting transfers between devices, with_halo(): before = lax.ppermute(last, axis, up)  6.96 us
  transfers between devices with their start and end apart: 15, of which 13 were waited for; matrix products, arithmetic and copies ran while one was open for 39% of the time, Pallas kernels for 0%

profile of v8, /device:TPU:120, one launch (start us, length us, event | category | flops | bytes accessed | tf_op | source)
XLA Modules:
  0.0 246.1 jit_solution(5160934806282927669)
XLA Ops:
  9.7 5.0 %collective-permute-start = (bf16[3,3,16,1024]{3,2,1,0:T(8,128)(2,1)S(1)}, bf16[3,3,16,1024]{3,2,1,0:T(8,128)(2,1)S(1)}, u32[]{:S(2)}, u32[]{:S(2)}) collective-permute-start(bf16[3,3,16,1024]{3,2,1,0:T(8,128)(2,1)S(1)} %get-tuple-element.10), channel_id=1, source_target_pairs={{0,16},{16,32},{32,48},{48,64},{64,80},{80,96},{96,112},{112,128},... | collective-permute-start | bytes 884744 | tf_op jit(solution)/shard_map/ppermute | solution.py:19
  21.3 5.1 %collective-permute-done.1 = bf16[3,3,16,1024]{3,2,1,0:T(8,128)(2,1)S(1)} collective-permute-done((bf16[3,3,16,1024]{3,2,1,0:T(8,128)(2,1)S(1)}, bf16[3,3,16,1024]{3,2,1,0:T(8,128)(2,1)S(1)}, u32[]{:S(2)}, u32[]{:S(2)}) %collective-permute-start.1) | collective-permute-done | bytes 294944 | tf_op jit(solution)/shard_map/ppermute | solution.py:20
  26.6 3.0 %pad_maximum_fusion.1 = bf16[3,22,16,1024]{3,1,2,0:T(8,128)(2,1)S(1)} fusion(bf16[3,3,16,1024]{3,1,2,0:T(4,128)(2,1)S(1)} %copy.55, bf16[3,16,16,1024]{3,1,2,0:T(8,128)(2,1)} %copy.54, bf16[3,3,16,1024]{3,1,2,0:T(4,128)(2,1)S(1)} %copy.53), kind=kLoop, calls=%fused_computation.108 | loop fusion | flops 6488064 | bytes 4325376 | tf_op jit(solution)/shard_map/concatenate | solution.py:21
  31.6 3.6 %collective-permute-start.3 = (bf16[3,22,3,1024]{3,1,2,0:T(8,128)(2,1)S(1)}, bf16[3,22,3,1024]{3,1,2,0:T(8,128)(2,1)}, u32[]{:S(2)}, u32[]{:S(2)}) collective-permute-start(bf16[3,22,3,1024]{3,1,2,0:T(8,128)(2,1)S(1)} %get-tuple-element.5), channel_id=1, source_target_pairs={{1,0},{2,1},{3,2},{4,3},{5,4},{6,5},{7,6},{8,7},{9,8},{10,9},{11,1... | collective-permute-start | bytes 1216520 | tf_op jit(solution)/shard_map/ppermute | solution.py:20
  39.3 5.9 %collective-permute-done.2 = bf16[3,22,3,1024]{3,1,2,0:T(8,128)(2,1)} collective-permute-done((bf16[3,22,3,1024]{3,1,2,0:T(8,128)(2,1)S(1)}, bf16[3,22,3,1024]{3,1,2,0:T(8,128)(2,1)}, u32[]{:S(2)}, u32[]{:S(2)}) %collective-permute-start.2) | collective-permute-done | bytes 405536 | tf_op jit(solution)/shard_map/ppermute | solution.py:19
  46.5 2.9 %collective-permute-done.3 = bf16[3,22,3,1024]{3,1,2,0:T(8,128)(2,1)} collective-permute-done((bf16[3,22,3,1024]{3,1,2,0:T(8,128)(2,1)S(1)}, bf16[3,22,3,1024]{3,1,2,0:T(8,128)(2,1)}, u32[]{:S(2)}, u32[]{:S(2)}) %collective-permute-start.3) | collective-permute-done | bytes 405536 | tf_op jit(solution)/shard_map/ppermute | solution.py:20
  50.9 4.0 %copy_convert_fusion = f32[3,22,22,8,128]{4,3,2,1,0:T(8,128)} fusion(bf16[3,22,3,8,128]{4,3,1,2,0:T(8,128)(2,1)S(1)} %concatenate.31, bf16[3,22,16,8,128]{4,3,1,2,0:T(8,128)(2,1)} %reshape.217, bf16[3,22,3,8,128]{4,3,1,2,0:T(8,128)(2,1)S(1)} %concatenate.29), kind=kLoop, calls=%fused_computation.107 | loop fusion | flops 4460544 | bytes 8921088 | tf_op jit(solution)/shard_map/convert_element_type | solution.py:124
  55.1 62.4 %fusion.70 = (f32[3,16,16]{2,1,0:T(8,128)S(1)}, f32[3,16,16,8,128]{4,3,2,1,0:T(8,128)S(1)}) fusion(f32[8,128]{1,0:T(8,128)S(1)} %get-tuple-element.17, f32[3,22,22,8,128]{4,3,2,1,0:T(8,128)} %copy_convert_fusion, f32[8,128]{1,0:T(8,128)S(1)} %get-tuple-element.18, f32[8,128]{1,0:T(8,128)S(1)} %get-tuple-element.19, f32[8,128]{1,0:T(8,128)S(1)} %get-tuple-element.20, ...), kind=kLoop, calls=%fused_computation.207 | loop fusion | flops 77069568 | bytes 157490176 | tf_op jit(solution)/shard_map/reduce_sum | solution.py:26
  117.6 11.0 %multiply_reduce_fusion = f32[3,16,16]{2,1,0:T(8,128)S(1)} fusion(f32[3,16,16,8,128]{4,3,2,1,0:T(8,128)S(1)} %get-tuple-element.3, f32[3,16,16]{2,1,0:T(8,128)S(1)} %broadcast_multiply_fusion.1), kind=kLoop, calls=%fused_computation.105 | loop fusion | flops 2358528 | bytes 3151872 | tf_op jit(solution)/shard_map/reduce_sum | solution.py:28
  128.6 3.0 %multiply_convert_fusion.1 = bf16[3,16,16,8,128]{4,3,2,1,0:T(8,128)(2,1)} fusion(f32[3,16,16,8,128]{4,3,2,1,0:T(8,128)S(1)} %get-tuple-element.3, f32[8,128]{1,0:T(8,128)S(1)} %bitcast.194, f32[3,16,16]{2,1,0:T(8,128)S(1)} %add_rsqrt_fusion, f32[3,16,16]{2,1,0:T(8,128)S(1)} %broadcast_multiply_fusion.1), kind=kLoop, calls=%fused_computation.104 | loop fusion | flops 3145728 | bytes 4728832 | tf_op jit(solution)/shard_map/convert_element_type | solution.py:29
  131.6 21.1 %broadcast_multiply_fusion = (bf16[768,1024]{1,0:T(8,128)(2,1)S(1)}, bf16[768,1024]{1,0:T(8,128)(2,1)}) fusion(bf16[768]{0:T(1024)(128)(2,1)S(1)} %copy-done.28, bf16[2,1024,4096]{2,1,0:T(8,128)(2,1)} %all-gather.2.cloned.1.call-done, bf16[96,8,8,128]{3,2,1,0:T(8,128)(2,1)} %bitcast.187, f32[1024]{0:T(1024)S(1)} %copy-done.29, bf16[768,1024]{1,0:T(8,128)(2,1)} %bitcast.185), kind=kOutput, calls=%fused_computation.117 | convolution fusion | flops 12906921984 | bytes 23074304 | tf_op jit(solution)/shard_map/dot_general | solution.py:38
  155.0 3.9 %fusion.55 = f32[512,1040]{0,1:T(8,128)} fusion(bf16[768,16]{1,0:T(8,128)(2,1)S(1)} %copy-done.1, bf16[768,1024]{1,0:T(8,128)(2,1)} %get-tuple-element.73, bf16[768,1024]{0,1:T(8,128)(2,1)S(1)} %reshape.192, s32[]{:T(128)S(6)} %select_n.160), kind=kOutput, calls=%fused_computation.112 | convolution fusion | flops 821084160 | bytes 4685828 | tf_op jit(solution)/shard_map/dot_general | solution.py:149
  159.0 4.4 %collective-permute-start.4 = (f32[512,1040]{0,1:T(8,128)}, f32[512,1040]{0,1:T(8,128)}, u32[]{:S(2)}, u32[]{:S(2)}) collective-permute-start(f32[512,1040]{0,1:T(8,128)} %fusion.55), channel_id=1, source_target_pairs={{0,1},{1,0},{2,3},{3,2},{4,5},{5,4},{6,7},{7,6},{8,9},{9,8},{10,11... | collective-permute-start | bytes 6389768 | tf_op jit(solution)/shard_map/ppermute | solution.py:154
  164.4 3.1 %collective-permute-done.4 = f32[512,1040]{0,1:T(8,128)} collective-permute-done((f32[512,1040]{0,1:T(8,128)}, f32[512,1040]{0,1:T(8,128)}, u32[]{:S(2)}, u32[]{:S(2)}) %collective-permute-start.4) | collective-permute-done | bytes 2129952 | tf_op jit(solution)/shard_map/ppermute | solution.py:154
  172.2 4.5 %constant_dynamic-slice_fusion.3 = (f32[1,1,128,1040]{2,1,0,3:T(1,128)S(1)}, f32[1,1,128,1040]{2,1,0,3:T(1,128)S(1)}, f32[1,1,128,1040]{2,1,0,3:T(1,128)}, f32[1,1,128,1040]{2,1,0,3:T(1,128)}) fusion(f32[2,2,128,1040]{2,1,0,3:T(2,128)} %reshape.193, s32[]{:T(128)S(6)} %select_n.161, s32[]{:T(128)S(6)} %select_n.162, s32[]{:T(128)S(6)} %select_n.163, ...), kind=kLoop, calls=%fused_computation.149 | loop fusion | bytes 4259856 | tf_op jit(solution)/shard_map/dynamic_slice | solution.py:102
  177.1 3.1 %collective-permute-start.7 = (f32[128,1040]{0,1:T(8,128)S(1)}, f32[128,1040]{0,1:T(8,128)S(1)}, u32[]{:S(2)}, u32[]{:S(2)}) collective-permute-start(f32[128,1040]{0,1:T(8,128)S(1)} %bitcast.191), channel_id=1, source_target_pairs={{0,10},{1,11},{2,8},{3,9},{4,14},{5,15},{6,12},{7,13},{8,2},{9,3},... | collective-permute-start | bytes 1597448 | tf_op jit(solution)/shard_map/ppermute | solution.py:111
  181.1 10.2 %collective-permute-done.5 = f32[128,1040]{0,1:T(8,128)S(1)} collective-permute-done((f32[128,1040]{0,1:T(8,128)}, f32[128,1040]{0,1:T(8,128)S(1)}, u32[]{:S(2)}, u32[]{:S(2)}) %collective-permute-start.5) | collective-permute-done | bytes 532512 | tf_op jit(solution)/shard_map/ppermute | solution.py:111
  192.3 11.7 %collective-permute-done.7 = f32[128,1040]{0,1:T(8,128)S(1)} collective-permute-done((f32[128,1040]{0,1:T(8,128)S(1)}, f32[128,1040]{0,1:T(8,128)S(1)}, u32[]{:S(2)}, u32[]{:S(2)}) %collective-permute-start.7) | collective-permute-done | bytes 532512 | tf_op jit(solution)/shard_map/ppermute | solution.py:111
  204.5 6.7 %collective-permute-done.8 = f32[64,1040]{1,0:T(8,128)S(1)} collective-permute-done((f32[64,1040]{1,0:T(8,128)S(1)}, f32[64,1040]{1,0:T(8,128)S(1)}, u32[]{:S(2)}, u32[]{:S(2)}) %collective-permute-start.8) | collective-permute-done | bytes 266272 | tf_op jit(solution)/shard_map/ppermute | solution.py:85
  211.4 6.6 %collective-permute-done.9 = f32[32,1040]{1,0:T(8,128)S(1)} collective-permute-done((f32[32,1040]{1,0:T(8,128)S(1)}, f32[32,1040]{1,0:T(8,128)S(1)}, u32[]{:S(2)}, u32[]{:S(2)}) %collective-permute-start.9) | collective-permute-done | bytes 133152 | tf_op jit(solution)/shard_map/ppermute | solution.py:85
  218.2 5.8 %collective-permute-done.10 = f32[16,1040]{1,0:T(8,128)S(1)} collective-permute-done((f32[16,1040]{1,0:T(8,128)S(1)}, f32[16,1040]{1,0:T(8,128)S(1)}, u32[]{:S(2)}, u32[]{:S(2)}) %collective-permute-start.10) | collective-permute-done | bytes 66592 | tf_op jit(solution)/shard_map/ppermute | solution.py:85
  224.1 2.8 %collective-permute-start.11 = (f32[4,1040]{1,0:T(4,128)S(1)}, f32[4,1040]{1,0:T(4,128)S(1)}, u32[]{:S(2)}, u32[]{:S(2)}) collective-permute-start(f32[4,1040]{1,0:T(4,128)S(1)} %get-tuple-element.69), channel_id=1, source_target_pairs={{0,128},{1,33},{2,130},{3,35},{4,132},{5,37},{6,134},{7,39},{8,136... | collective-permute-start | bytes 49928 | tf_op jit(solution)/shard_map/ppermute | solution.py:111
  228.0 5.1 %collective-permute-start.13 = (f32[4,1040]{1,0:T(4,128)S(1)}, f32[4,1040]{1,0:T(4,128)S(1)}, u32[]{:S(2)}, u32[]{:S(2)}) collective-permute-start(f32[4,1040]{1,0:T(4,128)S(1)} %get-tuple-element.70), channel_id=1, source_target_pairs={{0,192},{1,97},{2,194},{3,99},{4,196},{5,101},{6,198},{7,103},{8,2... | collective-permute-start | bytes 49928 | tf_op jit(solution)/shard_map/ppermute | solution.py:111
  234.6 3.5 %collective-permute-done.13 = f32[4,1040]{1,0:T(4,128)S(1)} collective-permute-done((f32[4,1040]{1,0:T(4,128)S(1)}, f32[4,1040]{1,0:T(4,128)S(1)}, u32[]{:S(2)}, u32[]{:S(2)}) %collective-permute-start.13) | collective-permute-done | bytes 16672 | tf_op jit(solution)/shard_map/ppermute | solution.py:111
  (122 shorter events, 32.7 us)
Async XLA Ops:
  7.2 9.5 %copy-start.3 = (s32[3,16,16]{2,1,0:T(8,128)S(1)}, s32[3,16,16]{2,1,0:T(8,128)}, u32[]{:S(2)}) copy-start(s32[3,16,16]{2,1,0:T(8,128)} %param.14) | copy-start | bytes 9220
  7.2 124.4 %all-gather.2.cloned.1.call-start = ((), (), s32[]{:S(2)}) async-start(), calls=%async_computation | async-start | bytes 17825792 | tf_op jit(solution)/shard_map/all_gather | solution.py:133
  9.7 9.2 %copy-start.2 = (bf16[7,7,1024]{2,1,0:T(8,128)(2,1)S(1)}, bf16[7,7,1024]{2,1,0:T(8,128)(2,1)}, u32[]{:S(2)}) copy-start(bf16[7,7,1024]{2,1,0:T(8,128)(2,1)} %param.9) | copy-start | bytes 301060
  9.7 9.3 %copy-start.4 = (s32[3,16,16]{2,1,0:T(8,128)S(1)}, s32[3,16,16]{2,1,0:T(8,128)}, u32[]{:S(2)}) copy-start(s32[3,16,16]{2,1,0:T(8,128)} %param.15) | copy-start | bytes 9220
  9.7 11.3 %collective-permute-start = (bf16[3,3,16,1024]{3,2,1,0:T(8,128)(2,1)S(1)}, bf16[3,3,16,1024]{3,2,1,0:T(8,128)(2,1)S(1)}, u32[]{:S(2)}, u32[]{:S(2)}) collective-permute-start(bf16[3,3,16,1024]{3,2,1,0:T(8,128)(2,1)S(1)} %get-tuple-element.10), channel_id=1, source_target_pairs={{0,16},{16,32},{32,48},{48,64},{64,80},{80,96},{96,112},{112,128},... | collective-permute-start | bytes 884744 | tf_op jit(solution)/shard_map/ppermute | solution.py:19
  14.8 11.6 %collective-permute-start.1 = (bf16[3,3,16,1024]{3,2,1,0:T(8,128)(2,1)S(1)}, bf16[3,3,16,1024]{3,2,1,0:T(8,128)(2,1)S(1)}, u32[]{:S(2)}, u32[]{:S(2)}) collective-permute-start(bf16[3,3,16,1024]{3,2,1,0:T(8,128)(2,1)S(1)} %get-tuple-element.11), channel_id=1, source_target_pairs={{16,0},{32,16},{48,32},{64,48},{80,64},{96,80},{112,96},{128,112},... | collective-permute-start | bytes 884744 | tf_op jit(solution)/shard_map/ppermute | solution.py:20
  29.7 15.5 %collective-permute-start.2 = (bf16[3,22,3,1024]{3,1,2,0:T(8,128)(2,1)S(1)}, bf16[3,22,3,1024]{3,1,2,0:T(8,128)(2,1)}, u32[]{:S(2)}, u32[]{:S(2)}) collective-permute-start(bf16[3,22,3,1024]{3,1,2,0:T(8,128)(2,1)S(1)} %get-tuple-element.4), channel_id=1, source_target_pairs={{0,1},{1,2},{2,3},{3,4},{4,5},{5,6},{6,7},{7,8},{8,9},{9,10},{10,1... | collective-permute-start | bytes 1216520 | tf_op jit(solution)/shard_map/ppermute | solution.py:19
  31.6 17.7 %collective-permute-start.3 = (bf16[3,22,3,1024]{3,1,2,0:T(8,128)(2,1)S(1)}, bf16[3,22,3,1024]{3,1,2,0:T(8,128)(2,1)}, u32[]{:S(2)}, u32[]{:S(2)}) collective-permute-start(bf16[3,22,3,1024]{3,1,2,0:T(8,128)(2,1)S(1)} %get-tuple-element.5), channel_id=1, source_target_pairs={{1,0},{2,1},{3,2},{4,3},{5,4},{6,5},{7,6},{8,7},{9,8},{10,9},{11,1... | collective-permute-start | bytes 1216520 | tf_op jit(solution)/shard_map/ppermute | solution.py:20
  50.6 4.3 %copy-start.5 = (f32[8,128]{1,0:T(8,128)S(1)}, f32[8,128]{1,0:T(8,128)}, u32[]{:S(2)}) copy-start(f32[8,128]{1,0:T(8,128)} %get-tuple-element.62) | copy-start | bytes 12292
  50.7 4.3 %copy-start.6 = (f32[8,128]{1,0:T(8,128)S(1)}, f32[8,128]{1,0:T(8,128)}, u32[]{:S(2)}) copy-start(f32[8,128]{1,0:T(8,128)} %get-tuple-element.63) | copy-start | bytes 12292
  50.7 4.2 %copy-start.7 = (f32[8,128]{1,0:T(8,128)S(1)}, f32[8,128]{1,0:T(8,128)}, u32[]{:S(2)}) copy-start(f32[8,128]{1,0:T(8,128)} %get-tuple-element.64) | copy-start | bytes 12292
  50.7 4.2 %copy-start.8 = (f32[8,128]{1,0:T(8,128)S(1)}, f32[8,128]{1,0:T(8,128)}, u32[]{:S(2)}) copy-start(f32[8,128]{1,0:T(8,128)} %get-tuple-element.35) | copy-start | bytes 12292
  117.5 11.1 %copy-start.27 = (f32[1024]{0:T(1024)S(1)}, f32[1024]{0:T(1024)}, u32[]{:S(2)}) copy-start(f32[1024]{0:T(1024)} %param.10) | copy-start | bytes 12292
  155.0 8.3 %copy-start.30 = (bf16[768,1024]{1,0:T(8,128)(2,1)S(1)}, bf16[768,1024]{1,0:T(8,128)(2,1)}, u32[]{:S(2)}) copy-start(bf16[768,1024]{1,0:T(8,128)(2,1)} %get-tuple-element.73) | copy-start | bytes 4718596
  159.0 8.6 %collective-permute-start.4 = (f32[512,1040]{0,1:T(8,128)}, f32[512,1040]{0,1:T(8,128)}, u32[]{:S(2)}, u32[]{:S(2)}) collective-permute-start(f32[512,1040]{0,1:T(8,128)} %fusion.55), channel_id=1, source_target_pairs={{0,1},{1,0},{2,3},{3,2},{4,5},{5,4},{6,7},{7,6},{8,9},{9,8},{10,11... | collective-permute-start | bytes 6389768 | tf_op jit(solution)/shard_map/ppermute | solution.py:154
  176.8 14.6 %collective-permute-start.5 = (f32[128,1040]{0,1:T(8,128)}, f32[128,1040]{0,1:T(8,128)S(1)}, u32[]{:S(2)}, u32[]{:S(2)}) collective-permute-start(f32[128,1040]{0,1:T(8,128)} %bitcast.57), channel_id=1, source_target_pairs={{0,2},{1,3},{2,0},{3,1},{4,6},{5,7},{6,4},{7,5},{8,10},{9,11},{10,... | collective-permute-start | bytes 1597448 | tf_op jit(solution)/shard_map/ppermute | solution.py:111
  176.8 15.3 %collective-permute-start.6 = (f32[128,1040]{0,1:T(8,128)}, f32[128,1040]{0,1:T(8,128)S(1)}, u32[]{:S(2)}, u32[]{:S(2)}) collective-permute-start(f32[128,1040]{0,1:T(8,128)} %bitcast.58), channel_id=1, source_target_pairs={{0,8},{1,9},{2,10},{3,11},{4,12},{5,13},{6,14},{7,15},{8,0},{9,1},... | collective-permute-start | bytes 1597448 | tf_op jit(solution)/shard_map/ppermute | solution.py:111
  177.1 26.8 %collective-permute-start.7 = (f32[128,1040]{0,1:T(8,128)S(1)}, f32[128,1040]{0,1:T(8,128)S(1)}, u32[]{:S(2)}, u32[]{:S(2)}) collective-permute-start(f32[128,1040]{0,1:T(8,128)S(1)} %bitcast.191), channel_id=1, source_target_pairs={{0,10},{1,11},{2,8},{3,9},{4,14},{5,15},{6,12},{7,13},{8,2},{9,3},... | collective-permute-start | bytes 1597448 | tf_op jit(solution)/shard_map/ppermute | solution.py:111
  204.4 6.8 %collective-permute-start.8 = (f32[64,1040]{1,0:T(8,128)S(1)}, f32[64,1040]{1,0:T(8,128)S(1)}, u32[]{:S(2)}, u32[]{:S(2)}) collective-permute-start(f32[64,1040]{1,0:T(8,128)S(1)} %pad_maximum_fusion.6), channel_id=1, source_target_pairs={{0,16},{1,5},{2,18},{3,7},{4,20},{5,1},{6,22},{7,3},{8,24},{9,13},... | collective-permute-start | bytes 798728 | tf_op jit(solution)/shard_map/ppermute | solution.py:85
  211.3 6.7 %collective-permute-start.9 = (f32[32,1040]{1,0:T(8,128)S(1)}, f32[32,1040]{1,0:T(8,128)S(1)}, u32[]{:S(2)}, u32[]{:S(2)}) collective-permute-start(f32[32,1040]{1,0:T(8,128)S(1)} %dynamic-slice_bitcast_fusion), channel_id=1, source_target_pairs={{0,4},{1,17},{2,6},{3,19},{4,0},{5,21},{6,2},{7,23},{8,12},{9,25},... | collective-permute-start | bytes 399368 | tf_op jit(solution)/shard_map/ppermute | solution.py:85
  218.1 6.0 %collective-permute-start.10 = (f32[16,1040]{1,0:T(8,128)S(1)}, f32[16,1040]{1,0:T(8,128)S(1)}, u32[]{:S(2)}, u32[]{:S(2)}) collective-permute-start(f32[16,1040]{1,0:T(8,128)S(1)} %pad_maximum_fusion.7), channel_id=1, source_target_pairs={{0,32},{1,129},{2,34},{3,131},{4,36},{5,133},{6,38},{7,135},{8,40}... | collective-permute-start | bytes 199688 | tf_op jit(solution)/shard_map/ppermute | solution.py:85
  224.1 9.0 %collective-permute-start.11 = (f32[4,1040]{1,0:T(4,128)S(1)}, f32[4,1040]{1,0:T(4,128)S(1)}, u32[]{:S(2)}, u32[]{:S(2)}) collective-permute-start(f32[4,1040]{1,0:T(4,128)S(1)} %get-tuple-element.69), channel_id=1, source_target_pairs={{0,128},{1,33},{2,130},{3,35},{4,132},{5,37},{6,134},{7,39},{8,136... | collective-permute-start | bytes 49928 | tf_op jit(solution)/shard_map/ppermute | solution.py:111
  226.9 7.7 %collective-permute-start.12 = (f32[4,1040]{1,0:T(4,128)S(1)}, f32[4,1040]{1,0:T(4,128)S(1)}, u32[]{:S(2)}, u32[]{:S(2)}) collective-permute-start(f32[4,1040]{1,0:T(4,128)S(1)} %get-tuple-element.71), channel_id=1, source_target_pairs={{0,64},{1,65},{2,66},{3,67},{4,68},{5,69},{6,70},{7,71},{8,72},{9,... | collective-permute-start | bytes 49928 | tf_op jit(solution)/shard_map/ppermute | solution.py:111
  228.0 10.1 %collective-permute-start.13 = (f32[4,1040]{1,0:T(4,128)S(1)}, f32[4,1040]{1,0:T(4,128)S(1)}, u32[]{:S(2)}, u32[]{:S(2)}) collective-permute-start(f32[4,1040]{1,0:T(4,128)S(1)} %get-tuple-element.70), channel_id=1, source_target_pairs={{0,192},{1,97},{2,194},{3,99},{4,196},{5,101},{6,198},{7,103},{8,2... | collective-permute-start | bytes 49928 | tf_op jit(solution)/shard_map/ppermute | solution.py:111
  (22 other events, 86.1 us)
Sparse Core Ops, SparseCore 0:
  9.8 105.7 all-gather.1
